TPU v7x, 256 devices: a whole 4x4x8 slice. The times are simulated.
256 devices in a mesh: row: 8 (over x, core), col: 32 (over y, z).
Axes of the slice: x: 4, y: 4, z: 8, core: 2. Of those that a mesh axis runs over, the one named last changes fastest.
Arguments:
- tokens: bfloat16 [512, 8192], P('col', 'row'), may hold values from -6 to 6
- cotangent: bfloat16 [512, 8192], P('col', 'row'), may hold values from -6 to 6
- gate_weight: bfloat16 [8192, 28672], P('row', 'col'), may hold values from -0.09375 to 0.09375
- up_weight: bfloat16 [8192, 28672], P('row', 'col'), may hold values from -0.09375 to 0.09375
- down_weight: bfloat16 [28672, 8192], P('col', 'row'), may hold values from -0.046875 to 0.046875
- block_mask: int32 [3, 64, 224], P(None, 'row', 'col'), may hold values 0 or 1
Outputs:
- layer_out: bfloat16 [512, 8192], P('col', 'row')
- token_grad: bfloat16 [512, 8192], P('col', 'row')
- gate_grad: bfloat16 [8192, 28672], P('row', 'col')
- up_grad: bfloat16 [8192, 28672], P('row', 'col')
- down_grad: bfloat16 [28672, 8192], P('col', 'row')
All inputs are finite; a program needn't handle non-finite values. No bound on the sum of `block_mask` on one device may be relied on, other than what follows from the above.
Results may differ from a plain program's by a relative error of at most 0.025.
Values may be sent and summed in bfloat16 or wider, within the bound.
No kernel may reach another device: no remote copies, remote signals or barrier semaphores. Data moves between devices by JAX's collectives and lax.ppermute only.
A program may use at most 64 MiB of HBM per device.

v0:
```python
import jax
import jax.numpy as jnp
from jax import lax
from jax.sharding import PartitionSpec as P


def masked(weight, mask):
    rows, cols = mask.shape
    shaped = weight.reshape(rows, weight.shape[0] // rows, cols, weight.shape[1] // cols)
    return (shaped * mask.astype(weight.dtype)[:, None, :, None]).reshape(weight.shape)


def product(left, weight):
    return jnp.dot(left, weight, preferred_element_type=jnp.float32)


def product_t(left, weight):
    return lax.dot_general(
        left, weight, (((1,), (1,)), ((), ())), preferred_element_type=jnp.float32
    )


def contract_rows(left, right):
    return lax.dot_general(
        left, right, (((0,), (0,)), ((), ())), preferred_element_type=jnp.float32
    )


def shards(tokens, cotangent, gate_weight, up_weight, down_weight, block_mask):
    masked_gate = masked(gate_weight, block_mask[0])
    masked_up = masked(up_weight, block_mask[1])
    masked_down = masked(down_weight, block_mask[2].T)
    panel = lax.all_gather(tokens, "col", axis=0, tiled=True)
    grad_panel = lax.all_gather(cotangent, "col", axis=0, tiled=True)
    total_rows = panel.shape[0]
    width = masked_gate.shape[1]
    stacked = lax.psum_scatter(
        jnp.concatenate([product(panel, masked_gate), product(panel, masked_up)], axis=1).astype(
            jnp.bfloat16
        ),
        "row",
        scatter_dimension=0,
        tiled=True,
    ).astype(jnp.float32)
    gate = stacked[:, :width]
    up = stacked[:, width:]
    sigma = jax.nn.sigmoid(gate)
    act = (gate * sigma * up).astype(jnp.bfloat16)
    act_full = lax.all_gather(act, "row", axis=0, tiled=True)
    layer_out = lax.psum_scatter(
        product(act_full, masked_down).astype(jnp.bfloat16), "col", scatter_dimension=0, tiled=True
    )
    dact = lax.psum_scatter(
        product_t(grad_panel, masked_down).astype(jnp.bfloat16),
        "row",
        scatter_dimension=0,
        tiled=True,
    ).astype(jnp.float32)
    dgate = (dact * up * sigma * (1.0 + gate * (1.0 - sigma))).astype(jnp.bfloat16)
    dup = (dact * gate * sigma).astype(jnp.bfloat16)
    dgate_full, dup_full = (
        lax.all_gather(dgate, "row", axis=0, tiled=True),
        lax.all_gather(dup, "row", axis=0, tiled=True),
    )
    token_grad = lax.psum_scatter(
        (product_t(dgate_full, masked_gate) + product_t(dup_full, masked_up)).astype(jnp.bfloat16),
        "col",
        scatter_dimension=0,
        tiled=True,
    )
    scale = total_rows ** (-0.5)
    gate_grad = masked(contract_rows(panel, dgate_full) * scale, block_mask[0]).astype(jnp.bfloat16)
    up_grad = masked(contract_rows(panel, dup_full) * scale, block_mask[1]).astype(jnp.bfloat16)
    down_grad = masked(contract_rows(act_full, grad_panel) * scale, block_mask[2].T).astype(
        jnp.bfloat16
    )
    return (layer_out, token_grad, gate_grad, up_grad, down_grad)


def solution(mesh):
    in_specs = (
        P("col", "row"),
        P("col", "row"),
        P("row", "col"),
        P("row", "col"),
        P("col", "row"),
        P(None, "row", "col"),
    )
    out_specs = (
        P("col", "row"),
        P("col", "row"),
        P("row", "col"),
        P("row", "col"),
        P("col", "row"),
    )
    return jax.shard_map(shards, mesh=mesh, in_specs=in_specs, out_specs=out_specs, check_vma=False)
```

profile of v0, /device:TPU:1, one launch (start us, length us, event | category | flops | bytes accessed | tf_op | source)
XLA Modules:
  0.0 712.2 jit_solution(12259170415317901651)
XLA Ops:
  9.5 3.9 copy.41
  13.5 2.4 copy.43
  15.9 69.8 %all-gather.3.cloned.1.call-done = bf16[512,1024]{1,0:T(8,128)(2,1)} async-done(((bf16[16,1024]{1,0:T(8,128)(2,1)}), bf16[512,1024]{1,0:T(8,128)(2,1)}) %all-gather.3.cloned.1.call-update) | async-done | bytes 1048592 | tf_op jit(solution)/shard_map/all_gather | solution.py:33
  86.0 1.2 copy-done.13
  87.2 2.6 fusion.3
  90.2 1.7 copy-done.8
  91.9 1.2 fusion.4
  93.2 2.4 copy.52
  95.8 66.3 %all-gather.5.cloned.1.call-done = bf16[512,1024]{1,0:T(8,128)(2,1)} async-done(((bf16[16,1024]{1,0:T(8,128)(2,1)}), bf16[512,1024]{1,0:T(8,128)(2,1)}) %all-gather.5.cloned.1.call-update) | async-done | bytes 1048592 | tf_op jit(solution)/shard_map/all_gather | solution.py:34
  162.5 1.2 copy-done.14
  163.7 2.6 fusion.5
  166.4 1.3 copy.54
  167.7 33.7 %reduce-scatter.13.cloned.1.call-done = bf16[64,1792]{1,0:T(8,128)(2,1)} async-done(((bf16[512,1792]{1,0:T(8,128)(2,1)}), bf16[64,1792]{1,0:T(8,128)(2,1)}) %reduce-scatter.13.cloned.1.call-update) | async-done | bytes 229392 | tf_op jit(solution)/shard_map/reduce_scatter | solution.py:37
  201.4 1.0 convert_element_type.99
  202.4 34.8 %reduce-scatter.15.cloned.1.call-done = bf16[64,896]{1,0:T(8,128)(2,1)} async-done(((bf16[512,896]{1,0:T(8,128)(2,1)}), bf16[64,896]{1,0:T(8,128)(2,1)}) %reduce-scatter.15.cloned.1.call-update) | async-done | bytes 114704 | tf_op jit(solution)/shard_map/reduce_scatter | solution.py:53
  237.2 1.0 fusion.11
  238.2 16.3 %all_gather.18 = bf16[512,896]{1,0:T(8,128)(2,1)S(1)} all-gather(bf16[64,896]{1,0:T(8,128)(2,1)S(1)} %get-tuple-element.26), channel_id=1, replica_groups=mesh['row'=8,'col'=32] {'row'}, dimensions={0}, use_global_device_ids=true | all-gather | bytes 1032192 | tf_op jit(solution)/shard_map/all_gather | solution.py:62
  254.6 3.2 fusion.6
  257.8 13.6 %all_gather.19 = bf16[512,896]{1,0:T(8,128)(2,1)S(1)} all-gather(bf16[64,896]{1,0:T(8,128)(2,1)S(1)} %get-tuple-element.25), channel_id=1, replica_groups=mesh['row'=8,'col'=32] {'row'}, dimensions={0}, use_global_device_ids=true | all-gather | bytes 1032192 | tf_op jit(solution)/shard_map/all_gather | solution.py:63
  271.4 0.9 copy-done.1
  272.3 2.3 add_convert_fusion
  274.6 13.9 %all_gather.16 = bf16[512,896]{1,0:T(8,128)(2,1)S(1)} all-gather(bf16[64,896]{1,0:T(8,128)(2,1)S(1)} %get-tuple-element.27), channel_id=1, replica_groups=mesh['row'=8,'col'=32] {'row'}, dimensions={0}, use_global_device_ids=true | all-gather | bytes 1032192 | tf_op jit(solution)/shard_map/all_gather | solution.py:49
  288.6 0.9 copy-done.5
  289.5 3.8 convolution_convert_fusion
  293.9 0.9 copy-done.4
  294.7 1.6 fusion.2
  296.3 2.5 copy.50
  300.0 1.6 fusion.1
  301.6 2.5 copy.51
  305.5 2.8 fusion
  308.3 177.4 %reduce-scatter.11.cloned.1.call-done = bf16[16,1024]{1,0:T(8,128)(2,1)} async-done(((bf16[512,1024]{1,0:T(8,128)(2,1)}), bf16[16,1024]{1,0:T(8,128)(2,1)}) %reduce-scatter.11.cloned.1.call-update) | async-done | bytes 32784 | tf_op jit(solution)/shard_map/reduce_scatter | solution.py:65
  485.7 219.6 %reduce-scatter.9.cloned.1.call-done = bf16[16,1024]{1,0:T(8,128)(2,1)} async-done(((bf16[512,1024]{1,0:T(8,128)(2,1)}), bf16[16,1024]{1,0:T(8,128)(2,1)}) %reduce-scatter.9.cloned.1.call-update) | async-done | bytes 32784 | tf_op jit(solution)/shard_map/reduce_scatter | solution.py:50
  (56 shorter events, 7.0 us)
Async XLA Ops:
  7.2 78.5 %all-gather.3.cloned.1.call-start = ((), (), s32[]{:S(2)}) async-start(), calls=%async_computation.4 | async-start | bytes 1081344 | tf_op jit(solution)/shard_map/all_gather | solution.py:33
  7.9 154.2 %all-gather.5.cloned.1.call-start = ((), (), s32[]{:S(2)}) async-start(), calls=%async_computation.6 | async-start | bytes 1081344 | tf_op jit(solution)/shard_map/all_gather | solution.py:34
  8.6 192.8 %reduce-scatter.13.cloned.1.call-start = ((), (), s32[]{:S(2)}) async-start(), calls=%async_computation.8 | async-start | bytes 2064384 | tf_op jit(solution)/shard_map/reduce_scatter | solution.py:37
  9.5 4.0 copy-start.7
  85.7 1.5 copy-start
  86.0 1.2 copy-start.13
  89.9 2.0 copy-start.8
  90.2 2.9 copy-start.11
  95.7 141.5 %reduce-scatter.15.cloned.1.call-start = ((), (), s32[]{:S(2)}) async-start(), calls=%async_computation.9 | async-start | bytes 1032192 | tf_op jit(solution)/shard_map/reduce_scatter | solution.py:53
  162.1 1.6 copy-start.16
  162.4 1.3 copy-start.14
  167.6 86.9 %copy-start.10 = (bf16[1024,896]{0,1:T(8,128)(2,1)S(1)}, bf16[1024,896]{0,1:T(8,128)(2,1)}, u32[]{:S(2)}) copy-start(bf16[1024,896]{0,1:T(8,128)(2,1)} %copy.41) | copy-start | bytes 5505028
  167.7 318.0 %reduce-scatter.11.cloned.1.call-start = ((), (), s32[]{:S(2)}) async-start(), calls=%async_computation.7 | async-start | bytes 1081344 | tf_op jit(solution)/shard_map/reduce_scatter | solution.py:65
  254.6 3.2 copy-start.3
  254.6 17.7 %copy-start.9 = (bf16[1024,896]{0,1:T(8,128)(2,1)S(1)}, bf16[1024,896]{0,1:T(8,128)(2,1)}, u32[]{:S(2)}) copy-start(bf16[1024,896]{0,1:T(8,128)(2,1)} %copy.43) | copy-start | bytes 5505028
  254.6 17.7 %copy-start.12 = (bf16[8,128,7,128]{1,0,3,2:T(8,128)(2,1)S(1)}, bf16[8,128,7,128]{1,0,3,2:T(8,128)(2,1)}, u32[]{:S(2)}) copy-start(bf16[8,128,7,128]{1,0,3,2:T(8,128)(2,1)} %copy-done.11) | copy-start | bytes 5505028
  271.4 0.9 copy-start.1
  274.6 14.9 %copy-start.15 = (bf16[7,128,8,128]{3,2,1,0:T(8,128)(2,1)S(1)}, bf16[7,128,8,128]{3,2,1,0:T(8,128)(2,1)}, u32[]{:S(2)}) copy-start(bf16[7,128,8,128]{3,2,1,0:T(8,128)(2,1)} %copy-done.14) | copy-start | bytes 5505028
  274.6 430.8 %reduce-scatter.9.cloned.1.call-start = ((), (), s32[]{:S(2)}) async-start(), calls=%async_computation.5 | async-start | bytes 1081344 | tf_op jit(solution)/shard_map/reduce_scatter | solution.py:50
  288.6 0.9 copy-start.5
  293.6 1.2 copy-start.4
  298.8 1.2 copy-start.2
  304.0 1.2 copy-start.6
  304.0 1.5 copy-start.17
Sparse Core Ops, SparseCore 0:
  10.6 75.0 all-gather.2
  88.3 73.8 all-gather.4
  165.3 36.0 reduce-scatter.12
  203.8 33.3 reduce-scatter.14
  274.7 210.9 reduce-scatter.10
  489.9 215.3 reduce-scatter.8
where the time goes:
time: 717 us; the launch traced here: 712 us
  waiting for transfers between devices  603 us (84%)
  blocking collectives  43.9 us (6%)
  local copies, waits for them, and re-layouts  26.2 us (4%)
  matrix products  21.7 us (3%)
  between operations  14.3 us (2%)
    reduce_scatter x1, waiting for transfers between devices, shards(): lax.psum_scatter(product(act_full, masked_down).astype(jnp.bfloat16), 'co...  220 us
    reduce_scatter x1, waiting for transfers between devices, shards(): lax.psum_scatter((product_t(dgate_full, masked_gate) + product_t(dup_full...  177 us
    all_gather x1, waiting for transfers between devices, shards(): panel = lax.all_gather(tokens, 'col', axis=0, tiled=True)  69.8 us
    all_gather x1, waiting for transfers between devices, shards(): grad_panel = lax.all_gather(cotangent, 'col', axis=0, tiled=True)  66.3 us
    reduce_scatter x1, waiting for transfers between devices, shards(): lax.psum_scatter(product_t(grad_panel, masked_down).astype(jnp.bfloat16),...  34.8 us
    reduce_scatter x1, waiting for transfers between devices, shards(): lax.psum_scatter(jnp.concatenate([product(panel, masked_gate), product(pa...  33.7 us
    unnamed x42, local copies, waits for them, and re-layouts  23.9 us
    all_gather x1, blocking collectives, shards(): lax.all_gather(dgate, 'row', axis=0, tiled=True)  16.3 us
  transfers between devices with their start and end apart: 6, of which 6 were waited for; matrix products, arithmetic and copies ran while one was open for 5% of the time, Pallas kernels for 0%

commit v1 on v0

--- a/solution.py
+++ b/solution.py
@@ -26,48 +26,62 @@
     )
 
 
+def gather_rows(local, axis, size):
+    sent = jnp.broadcast_to(local[None], (size,) + local.shape)
+    got = lax.all_to_all(sent, axis, 0, 0, tiled=False)
+    return got.reshape((size * local.shape[0],) + local.shape[1:])
+
+
+def reduce_rows(partial, axis, size):
+    chunks = partial.astype(jnp.bfloat16).reshape((size, partial.shape[0] // size) + partial.shape[1:])
+    got = lax.all_to_all(chunks, axis, 0, 0, tiled=False)
+    return got.astype(jnp.float32).sum(axis=0)
+
+
 def shards(tokens, cotangent, gate_weight, up_weight, down_weight, block_mask):
+    n_row = lax.axis_size("row")
+    n_col = lax.axis_size("col")
     masked_gate = masked(gate_weight, block_mask[0])
     masked_up = masked(up_weight, block_mask[1])
     masked_down = masked(down_weight, block_mask[2].T)
-    panel = lax.all_gather(tokens, "col", axis=0, tiled=True)
-    grad_panel = lax.all_gather(cotangent, "col", axis=0, tiled=True)
+    feat = tokens.shape[1]
+    both = gather_rows(jnp.concatenate([tokens, cotangent], axis=1), "col", n_col)
+    panel = both[:, :feat]
+    grad_panel = both[:, feat:]
     total_rows = panel.shape[0]
     width = masked_gate.shape[1]
-    stacked = lax.psum_scatter(
-        jnp.concatenate([product(panel, masked_gate), product(panel, masked_up)], axis=1).astype(
-            jnp.bfloat16
-        ),
-        "row",
-        scatter_dimension=0,
-        tiled=True,
-    ).astype(jnp.float32)
-    gate = stacked[:, :width]
-    up = stacked[:, width:]
+    partials = jnp.concatenate(
+        [
+            product(panel, masked_gate).astype(jnp.bfloat16),
+            product(panel, masked_up).astype(jnp.bfloat16),
+            product_t(grad_panel, masked_down).astype(jnp.bfloat16),
+        ],
+        axis=1,
+    )
+    sums = reduce_rows(partials, "row", n_row)
+    gate = sums[:, :width]
+    up = sums[:, width : 2 * width]
+    dact = sums[:, 2 * width :]
     sigma = jax.nn.sigmoid(gate)
     act = (gate * sigma * up).astype(jnp.bfloat16)
-    act_full = lax.all_gather(act, "row", axis=0, tiled=True)
-    layer_out = lax.psum_scatter(
-        product(act_full, masked_down).astype(jnp.bfloat16), "col", scatter_dimension=0, tiled=True
-    )
-    dact = lax.psum_scatter(
-        product_t(grad_panel, masked_down).astype(jnp.bfloat16),
-        "row",
-        scatter_dimension=0,
-        tiled=True,
-    ).astype(jnp.float32)
     dgate = (dact * up * sigma * (1.0 + gate * (1.0 - sigma))).astype(jnp.bfloat16)
     dup = (dact * gate * sigma).astype(jnp.bfloat16)
-    dgate_full, dup_full = (
-        lax.all_gather(dgate, "row", axis=0, tiled=True),
-        lax.all_gather(dup, "row", axis=0, tiled=True),
+    full = lax.all_gather(jnp.concatenate([act, dgate, dup], axis=1), "row", axis=0, tiled=True)
+    act_full = full[:, :width]
+    dgate_full = full[:, width : 2 * width]
+    dup_full = full[:, 2 * width :]
+    out_partials = jnp.concatenate(
+        [
+            product(act_full, masked_down).astype(jnp.bfloat16),
+            (product_t(dgate_full, masked_gate) + product_t(dup_full, masked_up)).astype(
+                jnp.bfloat16
+            ),
+        ],
+        axis=1,
     )
-    token_grad = lax.psum_scatter(
-        (product_t(dgate_full, masked_gate) + product_t(dup_full, masked_up)).astype(jnp.bfloat16),
-        "col",
-        scatter_dimension=0,
-        tiled=True,
-    )
+    outs = reduce_rows(out_partials, "col", n_col).astype(jnp.bfloat16)
+    layer_out = outs[:, :feat]
+    token_grad = outs[:, feat:]
     scale = total_rows ** (-0.5)
     gate_grad = masked(contract_rows(panel, dgate_full) * scale, block_mask[0]).astype(jnp.bfloat16)
     up_grad = masked(contract_rows(panel, dup_full) * scale, block_mask[1]).astype(jnp.bfloat16)

time: 717 us -> 223 us (0.31)
  waiting for transfers between devices: 603 us -> 87.7 us
  starting transfers between devices: 0.24 us -> 22.1 us
    reduce_scatter x4 -> x0, waiting for transfers between devices: 466 us -> none  [the longest x1 220 us: shards(): lax.psum_scatter(product(act_full, masked_down).astype(jnp.bfloat16), 'co...]
    all_gather x2 -> x1, waiting for transfers between devices: 136 us -> 25.1 us  [shards(): lax.all_gather(jnp.concatenate([act, dgate, dup], axis=1), 'row', axis=0,...]
    all_to_all x0 -> x2, waiting for transfers between devices: none -> 62.6 us  [the longest x1 41 us: gather_rows(): got = lax.all_to_all(sent, axis, 0, 0, tiled=False)]
    all_gather x3 -> x0, blocking collectives: 43.9 us -> none  [the longest x1 16.3 us: shards(): lax.all_gather(dgate, 'row', axis=0, tiled=True)]
    all_to_all x0 -> x1, blocking collectives: none -> 39.6 us  [reduce_rows(): got = lax.all_to_all(chunks, axis, 0, 0, tiled=False)]
    all_to_all x0 -> x2, starting transfers between devices: none -> 22 us  [the longest x1 12.2 us: gather_rows(): got = lax.all_to_all(sent, axis, 0, 0, tiled=False)]
    mul x6 -> x8, local copies, waits for them, and re-layouts: 1.81 us -> 11.8 us  [masked(): shaped * mask.astype(weight.dtype)[:, None, :, None]]
    unnamed x42 -> x30, local copies, waits for them, and re-layouts: 23.9 us -> 15.6 us
  transfers between devices with their start and end apart: 6 -> 3, of which waited for: 6 -> 3; matrix products, arithmetic and copies ran while one was open for 5% -> 16% of each run, Pallas kernels for 0% -> 0%
where the time goes in v1:
time: 223 us; the launch traced here: 222 us
  waiting for transfers between devices  87.7 us (39%)
  blocking collectives  39.6 us (18%)
  local copies, waits for them, and re-layouts  30.2 us (14%)
  matrix products  22.8 us (10%)
  starting transfers between devices  22.1 us (10%)
  between operations  14.3 us (6%)
  other arithmetic  5.63 us (3%)
    all_to_all x1, waiting for transfers between devices, gather_rows(): got = lax.all_to_all(sent, axis, 0, 0, tiled=False)  41 us
    all_to_all x1, blocking collectives, reduce_rows(): got = lax.all_to_all(chunks, axis, 0, 0, tiled=False)  39.6 us
    all_gather x1, waiting for transfers between devices, shards(): lax.all_gather(jnp.concatenate([act, dgate, dup], axis=1), 'row', axis=0,...  25.1 us
    all_to_all x1, waiting for transfers between devices, reduce_rows(): got = lax.all_to_all(chunks, axis, 0, 0, tiled=False)  21.6 us
    unnamed x30, local copies, waits for them, and re-layouts  15.6 us
    all_to_all x1, starting transfers between devices, gather_rows(): got = lax.all_to_all(sent, axis, 0, 0, tiled=False)  12.2 us
    mul x8, local copies, waits for them, and re-layouts, masked(): shaped * mask.astype(weight.dtype)[:, None, :, None]  11.8 us
    dot_general x3, matrix products, contract_rows(): lax.dot_general(left, right, (((0,), (0,)), ((), ())), preferred_element_...  10.4 us
  transfers between devices with their start and end apart: 3, of which 3 were waited for; matrix products, arithmetic and copies ran while one was open for 16% of the time, Pallas kernels for 0%

profile of v1, /device:TPU:1, one launch (start us, length us, event | category | flops | bytes accessed | tf_op | source)
XLA Modules:
  0.0 222.2 jit_solution(18016851430393765211)
XLA Ops:
  7.2 0.8 pad_maximum_fusion.3
  7.9 1.6 broadcast_in_dim.2
  9.5 12.2 %all-to-all-start = ((bf16[32,16,2048]{2,1,0:T(8,128)(2,1)}), bf16[32,16,2048]{2,1,0:T(8,128)(2,1)S(1)}, u32[]{:S(2)}, u32[]{:S(2)}) async-start(bf16[32,16,2048]{2,1,0:T(8,128)(2,1)} %broadcast_in_dim.2), calls=%async_computation | async-start | bytes 4194304 | tf_op jit(solution)/shard_map/all_to_all | solution.py:31
  22.1 3.8 %copy.14 = bf16[1024,896]{0,1:T(8,128)(2,1)} copy(bf16[1024,896]{1,0:T(8,128)(2,1)} %param.8) | data formatting | bytes 3670016 | tf_op args[2]
  25.8 3.8 %copy.16 = bf16[1024,896]{0,1:T(8,128)(2,1)} copy(bf16[1024,896]{1,0:T(8,128)(2,1)} %param.9) | data formatting | bytes 3670016 | tf_op args[3]
  29.6 41.0 %all-to-all-done = bf16[32,16,2048]{2,1,0:T(8,128)(2,1)S(1)} async-done(((bf16[32,16,2048]{2,1,0:T(8,128)(2,1)}), bf16[32,16,2048]{2,1,0:T(8,128)(2,1)S(1)}, u32[]{:S(2)}, u32[]{:S(2)}) %all-to-all-start) | async-done | bytes 2097184 | tf_op jit(solution)/shard_map/all_to_all | solution.py:31
  70.9 3.5 %convolution_convert_fusion.2 = bf16[512,896]{1,0:T(8,128)(2,1)S(1)} fusion(bf16[512,2048]{1,0:T(8,128)(2,1)S(1)} %bitcast.66, bf16[1024,896]{0,1:T(8,128)(2,1)} %copy.16, bf16[112,8,8,128]{3,2,1,0:T(8,128)(2,1)S(1)} %bitcast.74), kind=kOutput, calls=%fused_computation.15 | convolution fusion | flops 940900352 | bytes 5636096 | tf_op jit(solution)/shard_map/dot_general | solution.py:14
  74.8 1.3 convolution_convert_fusion.1
  76.4 1.2 copy-done.7
  77.7 1.3 convolution_convert_fusion.3
  79.2 39.6 %all_to_all.15 = bf16[8,64,2688]{2,1,0:T(8,128)(2,1)S(1)} all-to-all(bf16[8,64,2688]{2,1,0:T(8,128)(2,1)S(1)} %bitcast.65), channel_id=1, replica_groups=mesh['row'=8,'col'=32] {'row'}, dimensions={0} | all-to-all | bytes 5505024 | tf_op jit(solution)/shard_map/all_to_all | solution.py:37
  118.8 0.4 convert_reduce_fusion
  119.3 0.8 pad_maximum_fusion.2
  120.1 25.1 %all-gather.2.cloned.1.call-done = bf16[512,2688]{1,0:T(8,128)(2,1)} async-done(((bf16[64,2688]{1,0:T(8,128)(2,1)}), bf16[512,2688]{1,0:T(8,128)(2,1)}) %all-gather.2.cloned.1.call-update) | async-done | bytes 2752528 | tf_op jit(solution)/shard_map/all_gather | solution.py:69
  145.2 3.7 %fusion.6 = f32[512,1024]{1,0:T(8,128)S(1)} fusion(bf16[512,2688]{1,0:T(8,128)(2,1)} %all-gather.2.cloned.1.call-done, bf16[1024,896]{0,1:T(8,128)(2,1)} %copy.14, bf16[112,8,8,128]{3,2,1,0:T(8,128)(2,1)} %bitcast.79), kind=kOutput, calls=%fused_computation.22 | convolution fusion | flops 940441600 | bytes 6684672 | tf_op jit(solution)/shard_map/dot_general | solution.py:18
  148.9 0.5 copy-done.12
  149.4 1.3 convolution_convert_fusion
  150.9 0.6 copy-done.4
  151.5 1.3 add_convert_fusion
  152.7 1.5 pad_maximum_fusion.1
  154.2 9.9 %all-to-all-start.2 = ((bf16[32,16,2048]{2,1,0:T(8,128)(2,1)}), bf16[32,16,2048]{2,1,0:T(8,128)(2,1)}, u32[]{:S(2)}, u32[]{:S(2)}) async-start(bf16[32,16,2048]{2,1,0:T(8,128)(2,1)} %bitcast.72), calls=%async_computation.2 | async-start | bytes 4194304 | tf_op jit(solution)/shard_map/all_to_all | solution.py:37
  164.3 0.3 mul.124
  164.7 2.7 %copy.41 = f32[112,8,8,128]{3,1,2,0:T(8,128)} copy(f32[112,8,8,128]{3,2,1,0:T(8,128)S(1)} %bitcast.63) | data formatting | bytes 7340032
  167.4 5.0 %copy.21 = f32[1024,896]{1,0:T(8,128)} copy(f32[1024,896]{0,1:T(8,128)} %bitcast.61) | data formatting | bytes 7340032 | tf_op jit(solution)/shard_map/mul | solution.py:10
  172.7 2.8 %copy.42 = f32[112,8,8,128]{3,1,2,0:T(8,128)} copy(f32[112,8,8,128]{3,2,1,0:T(8,128)S(1)} %bitcast.64) | data formatting | bytes 7340032
  175.5 5.0 %copy.19 = f32[1024,896]{1,0:T(8,128)} copy(f32[1024,896]{0,1:T(8,128)} %bitcast.62) | data formatting | bytes 7340032 | tf_op jit(solution)/shard_map/mul | solution.py:10
  180.5 5.0 %multiply_convert_fusion = bf16[1024,896]{1,0:T(8,128)(2,1)} fusion(f32[1024,896]{1,0:T(8,128)} %copy.21, bf16[512,2688]{1,0:T(8,128)(2,1)} %all-gather.2.cloned.1.call-done, bf16[512,2048]{1,0:T(8,128)(2,1)S(1)} %bitcast.69), kind=kOutput, calls=%fused_computation.5 | convolution fusion | flops 942276608 | bytes 7471104 | tf_op jit(solution)/shard_map/dot_general | solution.py:24
  185.5 2.6 %multiply_convert_fusion.1 = bf16[1024,896]{1,0:T(8,128)(2,1)} fusion(f32[1024,896]{1,0:T(8,128)S(1)} %copy-done, bf16[512,2688]{1,0:T(8,128)(2,1)S(1)} %copy-done.9, bf16[512,2048]{1,0:T(8,128)(2,1)S(1)} %bitcast.70), kind=kOutput, calls=%fused_computation.6 | convolution fusion | flops 942276608 | bytes 7471104 | tf_op jit(solution)/shard_map/dot_general | solution.py:24
  188.4 2.8 %fusion = bf16[896,1024]{1,0:T(8,128)(2,1)} fusion(f32[112,8,8,128]{3,2,1,0:T(8,128)S(1)} %bitcast.73, bf16[512,2048]{1,0:T(8,128)(2,1)S(1)} %bitcast.71, bf16[512,2688]{1,0:T(8,128)(2,1)S(1)} %copy-done.9), kind=kOutput, calls=%fused_computation.2 | convolution fusion | flops 942276608 | bytes 7471104 | tf_op jit(solution)/shard_map/dot_general | solution.py:24
  191.2 21.6 %all-to-all-done.2 = bf16[32,16,2048]{2,1,0:T(8,128)(2,1)} async-done(((bf16[32,16,2048]{2,1,0:T(8,128)(2,1)}), bf16[32,16,2048]{2,1,0:T(8,128)(2,1)}, u32[]{:S(2)}, u32[]{:S(2)}) %all-to-all-start.2) | async-done | bytes 2097184 | tf_op jit(solution)/shard_map/all_to_all | solution.py:37
  212.8 1.9 reduce_sum.22
  214.7 0.6 fusion.17
  (39 shorter events, 2.7 us)
Async XLA Ops:
  9.5 12.2 %copy-start.10 = (s32[3,8,7]{2,1,0:T(8,128)S(1)}, s32[3,8,7]{2,1,0:T(8,128)}, u32[]{:S(2)}) copy-start(s32[3,8,7]{2,1,0:T(8,128)} %param.11) | copy-start | bytes 2020
  9.5 61.1 %all-to-all-start = ((bf16[32,16,2048]{2,1,0:T(8,128)(2,1)}), bf16[32,16,2048]{2,1,0:T(8,128)(2,1)S(1)}, u32[]{:S(2)}, u32[]{:S(2)}) async-start(bf16[32,16,2048]{2,1,0:T(8,128)(2,1)} %broadcast_in_dim.2), calls=%async_computation | async-start | bytes 4194304 | tf_op jit(solution)/shard_map/all_to_all | solution.py:31
  21.7 123.4 %all-gather.2.cloned.1.call-start = ((), (), s32[]{:S(2)}) async-start(), calls=%async_computation.3 | async-start | bytes 3096576 | tf_op jit(solution)/shard_map/all_gather | solution.py:69
  70.9 3.5 %copy-start.3 = (bf16[8,128,7,128]{1,0,3,2:T(8,128)(2,1)}, bf16[8,128,7,128]{1,0,3,2:T(8,128)(2,1)S(1)}, u32[]{:S(2)}) copy-start(bf16[8,128,7,128]{1,0,3,2:T(8,128)(2,1)S(1)} %mul.105) | copy-start | bytes 5505028
  70.9 3.9 %copy-start.11 = (bf16[896,1024]{1,0:T(8,128)(2,1)S(1)}, bf16[896,1024]{1,0:T(8,128)(2,1)}, u32[]{:S(2)}) copy-start(bf16[896,1024]{1,0:T(8,128)(2,1)} %param.10) | copy-start | bytes 5505028
  74.8 1.3 copy-start.5
  74.8 2.9 %copy-start.2 = (bf16[1024,896]{0,1:T(8,128)(2,1)S(1)}, bf16[1024,896]{0,1:T(8,128)(2,1)}, u32[]{:S(2)}) copy-start(bf16[1024,896]{0,1:T(8,128)(2,1)} %copy.14) | copy-start | bytes 5505028
  76.4 1.2 copy-start.7
  145.2 3.8 %copy-start.6 = (bf16[7,128,8,128]{3,2,1,0:T(8,128)(2,1)S(1)}, bf16[7,128,8,128]{3,2,1,0:T(8,128)(2,1)}, u32[]{:S(2)}) copy-start(bf16[7,128,8,128]{3,2,1,0:T(8,128)(2,1)} %copy-done.5) | copy-start | bytes 5505028
  145.2 3.8 %copy-start.8 = (bf16[512,2688]{1,0:T(8,128)(2,1)S(1)}, bf16[512,2688]{1,0:T(8,128)(2,1)}, u32[]{:S(2)}) copy-start(bf16[512,2688]{1,0:T(8,128)(2,1)} %all-gather.2.cloned.1.call-done) | copy-start | bytes 8257540
  145.2 4.3 %copy-start.12 = (bf16[896,1024]{1,0:T(8,128)(2,1)S(1)}, bf16[896,1024]{1,0:T(8,128)(2,1)}, u32[]{:S(2)}) copy-start(bf16[896,1024]{1,0:T(8,128)(2,1)} %param.10) | copy-start | bytes 5505028
  149.4 1.5 copy-start.1
  149.4 2.0 copy-start.4
  154.2 58.6 %all-to-all-start.2 = ((bf16[32,16,2048]{2,1,0:T(8,128)(2,1)}), bf16[32,16,2048]{2,1,0:T(8,128)(2,1)}, u32[]{:S(2)}, u32[]{:S(2)}) async-start(bf16[32,16,2048]{2,1,0:T(8,128)(2,1)} %bitcast.72), calls=%async_computation.2 | async-start | bytes 4194304 | tf_op jit(solution)/shard_map/all_to_all | solution.py:37
  180.5 5.0 %copy-start = (f32[1024,896]{1,0:T(8,128)S(1)}, f32[1024,896]{1,0:T(8,128)}, u32[]{:S(2)}) copy-start(f32[1024,896]{1,0:T(8,128)} %copy.19) | copy-start | bytes 11010052
  180.5 5.0 %copy-start.9 = (bf16[512,2688]{1,0:T(8,128)(2,1)S(1)}, bf16[512,2688]{1,0:T(8,128)(2,1)}, u32[]{:S(2)}) copy-start(bf16[512,2688]{1,0:T(8,128)(2,1)} %all-gather.2.cloned.1.call-done) | copy-start | bytes 8257540
Sparse Core Ops, SparseCore 0:
  120.2 24.9 all-gather.1

commit v2 on v1

--- a/solution.py
+++ b/solution.py
@@ -45,43 +45,36 @@
     masked_up = masked(up_weight, block_mask[1])
     masked_down = masked(down_weight, block_mask[2].T)
     feat = tokens.shape[1]
-    both = gather_rows(jnp.concatenate([tokens, cotangent], axis=1), "col", n_col)
-    panel = both[:, :feat]
-    grad_panel = both[:, feat:]
+    panel = gather_rows(tokens, "col", n_col)
+    grad_panel = gather_rows(cotangent, "col", n_col)
     total_rows = panel.shape[0]
     width = masked_gate.shape[1]
-    partials = jnp.concatenate(
-        [
-            product(panel, masked_gate).astype(jnp.bfloat16),
-            product(panel, masked_up).astype(jnp.bfloat16),
-            product_t(grad_panel, masked_down).astype(jnp.bfloat16),
-        ],
-        axis=1,
+    fwd = reduce_rows(
+        jnp.concatenate(
+            [
+                product(panel, masked_gate).astype(jnp.bfloat16),
+                product(panel, masked_up).astype(jnp.bfloat16),
+            ],
+            axis=1,
+        ),
+        "row",
+        n_row,
     )
-    sums = reduce_rows(partials, "row", n_row)
-    gate = sums[:, :width]
-    up = sums[:, width : 2 * width]
-    dact = sums[:, 2 * width :]
+    gate = fwd[:, :width]
+    up = fwd[:, width:]
     sigma = jax.nn.sigmoid(gate)
     act = (gate * sigma * up).astype(jnp.bfloat16)
+    act_full = lax.all_gather(act, "row", axis=0, tiled=True)
+    layer_out = reduce_rows(product(act_full, masked_down), "col", n_col).astype(jnp.bfloat16)
+    dact = reduce_rows(product_t(grad_panel, masked_down), "row", n_row)
     dgate = (dact * up * sigma * (1.0 + gate * (1.0 - sigma))).astype(jnp.bfloat16)
     dup = (dact * gate * sigma).astype(jnp.bfloat16)
-    full = lax.all_gather(jnp.concatenate([act, dgate, dup], axis=1), "row", axis=0, tiled=True)
-    act_full = full[:, :width]
-    dgate_full = full[:, width : 2 * width]
-    dup_full = full[:, 2 * width :]
-    out_partials = jnp.concatenate(
-        [
-            product(act_full, masked_down).astype(jnp.bfloat16),
-            (product_t(dgate_full, masked_gate) + product_t(dup_full, masked_up)).astype(
-                jnp.bfloat16
-            ),
-        ],
-        axis=1,
-    )
-    outs = reduce_rows(out_partials, "col", n_col).astype(jnp.bfloat16)
-    layer_out = outs[:, :feat]
-    token_grad = outs[:, feat:]
+    full = lax.all_gather(jnp.concatenate([dgate, dup], axis=1), "row", axis=0, tiled=True)
+    dgate_full = full[:, :width]
+    dup_full = full[:, width:]
+    token_grad = reduce_rows(
+        product_t(dgate_full, masked_gate) + product_t(dup_full, masked_up), "col", n_col
+    ).astype(jnp.bfloat16)
     scale = total_rows ** (-0.5)
     gate_grad = masked(contract_rows(panel, dgate_full) * scale, block_mask[0]).astype(jnp.bfloat16)
     up_grad = masked(contract_rows(panel, dup_full) * scale, block_mask[1]).astype(jnp.bfloat16)

time: 223 us -> 225 us (level); the launches traced: 222 us -> 221 us
  waiting for transfers between devices: 87.7 us -> 60.2 us
  blocking collectives: 39.6 us -> 52.2 us
  starting transfers between devices: 22.1 us -> 33.9 us
  matrix products: 22.8 us -> 28 us
    all_to_all x1, waiting for transfers between devices: 41 us -> 14.7 us  [gather_rows(): got = lax.all_to_all(sent, axis, 0, 0, tiled=False)]
    all_gather x1, waiting for transfers between devices: 25.1 us -> 0.02 us  [shards(): lax.all_gather(jnp.concatenate([dgate, dup], axis=1), 'row', axis=0, tile...]
    all_to_all x1 -> x4, waiting for transfers between devices: 21.6 us -> 45.4 us  [reduce_rows(): got = lax.all_to_all(chunks, axis, 0, 0, tiled=False)]
    all_gather x0 -> x1, blocking collectives: none -> 15.5 us  [shards(): act_full = lax.all_gather(act, 'row', axis=0, tiled=True)]
    all_to_all x1 -> x4, starting transfers between devices: 9.88 us -> 25.4 us  [reduce_rows(): got = lax.all_to_all(chunks, axis, 0, 0, tiled=False)]
    mul x8 -> x6, local copies, waits for them, and re-layouts: 11.8 us -> 1.81 us  [masked(): shaped * mask.astype(weight.dtype)[:, None, :, None]]
    unnamed x30 -> x38, local copies, waits for them, and re-layouts: 15.6 us -> 21.6 us
    all_to_all x1, starting transfers between devices: 12.2 us -> 8.47 us  [gather_rows(): got = lax.all_to_all(sent, axis, 0, 0, tiled=False)]
  transfers between devices with their start and end apart: 3 -> 6, of which waited for: 3 -> 5; matrix products, arithmetic and copies ran while one was open for 16% -> 22% of each run, Pallas kernels for 0% -> 0%
where the time goes in v2:
time: 225 us; the launch traced here: 221 us
  waiting for transfers between devices  60.2 us (27%)
  blocking collectives  52.2 us (23%)
  starting transfers between devices  33.9 us (15%)
  local copies, waits for them, and re-layouts  28.3 us (13%)
  matrix products  28 us (12%)
  between operations  14.3 us (6%)
  other arithmetic  4.1 us (2%)
    all_to_all x4, waiting for transfers between devices, reduce_rows(): got = lax.all_to_all(chunks, axis, 0, 0, tiled=False)  45.4 us
    all_to_all x1, blocking collectives, gather_rows(): got = lax.all_to_all(sent, axis, 0, 0, tiled=False)  36.7 us
    all_to_all x4, starting transfers between devices, reduce_rows(): got = lax.all_to_all(chunks, axis, 0, 0, tiled=False)  25.4 us
    unnamed x38, local copies, waits for them, and re-layouts  21.6 us
    all_gather x1, blocking collectives, shards(): act_full = lax.all_gather(act, 'row', axis=0, tiled=True)  15.5 us
    all_to_all x1, waiting for transfers between devices, gather_rows(): got = lax.all_to_all(sent, axis, 0, 0, tiled=False)  14.7 us
    dot_general x3, matrix products, contract_rows(): lax.dot_general(left, right, (((0,), (0,)), ((), ())), preferred_element_...  10.9 us
    dot_general x3, matrix products, product(): return jnp.dot(left, weight, preferred_element_type=jnp.float32)  8.87 us
  transfers between devices with their start and end apart: 6, of which 5 were waited for; matrix products, arithmetic and copies ran while one was open for 22% of the time, Pallas kernels for 0%

profile of v2, /device:TPU:1, one launch (start us, length us, event | category | flops | bytes accessed | tf_op | source)
XLA Modules:
  0.0 220.9 jit_solution(11346078941495549265)
XLA Ops:
  8.1 36.7 %all_to_all.30 = bf16[32,16,1024]{2,1,0:T(8,128)(2,1)S(1)} all-to-all(bf16[32,16,1024]{2,1,0:T(8,128)(2,1)S(1)} %broadcast_in_dim.5), channel_id=1, replica_groups=mesh['row'=8,'col'=32] {'col'}, dimensions={0} | all-to-all | bytes 2097152 | tf_op jit(solution)/shard_map/all_to_all | solution.py:31
  45.9 8.5 %all-to-all-start = ((bf16[32,16,1024]{2,1,0:T(8,128)(2,1)}), bf16[32,16,1024]{2,1,0:T(8,128)(2,1)}, u32[]{:S(2)}, u32[]{:S(2)}) async-start(bf16[32,16,1024]{2,1,0:T(8,128)(2,1)} %broadcast_in_dim.4), calls=%async_computation | async-start | bytes 2097152 | tf_op jit(solution)/shard_map/all_to_all | solution.py:31
  54.5 2.4 %copy.20 = bf16[1024,896]{0,1:T(8,128)(2,1)} copy(bf16[1024,896]{1,0:T(8,128)(2,1)S(1)} %copy-done.2) | data formatting | bytes 3670016 | tf_op args[3]
  56.9 3.8 %copy.18 = bf16[1024,896]{0,1:T(8,128)(2,1)} copy(bf16[1024,896]{1,0:T(8,128)(2,1)} %param.8) | data formatting | bytes 3670016 | tf_op args[2]
  61.1 1.2 copy-done.8
  62.5 2.3 %convolution_convert_fusion.1 = bf16[896,512]{0,1:T(8,128)(2,1)} fusion(bf16[512,1024]{1,0:T(8,128)(2,1)S(1)} %bitcast.85, bf16[896,1024]{1,0:T(8,128)(2,1)S(1)} %copy-done.13, bf16[112,8,8,128]{3,2,1,0:T(8,128)(2,1)S(1)} %bitcast.91), kind=kOutput, calls=%fused_computation.14 | convolution fusion | flops 940900352 | bytes 5636096 | tf_op jit(solution)/shard_map/dot_general | solution.py:18
  64.8 14.7 %all-to-all-done = bf16[32,16,1024]{2,1,0:T(8,128)(2,1)} async-done(((bf16[32,16,1024]{2,1,0:T(8,128)(2,1)}), bf16[32,16,1024]{2,1,0:T(8,128)(2,1)}, u32[]{:S(2)}, u32[]{:S(2)}) %all-to-all-start) | async-done | bytes 1048608 | tf_op jit(solution)/shard_map/all_to_all | solution.py:31
  79.5 9.0 %all-to-all-start.4 = ((bf16[8,64,896]{2,1,0:T(8,128)(2,1)}), bf16[8,64,896]{2,1,0:T(8,128)(2,1)}, u32[]{:S(2)}, u32[]{:S(2)}) async-start(bf16[8,64,896]{2,1,0:T(8,128)(2,1)} %bitcast.97), calls=%async_computation.4 | async-start | bytes 1835008 | tf_op jit(solution)/shard_map/all_to_all | solution.py:37
  88.8 1.2 copy-done.6
  90.0 2.4 %fusion.4 = bf16[512,896]{0,1:T(8,128)(2,1)S(1)} fusion(bf16[512,1024]{1,0:T(8,128)(2,1)} %bitcast.1, bf16[1024,896]{0,1:T(8,128)(2,1)S(1)} %copy-done.3, bf16[112,8,8,128]{3,2,1,0:T(8,128)(2,1)S(1)} %bitcast.89), kind=kOutput, calls=%fused_computation.18 | convolution fusion | flops 940900352 | bytes 5636096 | tf_op jit(solution)/shard_map/dot_general | solution.py:14
  92.7 1.7 copy-done.5
  94.4 2.4 %fusion.3 = bf16[512,896]{0,1:T(8,128)(2,1)S(1)} fusion(bf16[512,1024]{1,0:T(8,128)(2,1)} %bitcast.1, bf16[1024,896]{0,1:T(8,128)(2,1)S(1)} %copy-done.5, bf16[112,8,8,128]{3,2,1,0:T(8,128)(2,1)S(1)} %bitcast.93), kind=kOutput, calls=%fused_computation.17 | convolution fusion | flops 940900352 | bytes 5636096 | tf_op jit(solution)/shard_map/dot_general | solution.py:14
  97.0 2.4 %copy.21 = bf16[512,1792]{1,0:T(8,128)(2,1)} copy(bf16[512,1792]{0,1:T(8,128)(2,1)S(1)} %pad_maximum_fusion) | data formatting | bytes 3670016 | tf_op jit(solution)/shard_map/concatenate | solution.py:53
  99.4 2.8 %all-to-all-done.4 = bf16[8,64,896]{2,1,0:T(8,128)(2,1)} async-done(((bf16[8,64,896]{2,1,0:T(8,128)(2,1)}), bf16[8,64,896]{2,1,0:T(8,128)(2,1)}, u32[]{:S(2)}, u32[]{:S(2)}) %all-to-all-start.4) | async-done | bytes 917536 | tf_op jit(solution)/shard_map/all_to_all | solution.py:37
  102.1 4.5 %all-to-all-start.1 = ((bf16[8,64,1792]{2,1,0:T(8,128)(2,1)}), bf16[8,64,1792]{2,1,0:T(8,128)(2,1)S(1)}, u32[]{:S(2)}, u32[]{:S(2)}) async-start(bf16[8,64,1792]{2,1,0:T(8,128)(2,1)} %bitcast.5), calls=%async_computation.1 | async-start | bytes 3670016 | tf_op jit(solution)/shard_map/all_to_all | solution.py:37
  106.6 1.3 convert_reduce_fusion.1
  107.9 22.1 %all-to-all-done.1 = bf16[8,64,1792]{2,1,0:T(8,128)(2,1)S(1)} async-done(((bf16[8,64,1792]{2,1,0:T(8,128)(2,1)}), bf16[8,64,1792]{2,1,0:T(8,128)(2,1)S(1)}, u32[]{:S(2)}, u32[]{:S(2)}) %all-to-all-start.1) | async-done | bytes 1835040 | tf_op jit(solution)/shard_map/all_to_all | solution.py:37
  131.2 15.5 %all_gather.6 = bf16[512,896]{1,0:T(8,128)(2,1)S(1)} all-gather(bf16[64,896]{1,0:T(8,128)(2,1)S(1)} %get-tuple-element.17), channel_id=1, replica_groups=mesh['row'=8,'col'=32] {'row'}, dimensions={0}, use_global_device_ids=true | all-gather | bytes 1032192 | tf_op jit(solution)/shard_map/all_gather | solution.py:67
  146.7 4.1 %convolution_convert_fusion = bf16[512,1024]{1,0:T(8,128)(2,1)} fusion(bf16[512,896]{1,0:T(8,128)(2,1)S(1)} %all_gather.6, bf16[896,1024]{1,0:T(8,128)(2,1)} %param.10, bf16[112,8,8,128]{3,2,1,0:T(8,128)(2,1)S(1)} %bitcast.92), kind=kOutput, calls=%fused_computation.13 | convolution fusion | flops 940965888 | bytes 5636096 | tf_op jit(solution)/shard_map/dot_general | solution.py:14
  150.9 3.9 %all-to-all-start.2 = ((bf16[32,16,1024]{2,1,0:T(8,128)(2,1)}), bf16[32,16,1024]{2,1,0:T(8,128)(2,1)S(1)}, u32[]{:S(2)}, u32[]{:S(2)}) async-start(bf16[32,16,1024]{2,1,0:T(8,128)(2,1)} %bitcast.96), calls=%async_computation.2 | async-start | bytes 2097152 | tf_op jit(solution)/shard_map/all_to_all | solution.py:37
  154.9 3.7 %fusion.8 = f32[512,1024]{1,0:T(8,128)S(1)} fusion(bf16[512,1792]{1,0:T(8,128)(2,1)} %all-gather.2.cloned.1.call-done, bf16[1024,896]{0,1:T(8,128)(2,1)} %copy.18, bf16[112,8,8,128]{3,2,1,0:T(8,128)(2,1)} %bitcast.94), kind=kOutput, calls=%fused_computation.22 | convolution fusion | flops 940441600 | bytes 6684672 | tf_op jit(solution)/shard_map/dot_general | solution.py:18
  158.8 2.2 %add_convert_fusion = bf16[512,1024]{1,0:T(8,128)(2,1)} fusion(f32[512,1024]{1,0:T(8,128)S(1)} %fusion.8, bf16[512,1792]{1,0:T(8,128)(2,1)S(1)} %copy-done.14, bf16[1024,896]{0,1:T(8,128)(2,1)S(1)} %copy-done.4, bf16[112,8,8,128]{3,2,1,0:T(8,128)(2,1)S(1)} %bitcast.90), kind=kOutput, calls=%fused_computation.7 | convolution fusion | flops 941490176 | bytes 7733248 | tf_op jit(solution)/shard_map/dot_general | solution.py:18
  161.1 19.1 %all-to-all-done.2 = bf16[32,16,1024]{2,1,0:T(8,128)(2,1)S(1)} async-done(((bf16[32,16,1024]{2,1,0:T(8,128)(2,1)}), bf16[32,16,1024]{2,1,0:T(8,128)(2,1)S(1)}, u32[]{:S(2)}, u32[]{:S(2)}) %all-to-all-start.2) | async-done | bytes 1048608 | tf_op jit(solution)/shard_map/all_to_all | solution.py:37
  180.2 8.0 %all-to-all-start.5 = ((bf16[32,16,1024]{2,1,0:T(8,128)(2,1)}), bf16[32,16,1024]{2,1,0:T(8,128)(2,1)S(1)}, u32[]{:S(2)}, u32[]{:S(2)}) async-start(bf16[32,16,1024]{2,1,0:T(8,128)(2,1)} %bitcast.95), calls=%async_computation.5 | async-start | bytes 2097152 | tf_op jit(solution)/shard_map/all_to_all | solution.py:37
  189.7 2.8 %fusion = bf16[896,1024]{1,0:T(8,128)(2,1)} fusion(f32[112,8,8,128]{3,2,1,0:T(8,128)S(1)} %bitcast.84, bf16[512,896]{1,0:T(8,128)(2,1)S(1)} %copy-done.1, bf16[512,1024]{1,0:T(8,128)(2,1)S(1)} %bitcast.86), kind=kOutput, calls=%fused_computation.1 | convolution fusion | flops 942276608 | bytes 7471104 | tf_op jit(solution)/shard_map/dot_general | solution.py:24
  193.6 1.2 copy-done.15
  194.7 4.0 %fusion.2 = bf16[1024,896]{0,1:T(8,128)(2,1)} fusion(f32[112,8,8,128]{3,2,1,0:T(8,128)S(1)} %bitcast.88, bf16[512,1024]{1,0:T(8,128)(2,1)} %bitcast.1, bf16[512,1792]{1,0:T(8,128)(2,1)S(1)} %copy-done.15), kind=kOutput, calls=%fused_computation.5 | convolution fusion | flops 942276608 | bytes 7471104 | tf_op jit(solution)/shard_map/dot_general | solution.py:24
  198.8 3.8 %copy.26 = bf16[1024,896]{1,0:T(8,128)(2,1)} copy(bf16[1024,896]{0,1:T(8,128)(2,1)} %fusion.2) | data formatting | bytes 3670016
  202.9 1.2 copy-done.16
  204.1 4.0 %fusion.1 = bf16[1024,896]{0,1:T(8,128)(2,1)} fusion(f32[112,8,8,128]{3,2,1,0:T(8,128)S(1)} %bitcast.87, bf16[512,1024]{1,0:T(8,128)(2,1)} %bitcast.1, bf16[512,1792]{1,0:T(8,128)(2,1)S(1)} %copy-done.16), kind=kOutput, calls=%fused_computation.3 | convolution fusion | flops 942276608 | bytes 7471104 | tf_op jit(solution)/shard_map/dot_general | solution.py:24
  208.1 3.8 %copy.27 = bf16[1024,896]{1,0:T(8,128)(2,1)} copy(bf16[1024,896]{0,1:T(8,128)(2,1)} %fusion.1) | data formatting | bytes 3670016
  211.9 1.4 all-to-all-done.5
  (53 shorter events, 8.4 us)
Async XLA Ops:
  7.2 37.6 %copy-start.11 = (bf16[16,1024]{1,0:T(8,128)(2,1)S(1)}, bf16[16,1024]{1,0:T(8,128)(2,1)}, u32[]{:S(2)}) copy-start(bf16[16,1024]{1,0:T(8,128)(2,1)} %param.6) | copy-start | bytes 98308
  44.8 9.6 %copy-start.12 = (s32[3,8,7]{2,1,0:T(8,128)S(1)}, s32[3,8,7]{2,1,0:T(8,128)}, u32[]{:S(2)}) copy-start(s32[3,8,7]{2,1,0:T(8,128)} %param.11) | copy-start | bytes 2020
  44.8 9.7 %copy-start.2 = (bf16[1024,896]{1,0:T(8,128)(2,1)S(1)}, bf16[1024,896]{1,0:T(8,128)(2,1)}, u32[]{:S(2)}) copy-start(bf16[1024,896]{1,0:T(8,128)(2,1)} %param.9) | copy-start | bytes 5505028
  45.9 33.6 %all-to-all-start = ((bf16[32,16,1024]{2,1,0:T(8,128)(2,1)}), bf16[32,16,1024]{2,1,0:T(8,128)(2,1)}, u32[]{:S(2)}, u32[]{:S(2)}) async-start(bf16[32,16,1024]{2,1,0:T(8,128)(2,1)} %broadcast_in_dim.4), calls=%async_computation | async-start | bytes 2097152 | tf_op jit(solution)/shard_map/all_to_all | solution.py:31
  60.7 1.8 copy-start.13
  61.1 1.2 copy-start.8
  79.5 10.5 %copy-start.3 = (bf16[1024,896]{0,1:T(8,128)(2,1)S(1)}, bf16[1024,896]{0,1:T(8,128)(2,1)}, u32[]{:S(2)}) copy-start(bf16[1024,896]{0,1:T(8,128)(2,1)} %copy.20) | copy-start | bytes 5505028
  79.5 22.7 %all-to-all-start.4 = ((bf16[8,64,896]{2,1,0:T(8,128)(2,1)}), bf16[8,64,896]{2,1,0:T(8,128)(2,1)}, u32[]{:S(2)}, u32[]{:S(2)}) async-start(bf16[8,64,896]{2,1,0:T(8,128)(2,1)} %bitcast.97), calls=%async_computation.4 | async-start | bytes 1835008 | tf_op jit(solution)/shard_map/all_to_all | solution.py:37
  88.8 1.2 copy-start.6
  92.4 2.0 copy-start.5
  92.7 4.1 %copy-start.10 = (bf16[8,128,7,128]{1,0,3,2:T(8,128)(2,1)}, bf16[8,128,7,128]{1,0,3,2:T(8,128)(2,1)S(1)}, u32[]{:S(2)}) copy-start(bf16[8,128,7,128]{1,0,3,2:T(8,128)(2,1)S(1)} %mul.106) | copy-start | bytes 5505028
  102.1 27.9 %all-to-all-start.1 = ((bf16[8,64,1792]{2,1,0:T(8,128)(2,1)}), bf16[8,64,1792]{2,1,0:T(8,128)(2,1)S(1)}, u32[]{:S(2)}, u32[]{:S(2)}) async-start(bf16[8,64,1792]{2,1,0:T(8,128)(2,1)} %bitcast.5), calls=%async_computation.1 | async-start | bytes 3670016 | tf_op jit(solution)/shard_map/all_to_all | solution.py:37
  106.6 48.2 %all-gather.2.cloned.1.call-start = ((), (), s32[]{:S(2)}) async-start(), calls=%async_computation.6 | async-start | bytes 2064384 | tf_op jit(solution)/shard_map/all_gather | solution.py:72
  130.3 16.5 %copy-start.9 = (bf16[7,128,8,128]{3,2,1,0:T(8,128)(2,1)S(1)}, bf16[7,128,8,128]{3,2,1,0:T(8,128)(2,1)}, u32[]{:S(2)}) copy-start(bf16[7,128,8,128]{3,2,1,0:T(8,128)(2,1)} %copy-done.8) | copy-start | bytes 5505028
  146.7 4.1 %copy-start = (bf16[512,896]{1,0:T(8,128)(2,1)}, bf16[512,896]{1,0:T(8,128)(2,1)S(1)}, u32[]{:S(2)}) copy-start(bf16[512,896]{1,0:T(8,128)(2,1)S(1)} %all_gather.6) | copy-start | bytes 2752516
  150.9 29.3 %all-to-all-start.2 = ((bf16[32,16,1024]{2,1,0:T(8,128)(2,1)}), bf16[32,16,1024]{2,1,0:T(8,128)(2,1)S(1)}, u32[]{:S(2)}, u32[]{:S(2)}) async-start(bf16[32,16,1024]{2,1,0:T(8,128)(2,1)} %bitcast.96), calls=%async_computation.2 | async-start | bytes 2097152 | tf_op jit(solution)/shard_map/all_to_all | solution.py:37
  154.8 3.8 %copy-start.4 = (bf16[1024,896]{0,1:T(8,128)(2,1)S(1)}, bf16[1024,896]{0,1:T(8,128)(2,1)}, u32[]{:S(2)}) copy-start(bf16[1024,896]{0,1:T(8,128)(2,1)} %copy.20) | copy-start | bytes 5505028
  154.8 3.8 %copy-start.7 = (bf16[8,128,7,128]{1,0,3,2:T(8,128)(2,1)S(1)}, bf16[8,128,7,128]{1,0,3,2:T(8,128)(2,1)}, u32[]{:S(2)}) copy-start(bf16[8,128,7,128]{1,0,3,2:T(8,128)(2,1)} %copy-done.6) | copy-start | bytes 5505028
  154.9 4.0 %copy-start.14 = (bf16[512,1792]{1,0:T(8,128)(2,1)S(1)}, bf16[512,1792]{1,0:T(8,128)(2,1)}, u32[]{:S(2)}) copy-start(bf16[512,1792]{1,0:T(8,128)(2,1)} %all-gather.2.cloned.1.call-done) | copy-start | bytes 5505028
  180.2 33.1 %all-to-all-start.5 = ((bf16[32,16,1024]{2,1,0:T(8,128)(2,1)}), bf16[32,16,1024]{2,1,0:T(8,128)(2,1)S(1)}, u32[]{:S(2)}, u32[]{:S(2)}) async-start(bf16[32,16,1024]{2,1,0:T(8,128)(2,1)} %bitcast.95), calls=%async_computation.5 | async-start | bytes 2097152 | tf_op jit(solution)/shard_map/all_to_all | solution.py:37
  188.5 1.2 copy-start.1
  193.2 1.5 copy-start.15
  202.6 1.5 copy-start.16
Sparse Core Ops, SparseCore 0:
  131.3 22.8 all-gather.1

commit v3 on v1

--- a/solution.py
+++ b/solution.py
@@ -1,7 +1,11 @@
 import jax
 import jax.numpy as jnp
 from jax import lax
+from jax.sharding import Mesh
 from jax.sharding import PartitionSpec as P
+
+COL = ("y", "z")
+ROW = ("x", "core")
 
 
 def masked(weight, mask):
@@ -26,26 +30,45 @@
     )
 
 
-def gather_rows(local, axis, size):
+def gather_rows(local, axis):
+    size = lax.axis_size(axis)
     sent = jnp.broadcast_to(local[None], (size,) + local.shape)
     got = lax.all_to_all(sent, axis, 0, 0, tiled=False)
     return got.reshape((size * local.shape[0],) + local.shape[1:])
 
 
-def reduce_rows(partial, axis, size):
+def reduce_rows(partial, axis):
+    size = lax.axis_size(axis)
     chunks = partial.astype(jnp.bfloat16).reshape((size, partial.shape[0] // size) + partial.shape[1:])
     got = lax.all_to_all(chunks, axis, 0, 0, tiled=False)
     return got.astype(jnp.float32).sum(axis=0)
 
 
+def gather_col(local):
+    return gather_rows(gather_rows(local, "z"), "y")
+
+
+def reduce_col(partial):
+    return reduce_rows(reduce_rows(partial, "y"), "z")
+
+
+def reduce_row(partial):
+    n_x = lax.axis_size("x")
+    n_core = lax.axis_size("core")
+    rows = partial.shape[0] // (n_x * n_core)
+    split = partial.astype(jnp.bfloat16).reshape((n_x, n_core, rows) + partial.shape[1:])
+    split = jnp.swapaxes(split, 0, 1)
+    got = lax.all_to_all(split, "core", 0, 0, tiled=False).astype(jnp.float32).sum(axis=0)
+    got = lax.all_to_all(got.astype(jnp.bfloat16), "x", 0, 0, tiled=False)
+    return got.astype(jnp.float32).sum(axis=0)
+
+
 def shards(tokens, cotangent, gate_weight, up_weight, down_weight, block_mask):
-    n_row = lax.axis_size("row")
-    n_col = lax.axis_size("col")
     masked_gate = masked(gate_weight, block_mask[0])
     masked_up = masked(up_weight, block_mask[1])
     masked_down = masked(down_weight, block_mask[2].T)
     feat = tokens.shape[1]
-    both = gather_rows(jnp.concatenate([tokens, cotangent], axis=1), "col", n_col)
+    both = gather_col(jnp.concatenate([tokens, cotangent], axis=1))
     panel = both[:, :feat]
     grad_panel = both[:, feat:]
     total_rows = panel.shape[0]
@@ -58,7 +81,7 @@
         ],
         axis=1,
     )
-    sums = reduce_rows(partials, "row", n_row)
+    sums = reduce_row(partials)
     gate = sums[:, :width]
     up = sums[:, width : 2 * width]
     dact = sums[:, 2 * width :]
@@ -66,7 +89,7 @@
     act = (gate * sigma * up).astype(jnp.bfloat16)
     dgate = (dact * up * sigma * (1.0 + gate * (1.0 - sigma))).astype(jnp.bfloat16)
     dup = (dact * gate * sigma).astype(jnp.bfloat16)
-    full = lax.all_gather(jnp.concatenate([act, dgate, dup], axis=1), "row", axis=0, tiled=True)
+    full = lax.all_gather(jnp.concatenate([act, dgate, dup], axis=1), ROW, axis=0, tiled=True)
     act_full = full[:, :width]
     dgate_full = full[:, width : 2 * width]
     dup_full = full[:, 2 * width :]
@@ -79,7 +102,7 @@
         ],
         axis=1,
     )
-    outs = reduce_rows(out_partials, "col", n_col).astype(jnp.bfloat16)
+    outs = reduce_col(out_partials).astype(jnp.bfloat16)
     layer_out = outs[:, :feat]
     token_grad = outs[:, feat:]
     scale = total_rows ** (-0.5)
@@ -92,19 +115,21 @@
 
 
 def solution(mesh):
+    n_row, n_col = mesh.devices.shape
+    fine = Mesh(mesh.devices.reshape(n_row // 2, 2, 4, n_col // 4), ("x", "core", "y", "z"))
     in_specs = (
-        P("col", "row"),
-        P("col", "row"),
-        P("row", "col"),
-        P("row", "col"),
-        P("col", "row"),
-        P(None, "row", "col"),
+        P(COL, ROW),
+        P(COL, ROW),
+        P(ROW, COL),
+        P(ROW, COL),
+        P(COL, ROW),
+        P(None, ROW, COL),
     )
     out_specs = (
-        P("col", "row"),
-        P("col", "row"),
-        P("row", "col"),
-        P("row", "col"),
-        P("col", "row"),
+        P(COL, ROW),
+        P(COL, ROW),
+        P(ROW, COL),
+        P(ROW, COL),
+        P(COL, ROW),
     )
-    return jax.shard_map(shards, mesh=mesh, in_specs=in_specs, out_specs=out_specs, check_vma=False)
+    return jax.shard_map(shards, mesh=fine, in_specs=in_specs, out_specs=out_specs, check_vma=False)

time: 223 us -> 203 us (0.910)
  waiting for transfers between devices: 87.7 us -> 55 us
  blocking collectives: 39.6 us -> 56 us
  starting transfers between devices: 22.1 us -> 15.7 us
  other arithmetic: 5.63 us -> 8.45 us
    all_to_all x1, waiting for transfers between devices: 41 us -> 16 us  [gather_rows(): got = lax.all_to_all(sent, axis, 0, 0, tiled=False)]
    all_to_all x1 -> x3, blocking collectives: 39.6 us -> 56 us  [the longest x1 24.9 us: gather_rows(): got = lax.all_to_all(sent, axis, 0, 0, tiled=False)]
    all_to_all x1, starting transfers between devices: 12.2 us -> 4.31 us  [gather_rows(): got = lax.all_to_all(sent, axis, 0, 0, tiled=False)]
    all_to_all x1 -> x2, waiting for transfers between devices: 21.6 us -> 15.6 us  [reduce_rows(): got = lax.all_to_all(chunks, axis, 0, 0, tiled=False)]
    all_to_all x1 -> x2, starting transfers between devices: 9.88 us -> 11.4 us  [reduce_rows(): got = lax.all_to_all(chunks, axis, 0, 0, tiled=False)]
    unnamed x30 -> x36, local copies, waits for them, and re-layouts: 15.6 us -> 15.6 us
  transfers between devices with their start and end apart: 3 -> 4, of which waited for: 3 -> 4; matrix products, arithmetic and copies ran while one was open for 16% -> 17% of each run, Pallas kernels for 0% -> 0%
where the time goes in v3:
time: 203 us
  blocking collectives  56 us (28%)
  waiting for transfers between devices  55 us (27%)
  local copies, waits for them, and re-layouts  30.4 us (15%)
  matrix products  22.7 us (11%)
  starting transfers between devices  15.7 us (8%)
  between operations  14.3 us (7%)
  other arithmetic  8.45 us (4%)
    all_to_all x1, blocking collectives, gather_rows(): got = lax.all_to_all(sent, axis, 0, 0, tiled=False)  24.9 us
    all_gather x1, waiting for transfers between devices, shards(): lax.all_gather(jnp.concatenate([act, dgate, dup], axis=1), ROW, axis=0, t...  23.5 us
    all_to_all x1, blocking collectives, reduce_row(): got = lax.all_to_all(got.astype(jnp.bfloat16), 'x', 0, 0, tiled=False)  22.1 us
    all_to_all x1, waiting for transfers between devices, gather_rows(): got = lax.all_to_all(sent, axis, 0, 0, tiled=False)  16 us
    unnamed x36, local copies, waits for them, and re-layouts  15.6 us
    all_to_all x2, waiting for transfers between devices, reduce_rows(): got = lax.all_to_all(chunks, axis, 0, 0, tiled=False)  15.6 us
    mul x8, local copies, waits for them, and re-layouts, masked(): shaped * mask.astype(weight.dtype)[:, None, :, None]  11.9 us
    all_to_all x2, starting transfers between devices, reduce_rows(): got = lax.all_to_all(chunks, axis, 0, 0, tiled=False)  11.4 us
  transfers between devices with their start and end apart: 4, of which 4 were waited for; matrix products, arithmetic and copies ran while one was open for 17% of the time, Pallas kernels for 0%

profile of v3, /device:TPU:1, one launch (start us, length us, event | category | flops | bytes accessed | tf_op | source)
XLA Modules:
  0.0 202.6 jit_solution(4454215987512897486)
XLA Ops:
  7.2 0.8 pad_maximum_fusion.3
  8.0 24.9 %all_to_all.30 = bf16[8,16,2048]{2,1,0:T(8,128)(2,1)S(1)} all-to-all(bf16[8,16,2048]{2,1,0:T(8,128)(2,1)S(1)} %broadcast_in_dim.6), channel_id=1, replica_groups=mesh['x'=4,'core'=2,'y'=4,'z'=8] {'z'}, dimensions={0} | all-to-all | bytes 1048576 | tf_op jit(solution)/shard_map/all_to_all | solution.py:36
  32.9 1.6 broadcast_in_dim.8
  34.5 4.3 %all-to-all-start.1 = ((bf16[4,128,2048]{2,1,0:T(8,128)(2,1)}), bf16[4,128,2048]{2,1,0:T(8,128)(2,1)S(1)}, u32[]{:S(2)}, u32[]{:S(2)}) async-start(bf16[4,128,2048]{2,1,0:T(8,128)(2,1)} %broadcast_in_dim.8), calls=%async_computation.1 | async-start | bytes 4194304 | tf_op jit(solution)/shard_map/all_to_all | solution.py:36
  39.1 3.8 %copy.35 = bf16[1024,896]{0,1:T(8,128)(2,1)} copy(bf16[1024,896]{1,0:T(8,128)(2,1)} %param.8) | data formatting | bytes 3670016 | tf_op args[2]
  42.9 3.8 %copy.37 = bf16[1024,896]{0,1:T(8,128)(2,1)} copy(bf16[1024,896]{1,0:T(8,128)(2,1)} %param.9) | data formatting | bytes 3670016 | tf_op args[3]
  46.7 16.0 %all-to-all-done.1 = bf16[4,128,2048]{2,1,0:T(8,128)(2,1)S(1)} async-done(((bf16[4,128,2048]{2,1,0:T(8,128)(2,1)}), bf16[4,128,2048]{2,1,0:T(8,128)(2,1)S(1)}, u32[]{:S(2)}, u32[]{:S(2)}) %all-to-all-start.1) | async-done | bytes 2097184 | tf_op jit(solution)/shard_map/all_to_all | solution.py:36
  63.0 3.9 %convolution_convert_fusion.1 = bf16[512,896]{1,0:T(8,128)(2,1)S(1)} fusion(bf16[512,2048]{1,0:T(8,128)(2,1)S(1)} %bitcast.72, bf16[896,1024]{1,0:T(8,128)(2,1)} %param.10, bf16[112,8,8,128]{3,2,1,0:T(8,128)(2,1)S(1)} %bitcast.80), kind=kOutput, calls=%fused_computation.15 | convolution fusion | flops 940900352 | bytes 5636096 | tf_op jit(solution)/shard_map/dot_general | solution.py:22
  67.2 1.3 convolution_convert_fusion.3
  68.9 1.2 copy-done.9
  70.1 1.3 convolution_convert_fusion.2
  71.9 9.1 %all_to_all.31 = bf16[2,4,64,2688]{3,2,1,0:T(8,128)(2,1)S(1)} all-to-all(bf16[2,4,64,2688]{3,2,1,0:T(8,128)(2,1)S(1)} %bitcast.71), channel_id=1, replica_groups=mesh['x'=4,'core'=2,'y'=4,'z'=8] {'core'}, dimensions={0} | all-to-all | bytes 5505024 | tf_op jit(solution)/shard_map/all_to_all | solution.py:61
  80.9 1.9 reduce_sum.45
  82.9 22.1 %all_to_all.32 = bf16[4,64,2688]{2,1,0:T(8,128)(2,1)S(1)} all-to-all(bf16[4,64,2688]{2,1,0:T(8,128)(2,1)} %reduce_sum.45), channel_id=1, replica_groups=mesh['x'=4,'core'=2,'y'=4,'z'=8] {'x'}, dimensions={0} | all-to-all | bytes 2752512 | tf_op jit(solution)/shard_map/all_to_all | solution.py:62
  105.3 0.8 pad_maximum_fusion.2
  106.0 23.5 %all-gather.2.cloned.1.call-done = bf16[512,2688]{1,0:T(8,128)(2,1)} async-done(((bf16[64,2688]{1,0:T(8,128)(2,1)}), bf16[512,2688]{1,0:T(8,128)(2,1)}) %all-gather.2.cloned.1.call-update) | async-done | bytes 2752528 | tf_op jit(solution)/shard_map/all_gather | solution.py:92
  129.5 3.2 %fusion.6 = f32[512,1024]{1,0:T(8,128)S(1)} fusion(bf16[512,2688]{1,0:T(8,128)(2,1)} %all-gather.2.cloned.1.call-done, bf16[1024,896]{0,1:T(8,128)(2,1)S(1)} %copy-done.6, bf16[112,8,8,128]{3,2,1,0:T(8,128)(2,1)} %bitcast.85), kind=kOutput, calls=%fused_computation.23 | convolution fusion | flops 940441600 | bytes 6684672 | tf_op jit(solution)/shard_map/dot_general | solution.py:22
  133.2 1.3 convolution_convert_fusion
  135.3 1.3 add_convert_fusion
  136.6 1.5 pad_maximum_fusion.1
  138.0 4.6 %all-to-all-start.4 = ((bf16[4,128,2048]{2,1,0:T(8,128)(2,1)}), bf16[4,128,2048]{2,1,0:T(8,128)(2,1)}, u32[]{:S(2)}, u32[]{:S(2)}) async-start(bf16[4,128,2048]{2,1,0:T(8,128)(2,1)} %bitcast.8), calls=%async_computation.4 | async-start | bytes 4194304 | tf_op jit(solution)/shard_map/all_to_all | solution.py:43
  143.2 2.7 %copy.64 = f32[112,8,8,128]{3,1,2,0:T(8,128)} copy(f32[112,8,8,128]{3,2,1,0:T(8,128)S(1)} %bitcast.68) | data formatting | bytes 7340032
  145.9 5.0 %copy.43 = f32[1024,896]{1,0:T(8,128)} copy(f32[1024,896]{0,1:T(8,128)} %bitcast.66) | data formatting | bytes 7340032 | tf_op jit(solution)/shard_map/mul | solution.py:14
  151.2 2.8 %copy.65 = f32[112,8,8,128]{3,1,2,0:T(8,128)} copy(f32[112,8,8,128]{3,2,1,0:T(8,128)S(1)} %bitcast.69) | data formatting | bytes 7340032
  154.0 5.0 %copy.41 = f32[1024,896]{1,0:T(8,128)} copy(f32[1024,896]{0,1:T(8,128)} %bitcast.67) | data formatting | bytes 7340032 | tf_op jit(solution)/shard_map/mul | solution.py:14
  159.0 9.6 %all-to-all-done.4 = bf16[4,128,2048]{2,1,0:T(8,128)(2,1)} async-done(((bf16[4,128,2048]{2,1,0:T(8,128)(2,1)}), bf16[4,128,2048]{2,1,0:T(8,128)(2,1)}, u32[]{:S(2)}, u32[]{:S(2)}) %all-to-all-start.4) | async-done | bytes 2097184 | tf_op jit(solution)/shard_map/all_to_all | solution.py:43
  168.7 2.9 %reduce_sum.47 = bf16[128,2048]{1,0:T(8,128)(2,1)} reduce(bf16[4,128,2048]{2,1,0:T(8,128)(2,1)} %all-to-all-done.4, bf16[]{:T(256)} %constant.3.clone.1), dimensions={0}, to_apply=%region_2.0 | reduce | flops 786432 | bytes 2621442 | tf_op jit(solution)/shard_map/reduce_sum | solution.py:44
  171.6 6.7 %all-to-all-start.5 = ((bf16[8,16,2048]{2,1,0:T(8,128)(2,1)}), bf16[8,16,2048]{2,1,0:T(8,128)(2,1)S(1)}, u32[]{:S(2)}, u32[]{:S(2)}) async-start(bf16[8,16,2048]{2,1,0:T(8,128)(2,1)} %bitcast.9), calls=%async_computation.5 | async-start | bytes 1048576 | tf_op jit(solution)/shard_map/all_to_all | solution.py:43
  178.4 5.0 %multiply_convert_fusion = bf16[1024,896]{1,0:T(8,128)(2,1)} fusion(f32[1024,896]{1,0:T(8,128)} %copy.43, bf16[512,2688]{1,0:T(8,128)(2,1)} %all-gather.2.cloned.1.call-done, bf16[512,2048]{1,0:T(8,128)(2,1)S(1)} %bitcast.75), kind=kOutput, calls=%fused_computation.4 | convolution fusion | flops 942276608 | bytes 7471104 | tf_op jit(solution)/shard_map/dot_general | solution.py:28
  183.4 2.6 %multiply_convert_fusion.1 = bf16[1024,896]{1,0:T(8,128)(2,1)} fusion(f32[1024,896]{1,0:T(8,128)S(1)} %copy-done, bf16[512,2688]{1,0:T(8,128)(2,1)S(1)} %copy-done.13, bf16[512,2048]{1,0:T(8,128)(2,1)S(1)} %bitcast.76), kind=kOutput, calls=%fused_computation.5 | convolution fusion | flops 942276608 | bytes 7471104 | tf_op jit(solution)/shard_map/dot_general | solution.py:28
  186.3 2.8 %fusion = bf16[896,1024]{1,0:T(8,128)(2,1)} fusion(f32[112,8,8,128]{3,2,1,0:T(8,128)S(1)} %bitcast.78, bf16[512,2048]{1,0:T(8,128)(2,1)S(1)} %bitcast.77, bf16[512,2688]{1,0:T(8,128)(2,1)S(1)} %copy-done.13), kind=kOutput, calls=%fused_computation.1 | convolution fusion | flops 942276608 | bytes 7471104 | tf_op jit(solution)/shard_map/dot_general | solution.py:28
  189.1 5.9 %all-to-all-done.5 = bf16[8,16,2048]{2,1,0:T(8,128)(2,1)S(1)} async-done(((bf16[8,16,2048]{2,1,0:T(8,128)(2,1)}), bf16[8,16,2048]{2,1,0:T(8,128)(2,1)S(1)}, u32[]{:S(2)}, u32[]{:S(2)}) %all-to-all-start.5) | async-done | bytes 524320 | tf_op jit(solution)/shard_map/all_to_all | solution.py:43
  (53 shorter events, 5.2 us)
Async XLA Ops:
  34.5 4.3 %copy-start.14 = (s32[3,8,7]{2,1,0:T(8,128)S(1)}, s32[3,8,7]{2,1,0:T(8,128)}, u32[]{:S(2)}) copy-start(s32[3,8,7]{2,1,0:T(8,128)} %param.11) | copy-start | bytes 2020
  34.5 28.1 %all-to-all-start.1 = ((bf16[4,128,2048]{2,1,0:T(8,128)(2,1)}), bf16[4,128,2048]{2,1,0:T(8,128)(2,1)S(1)}, u32[]{:S(2)}, u32[]{:S(2)}) async-start(bf16[4,128,2048]{2,1,0:T(8,128)(2,1)} %broadcast_in_dim.8), calls=%async_computation.1 | async-start | bytes 4194304 | tf_op jit(solution)/shard_map/all_to_all | solution.py:36
  38.8 90.7 %all-gather.2.cloned.1.call-start = ((), (), s32[]{:S(2)}) async-start(), calls=%async_computation.6 | async-start | bytes 3096576 | tf_op jit(solution)/shard_map/all_gather | solution.py:92
  62.6 6.3 %copy-start.1 = (bf16[4,128,2048]{2,1,0:T(8,128)(2,1)}, bf16[4,128,2048]{2,1,0:T(8,128)(2,1)S(1)}, u32[]{:S(2)}) copy-start(bf16[4,128,2048]{2,1,0:T(8,128)(2,1)S(1)} %all-to-all-done.1) | copy-start | bytes 6291460
  62.9 3.9 %copy-start.7 = (bf16[7,128,8,128]{3,2,1,0:T(8,128)(2,1)}, bf16[7,128,8,128]{3,2,1,0:T(8,128)(2,1)S(1)}, u32[]{:S(2)}) copy-start(bf16[7,128,8,128]{3,2,1,0:T(8,128)(2,1)S(1)} %mul.108) | copy-start | bytes 5505028
  63.0 4.3 %copy-start.5 = (bf16[1024,896]{0,1:T(8,128)(2,1)S(1)}, bf16[1024,896]{0,1:T(8,128)(2,1)}, u32[]{:S(2)}) copy-start(bf16[1024,896]{0,1:T(8,128)(2,1)} %copy.35) | copy-start | bytes 5505028
  67.2 1.4 copy-start.11
  67.2 2.9 %copy-start.3 = (bf16[1024,896]{0,1:T(8,128)(2,1)S(1)}, bf16[1024,896]{0,1:T(8,128)(2,1)}, u32[]{:S(2)}) copy-start(bf16[1024,896]{0,1:T(8,128)(2,1)} %copy.37) | copy-start | bytes 5505028
  68.9 1.3 copy-start.9
  104.9 24.6 %copy-start.6 = (bf16[1024,896]{0,1:T(8,128)(2,1)S(1)}, bf16[1024,896]{0,1:T(8,128)(2,1)}, u32[]{:S(2)}) copy-start(bf16[1024,896]{0,1:T(8,128)(2,1)} %copy.35) | copy-start | bytes 5505028
  129.5 3.2 %copy-start.8 = (bf16[7,128,8,128]{3,2,1,0:T(8,128)(2,1)S(1)}, bf16[7,128,8,128]{3,2,1,0:T(8,128)(2,1)}, u32[]{:S(2)}) copy-start(bf16[7,128,8,128]{3,2,1,0:T(8,128)(2,1)} %copy-done.7) | copy-start | bytes 5505028
  129.5 3.2 %copy-start.12 = (bf16[512,2688]{1,0:T(8,128)(2,1)S(1)}, bf16[512,2688]{1,0:T(8,128)(2,1)}, u32[]{:S(2)}) copy-start(bf16[512,2688]{1,0:T(8,128)(2,1)} %all-gather.2.cloned.1.call-done) | copy-start | bytes 8257540
  129.5 3.7 %copy-start.15 = (bf16[896,1024]{1,0:T(8,128)(2,1)S(1)}, bf16[896,1024]{1,0:T(8,128)(2,1)}, u32[]{:S(2)}) copy-start(bf16[896,1024]{1,0:T(8,128)(2,1)} %param.10) | copy-start | bytes 5505028
  133.2 1.5 copy-start.4
  133.2 2.0 %copy-start.10 = (bf16[8,128,7,128]{1,0,3,2:T(8,128)(2,1)S(1)}, bf16[8,128,7,128]{1,0,3,2:T(8,128)(2,1)}, u32[]{:S(2)}) copy-start(bf16[8,128,7,128]{1,0,3,2:T(8,128)(2,1)} %copy-done.9) | copy-start | bytes 5505028
  138.0 30.7 %all-to-all-start.4 = ((bf16[4,128,2048]{2,1,0:T(8,128)(2,1)}), bf16[4,128,2048]{2,1,0:T(8,128)(2,1)}, u32[]{:S(2)}, u32[]{:S(2)}) async-start(bf16[4,128,2048]{2,1,0:T(8,128)(2,1)} %bitcast.8), calls=%async_computation.4 | async-start | bytes 4194304 | tf_op jit(solution)/shard_map/all_to_all | solution.py:43
  159.0 19.3 %copy-start.2 = (bf16[4,128,2048]{2,1,0:T(8,128)(2,1)S(1)}, bf16[4,128,2048]{2,1,0:T(8,128)(2,1)}, u32[]{:S(2)}) copy-start(bf16[4,128,2048]{2,1,0:T(8,128)(2,1)} %copy-done.1) | copy-start | bytes 6291460
  171.6 23.4 %all-to-all-start.5 = ((bf16[8,16,2048]{2,1,0:T(8,128)(2,1)}), bf16[8,16,2048]{2,1,0:T(8,128)(2,1)S(1)}, u32[]{:S(2)}, u32[]{:S(2)}) async-start(bf16[8,16,2048]{2,1,0:T(8,128)(2,1)} %bitcast.9), calls=%async_computation.5 | async-start | bytes 1048576 | tf_op jit(solution)/shard_map/all_to_all | solution.py:43
  178.3 5.0 %copy-start = (f32[1024,896]{1,0:T(8,128)S(1)}, f32[1024,896]{1,0:T(8,128)}, u32[]{:S(2)}) copy-start(f32[1024,896]{1,0:T(8,128)} %copy.41) | copy-start | bytes 11010052
  178.4 5.0 %copy-start.13 = (bf16[512,2688]{1,0:T(8,128)(2,1)S(1)}, bf16[512,2688]{1,0:T(8,128)(2,1)}, u32[]{:S(2)}) copy-start(bf16[512,2688]{1,0:T(8,128)(2,1)} %all-gather.2.cloned.1.call-done) | copy-start | bytes 8257540
Sparse Core Ops, SparseCore 0:
  106.2 23.3 all-gather.1

commit v4 on v3

--- a/solution.py
+++ b/solution.py
@@ -89,7 +89,7 @@
     act = (gate * sigma * up).astype(jnp.bfloat16)
     dgate = (dact * up * sigma * (1.0 + gate * (1.0 - sigma))).astype(jnp.bfloat16)
     dup = (dact * gate * sigma).astype(jnp.bfloat16)
-    full = lax.all_gather(jnp.concatenate([act, dgate, dup], axis=1), ROW, axis=0, tiled=True)
+    full = gather_rows(jnp.concatenate([act, dgate, dup], axis=1), ROW)
     act_full = full[:, :width]
     dgate_full = full[:, width : 2 * width]
     dup_full = full[:, 2 * width :]

time: 203 us -> 199 us (0.980)
  blocking collectives: 56 us -> 93.6 us
  waiting for transfers between devices: 55 us -> 30.1 us
  between operations: 14.3 us -> 0.95 us
  starting transfers between devices: 15.7 us -> 12.4 us
    all_to_all x1 -> x2, blocking collectives: 24.9 us -> 62.5 us  [gather_rows(): got = lax.all_to_all(sent, axis, 0, 0, tiled=False)]
    all_gather x1 -> x0, waiting for transfers between devices: 23.5 us -> none  [shards(): lax.all_gather(jnp.concatenate([act, dgate, dup], axis=1), ROW, axis=0, t...]
    all_to_all x2, starting transfers between devices: 11.4 us -> 8.11 us  [reduce_rows(): got = lax.all_to_all(chunks, axis, 0, 0, tiled=False)]
    unnamed x36 -> x38, local copies, waits for them, and re-layouts: 15.6 us -> 16.9 us
  transfers between devices with their start and end apart: 4 -> 3, of which waited for: 4 -> 3; matrix products, arithmetic and copies ran while one was open for 17% -> 18% of each run, Pallas kernels for 0% -> 0%
where the time goes in v4:
time: 199 us; the launch traced here: 198 us
  blocking collectives  93.6 us (47%)
  local copies, waits for them, and re-layouts  31.9 us (16%)
  waiting for transfers between devices  30.1 us (15%)
  matrix products  20.8 us (10%)
  starting transfers between devices  12.4 us (6%)
  other arithmetic  7.72 us (4%)
    all_to_all x2, blocking collectives, gather_rows(): got = lax.all_to_all(sent, axis, 0, 0, tiled=False)  62.5 us
    all_to_all x1, blocking collectives, reduce_row(): got = lax.all_to_all(got.astype(jnp.bfloat16), 'x', 0, 0, tiled=False)  22.1 us
    unnamed x38, local copies, waits for them, and re-layouts  16.9 us
    all_to_all x1, waiting for transfers between devices, gather_rows(): got = lax.all_to_all(sent, axis, 0, 0, tiled=False)  16 us
    all_to_all x2, waiting for transfers between devices, reduce_rows(): got = lax.all_to_all(chunks, axis, 0, 0, tiled=False)  14.2 us
    mul x8, local copies, waits for them, and re-layouts, masked(): shaped * mask.astype(weight.dtype)[:, None, :, None]  11.9 us
    dot_general x3, matrix products, contract_rows(): lax.dot_general(left, right, (((0,), (0,)), ((), ())), preferred_element_...  10.4 us
    all_to_all x1, blocking collectives, reduce_row(): lax.all_to_all(split, 'core', 0, 0, tiled=False).astype(jnp.float32)  9.04 us
  transfers between devices with their start and end apart: 3, of which 3 were waited for; matrix products, arithmetic and copies ran while one was open for 18% of the time, Pallas kernels for 0%

profile of v4, /device:TPU:1, one launch (start us, length us, event | category | flops | bytes accessed | tf_op | source)
XLA Modules:
  0.0 197.5 jit_solution(10004721010991812643)
XLA Ops:
  0.6 0.8 pad_maximum_fusion.3
  1.5 24.9 %all_to_all.35 = bf16[8,16,2048]{2,1,0:T(8,128)(2,1)S(1)} all-to-all(bf16[8,16,2048]{2,1,0:T(8,128)(2,1)S(1)} %broadcast_in_dim.8), channel_id=1, replica_groups=mesh['x'=4,'core'=2,'y'=4,'z'=8] {'z'}, dimensions={0} | all-to-all | bytes 1048576 | tf_op jit(solution)/shard_map/all_to_all | solution.py:36
  26.4 1.6 broadcast_in_dim.10
  28.0 4.3 %all-to-all-start.1 = ((bf16[4,128,2048]{2,1,0:T(8,128)(2,1)}), bf16[4,128,2048]{2,1,0:T(8,128)(2,1)S(1)}, u32[]{:S(2)}, u32[]{:S(2)}) async-start(bf16[4,128,2048]{2,1,0:T(8,128)(2,1)} %broadcast_in_dim.10), calls=%async_computation.1 | async-start | bytes 4194304 | tf_op jit(solution)/shard_map/all_to_all | solution.py:36
  32.6 3.8 %copy.35 = bf16[1024,896]{0,1:T(8,128)(2,1)} copy(bf16[1024,896]{1,0:T(8,128)(2,1)} %param.8) | data formatting | bytes 3670016 | tf_op args[2]
  36.4 3.8 %copy.37 = bf16[1024,896]{0,1:T(8,128)(2,1)} copy(bf16[1024,896]{1,0:T(8,128)(2,1)} %param.9) | data formatting | bytes 3670016 | tf_op args[3]
  40.1 16.0 %all-to-all-done.1 = bf16[4,128,2048]{2,1,0:T(8,128)(2,1)S(1)} async-done(((bf16[4,128,2048]{2,1,0:T(8,128)(2,1)}), bf16[4,128,2048]{2,1,0:T(8,128)(2,1)S(1)}, u32[]{:S(2)}, u32[]{:S(2)}) %all-to-all-start.1) | async-done | bytes 2097184 | tf_op jit(solution)/shard_map/all_to_all | solution.py:36
  56.4 3.9 %convolution_convert_fusion.1 = bf16[512,896]{1,0:T(8,128)(2,1)S(1)} fusion(bf16[512,2048]{1,0:T(8,128)(2,1)S(1)} %bitcast.73, bf16[896,1024]{1,0:T(8,128)(2,1)} %param.10, bf16[112,8,8,128]{3,2,1,0:T(8,128)(2,1)S(1)} %bitcast.87), kind=kOutput, calls=%fused_computation.15 | convolution fusion | flops 940900352 | bytes 5636096 | tf_op jit(solution)/shard_map/dot_general | solution.py:22
  60.7 1.3 convolution_convert_fusion.3
  62.4 1.3 copy-done.11
  63.6 1.3 convolution_convert_fusion.2
  65.4 9.0 %all_to_all.36 = bf16[2,4,64,2688]{3,2,1,0:T(8,128)(2,1)S(1)} all-to-all(bf16[2,4,64,2688]{3,2,1,0:T(8,128)(2,1)S(1)} %bitcast.72), channel_id=1, replica_groups=mesh['x'=4,'core'=2,'y'=4,'z'=8] {'core'}, dimensions={0} | all-to-all | bytes 5505024 | tf_op jit(solution)/shard_map/all_to_all | solution.py:61
  74.4 1.9 reduce_sum.45
  76.4 22.1 %all_to_all.37 = bf16[4,64,2688]{2,1,0:T(8,128)(2,1)S(1)} all-to-all(bf16[4,64,2688]{2,1,0:T(8,128)(2,1)} %reduce_sum.45), channel_id=1, replica_groups=mesh['x'=4,'core'=2,'y'=4,'z'=8] {'x'}, dimensions={0} | all-to-all | bytes 2752512 | tf_op jit(solution)/shard_map/all_to_all | solution.py:62
  99.0 37.6 %all_to_all.38 = bf16[8,64,2688]{2,1,0:T(8,128)(2,1)S(1)} all-to-all(bf16[8,64,2688]{2,1,0:T(8,128)(2,1)S(1)} %broadcast_in_dim.11), channel_id=1, replica_groups=mesh['x'=4,'core'=2,'y'=4,'z'=8] {'x','core'}, dimensions={0} | all-to-all | bytes 5505024 | tf_op jit(solution)/shard_map/all_to_all | solution.py:36
  136.6 1.3 fusion.6
  137.9 1.2 copy-done.10
  139.7 1.3 convolution_convert_fusion
  141.7 1.3 add_convert_fusion
  143.0 1.4 pad_maximum_fusion.1
  144.4 4.6 %all-to-all-start.5 = ((bf16[4,128,2048]{2,1,0:T(8,128)(2,1)}), bf16[4,128,2048]{2,1,0:T(8,128)(2,1)}, u32[]{:S(2)}, u32[]{:S(2)}) async-start(bf16[4,128,2048]{2,1,0:T(8,128)(2,1)} %bitcast.9), calls=%async_computation.5 | async-start | bytes 4194304 | tf_op jit(solution)/shard_map/all_to_all | solution.py:43
  149.6 2.7 %copy.64 = f32[112,8,8,128]{3,1,2,0:T(8,128)} copy(f32[112,8,8,128]{3,2,1,0:T(8,128)S(1)} %bitcast.69) | data formatting | bytes 7340032
  152.3 5.0 %copy.43 = f32[1024,896]{1,0:T(8,128)} copy(f32[1024,896]{0,1:T(8,128)} %bitcast.67) | data formatting | bytes 7340032 | tf_op jit(solution)/shard_map/mul | solution.py:14
  157.7 2.8 %copy.65 = f32[112,8,8,128]{3,1,2,0:T(8,128)} copy(f32[112,8,8,128]{3,2,1,0:T(8,128)S(1)} %bitcast.70) | data formatting | bytes 7340032
  160.4 5.0 %copy.41 = f32[1024,896]{1,0:T(8,128)} copy(f32[1024,896]{0,1:T(8,128)} %bitcast.68) | data formatting | bytes 7340032 | tf_op jit(solution)/shard_map/mul | solution.py:14
  165.5 9.0 %all-to-all-done.5 = bf16[4,128,2048]{2,1,0:T(8,128)(2,1)} async-done(((bf16[4,128,2048]{2,1,0:T(8,128)(2,1)}), bf16[4,128,2048]{2,1,0:T(8,128)(2,1)}, u32[]{:S(2)}, u32[]{:S(2)}) %all-to-all-start.5) | async-done | bytes 2097184 | tf_op jit(solution)/shard_map/all_to_all | solution.py:43
  174.5 2.9 %reduce_sum.47 = bf16[128,2048]{1,0:T(8,128)(2,1)} reduce(bf16[4,128,2048]{2,1,0:T(8,128)(2,1)} %all-to-all-done.5, bf16[]{:T(256)} %constant.3.clone.1), dimensions={0}, to_apply=%region_2.0 | reduce | flops 786432 | bytes 2621442 | tf_op jit(solution)/shard_map/reduce_sum | solution.py:44
  177.4 3.5 %all-to-all-start.6 = ((bf16[8,16,2048]{2,1,0:T(8,128)(2,1)}), bf16[8,16,2048]{2,1,0:T(8,128)(2,1)S(1)}, u32[]{:S(2)}, u32[]{:S(2)}) async-start(bf16[8,16,2048]{2,1,0:T(8,128)(2,1)} %bitcast.10), calls=%async_computation.6 | async-start | bytes 1048576 | tf_op jit(solution)/shard_map/all_to_all | solution.py:43
  180.9 5.0 %multiply_convert_fusion = bf16[1024,896]{1,0:T(8,128)(2,1)} fusion(f32[1024,896]{1,0:T(8,128)} %copy.43, bf16[512,2688]{1,0:T(8,128)(2,1)} %bitcast.82, bf16[512,2048]{1,0:T(8,128)(2,1)S(1)} %bitcast.76), kind=kOutput, calls=%fused_computation.4 | convolution fusion | flops 942276608 | bytes 7471104 | tf_op jit(solution)/shard_map/dot_general | solution.py:28
  185.9 2.6 %multiply_convert_fusion.1 = bf16[1024,896]{1,0:T(8,128)(2,1)} fusion(f32[1024,896]{1,0:T(8,128)S(1)} %copy-done, bf16[512,2688]{1,0:T(8,128)(2,1)S(1)} %bitcast.83, bf16[512,2048]{1,0:T(8,128)(2,1)S(1)} %bitcast.77), kind=kOutput, calls=%fused_computation.5 | convolution fusion | flops 942276608 | bytes 7471104 | tf_op jit(solution)/shard_map/dot_general | solution.py:28
  188.9 2.8 %fusion = bf16[896,1024]{1,0:T(8,128)(2,1)} fusion(f32[112,8,8,128]{3,2,1,0:T(8,128)S(1)} %bitcast.85, bf16[512,2048]{1,0:T(8,128)(2,1)S(1)} %bitcast.78, bf16[512,2688]{1,0:T(8,128)(2,1)S(1)} %bitcast.84), kind=kOutput, calls=%fused_computation.1 | convolution fusion | flops 942276608 | bytes 7471104 | tf_op jit(solution)/shard_map/dot_general | solution.py:28
  191.7 5.2 %all-to-all-done.6 = bf16[8,16,2048]{2,1,0:T(8,128)(2,1)S(1)} async-done(((bf16[8,16,2048]{2,1,0:T(8,128)(2,1)}), bf16[8,16,2048]{2,1,0:T(8,128)(2,1)S(1)}, u32[]{:S(2)}, u32[]{:S(2)}) %all-to-all-start.6) | async-done | bytes 524320 | tf_op jit(solution)/shard_map/all_to_all | solution.py:43
  (54 shorter events, 5.5 us)
Async XLA Ops:
  28.0 4.3 %copy-start.15 = (s32[3,8,7]{2,1,0:T(8,128)S(1)}, s32[3,8,7]{2,1,0:T(8,128)}, u32[]{:S(2)}) copy-start(s32[3,8,7]{2,1,0:T(8,128)} %param.11) | copy-start | bytes 2020
  28.0 28.1 %all-to-all-start.1 = ((bf16[4,128,2048]{2,1,0:T(8,128)(2,1)}), bf16[4,128,2048]{2,1,0:T(8,128)(2,1)S(1)}, u32[]{:S(2)}, u32[]{:S(2)}) async-start(bf16[4,128,2048]{2,1,0:T(8,128)(2,1)} %broadcast_in_dim.10), calls=%async_computation.1 | async-start | bytes 4194304 | tf_op jit(solution)/shard_map/all_to_all | solution.py:36
  56.1 6.3 %copy-start.1 = (bf16[4,128,2048]{2,1,0:T(8,128)(2,1)}, bf16[4,128,2048]{2,1,0:T(8,128)(2,1)S(1)}, u32[]{:S(2)}) copy-start(bf16[4,128,2048]{2,1,0:T(8,128)(2,1)S(1)} %all-to-all-done.1) | copy-start | bytes 6291460
  56.4 3.9 %copy-start.9 = (bf16[7,128,8,128]{3,2,1,0:T(8,128)(2,1)}, bf16[7,128,8,128]{3,2,1,0:T(8,128)(2,1)S(1)}, u32[]{:S(2)}) copy-start(bf16[7,128,8,128]{3,2,1,0:T(8,128)(2,1)S(1)} %mul.108) | copy-start | bytes 5505028
  56.4 4.3 %copy-start.7 = (bf16[1024,896]{0,1:T(8,128)(2,1)S(1)}, bf16[1024,896]{0,1:T(8,128)(2,1)}, u32[]{:S(2)}) copy-start(bf16[1024,896]{0,1:T(8,128)(2,1)} %copy.35) | copy-start | bytes 5505028
  60.7 1.4 copy-start.13
  60.7 2.9 %copy-start.5 = (bf16[1024,896]{0,1:T(8,128)(2,1)S(1)}, bf16[1024,896]{0,1:T(8,128)(2,1)}, u32[]{:S(2)}) copy-start(bf16[1024,896]{0,1:T(8,128)(2,1)} %copy.37) | copy-start | bytes 5505028
  62.4 1.3 copy-start.11
  99.0 37.6 %copy-start.8 = (bf16[1024,896]{0,1:T(8,128)(2,1)S(1)}, bf16[1024,896]{0,1:T(8,128)(2,1)}, u32[]{:S(2)}) copy-start(bf16[1024,896]{0,1:T(8,128)(2,1)} %copy.35) | copy-start | bytes 5505028
  99.0 37.6 %copy-start.14 = (bf16[8,128,7,128]{1,0,3,2:T(8,128)(2,1)S(1)}, bf16[8,128,7,128]{1,0,3,2:T(8,128)(2,1)}, u32[]{:S(2)}) copy-start(bf16[8,128,7,128]{1,0,3,2:T(8,128)(2,1)} %copy-done.13) | copy-start | bytes 5505028
  136.6 4.3 %copy-start.3 = (bf16[8,64,2688]{2,1,0:T(8,128)(2,1)}, bf16[8,64,2688]{2,1,0:T(8,128)(2,1)S(1)}, u32[]{:S(2)}) copy-start(bf16[8,64,2688]{2,1,0:T(8,128)(2,1)S(1)} %all_to_all.38) | copy-start | bytes 8257540
  136.6 2.5 %copy-start.10 = (bf16[7,128,8,128]{3,2,1,0:T(8,128)(2,1)S(1)}, bf16[7,128,8,128]{3,2,1,0:T(8,128)(2,1)}, u32[]{:S(2)}) copy-start(bf16[7,128,8,128]{3,2,1,0:T(8,128)(2,1)} %copy-done.9) | copy-start | bytes 5505028
  136.6 3.0 %copy-start.16 = (bf16[896,1024]{1,0:T(8,128)(2,1)S(1)}, bf16[896,1024]{1,0:T(8,128)(2,1)}, u32[]{:S(2)}) copy-start(bf16[896,1024]{1,0:T(8,128)(2,1)} %param.10) | copy-start | bytes 5505028
  139.7 1.5 copy-start.6
  139.7 2.0 %copy-start.12 = (bf16[8,128,7,128]{1,0,3,2:T(8,128)(2,1)S(1)}, bf16[8,128,7,128]{1,0,3,2:T(8,128)(2,1)}, u32[]{:S(2)}) copy-start(bf16[8,128,7,128]{1,0,3,2:T(8,128)(2,1)} %copy-done.11) | copy-start | bytes 5505028
  144.4 30.1 %all-to-all-start.5 = ((bf16[4,128,2048]{2,1,0:T(8,128)(2,1)}), bf16[4,128,2048]{2,1,0:T(8,128)(2,1)}, u32[]{:S(2)}, u32[]{:S(2)}) async-start(bf16[4,128,2048]{2,1,0:T(8,128)(2,1)} %bitcast.9), calls=%async_computation.5 | async-start | bytes 4194304 | tf_op jit(solution)/shard_map/all_to_all | solution.py:43
  165.5 15.4 %copy-start.2 = (bf16[4,128,2048]{2,1,0:T(8,128)(2,1)S(1)}, bf16[4,128,2048]{2,1,0:T(8,128)(2,1)}, u32[]{:S(2)}) copy-start(bf16[4,128,2048]{2,1,0:T(8,128)(2,1)} %copy-done.1) | copy-start | bytes 6291460
  177.4 19.4 %all-to-all-start.6 = ((bf16[8,16,2048]{2,1,0:T(8,128)(2,1)}), bf16[8,16,2048]{2,1,0:T(8,128)(2,1)S(1)}, u32[]{:S(2)}, u32[]{:S(2)}) async-start(bf16[8,16,2048]{2,1,0:T(8,128)(2,1)} %bitcast.10), calls=%async_computation.6 | async-start | bytes 1048576 | tf_op jit(solution)/shard_map/all_to_all | solution.py:43
  180.9 5.0 %copy-start = (f32[1024,896]{1,0:T(8,128)S(1)}, f32[1024,896]{1,0:T(8,128)}, u32[]{:S(2)}) copy-start(f32[1024,896]{1,0:T(8,128)} %copy.41) | copy-start | bytes 11010052
  180.9 5.0 %copy-start.4 = (bf16[8,64,2688]{2,1,0:T(8,128)(2,1)S(1)}, bf16[8,64,2688]{2,1,0:T(8,128)(2,1)}, u32[]{:S(2)}) copy-start(bf16[8,64,2688]{2,1,0:T(8,128)(2,1)} %copy-done.3) | copy-start | bytes 8257540

commit v5 on v4

--- a/solution.py
+++ b/solution.py
@@ -63,6 +63,15 @@
     return got.astype(jnp.float32).sum(axis=0)
 
 
+def gather_row(local):
+    n_x = lax.axis_size("x")
+    n_core = lax.axis_size("core")
+    over_x = gather_rows(local, "x").reshape((n_x,) + local.shape)
+    sent = jnp.broadcast_to(over_x[None], (n_core,) + over_x.shape)
+    both = lax.all_to_all(sent, "core", 0, 0, tiled=False)
+    return jnp.swapaxes(both, 0, 1).reshape((n_x * n_core * local.shape[0],) + local.shape[1:])
+
+
 def shards(tokens, cotangent, gate_weight, up_weight, down_weight, block_mask):
     masked_gate = masked(gate_weight, block_mask[0])
     masked_up = masked(up_weight, block_mask[1])
@@ -89,7 +98,7 @@
     act = (gate * sigma * up).astype(jnp.bfloat16)
     dgate = (dact * up * sigma * (1.0 + gate * (1.0 - sigma))).astype(jnp.bfloat16)
     dup = (dact * gate * sigma).astype(jnp.bfloat16)
-    full = gather_rows(jnp.concatenate([act, dgate, dup], axis=1), ROW)
+    full = gather_row(jnp.concatenate([act, dgate, dup], axis=1))
     act_full = full[:, :width]
     dgate_full = full[:, width : 2 * width]
     dup_full = full[:, 2 * width :]

time: 199 us -> 192 us (0.965)
  blocking collectives: 93.6 us -> 83.6 us
  local copies, waits for them, and re-layouts: 31.9 us -> 34.1 us
    all_to_all x2, blocking collectives: 62.5 us -> 44.5 us  [gather_rows(): got = lax.all_to_all(sent, axis, 0, 0, tiled=False)]
    all_to_all x0 -> x1, blocking collectives: none -> 7.94 us  [gather_row(): both = lax.all_to_all(sent, 'core', 0, 0, tiled=False)]
where the time goes in v5:
time: 192 us; the launch traced here: 191 us
  blocking collectives  83.6 us (44%)
  local copies, waits for them, and re-layouts  34.1 us (18%)
  waiting for transfers between devices  31.7 us (17%)
  matrix products  20.8 us (11%)
  starting transfers between devices  12.4 us (6%)
  other arithmetic  7.75 us (4%)
    all_to_all x2, blocking collectives, gather_rows(): got = lax.all_to_all(sent, axis, 0, 0, tiled=False)  44.5 us
    all_to_all x1, blocking collectives, reduce_row(): got = lax.all_to_all(got.astype(jnp.bfloat16), 'x', 0, 0, tiled=False)  22.1 us
    unnamed x38, local copies, waits for them, and re-layouts  18.7 us
    all_to_all x1, waiting for transfers between devices, gather_rows(): got = lax.all_to_all(sent, axis, 0, 0, tiled=False)  16 us
    all_to_all x2, waiting for transfers between devices, reduce_rows(): got = lax.all_to_all(chunks, axis, 0, 0, tiled=False)  15.7 us
    mul x8, local copies, waits for them, and re-layouts, masked(): shaped * mask.astype(weight.dtype)[:, None, :, None]  11.9 us
    dot_general x3, matrix products, contract_rows(): lax.dot_general(left, right, (((0,), (0,)), ((), ())), preferred_element_...  10.4 us
    all_to_all x1, blocking collectives, reduce_row(): lax.all_to_all(split, 'core', 0, 0, tiled=False).astype(jnp.float32)  9.05 us
  transfers between devices with their start and end apart: 3, of which 3 were waited for; matrix products, arithmetic and copies ran while one was open for 18% of the time, Pallas kernels for 0%

profile of v5, /device:TPU:1, one launch (start us, length us, event | category | flops | bytes accessed | tf_op | source)
XLA Modules:
  0.0 191.2 jit_solution(14016749533795899361)
XLA Ops:
  1.5 24.9 %all_to_all.40 = bf16[8,16,2048]{2,1,0:T(8,128)(2,1)S(1)} all-to-all(bf16[8,16,2048]{2,1,0:T(8,128)(2,1)S(1)} %broadcast_in_dim.10), channel_id=1, replica_groups=mesh['x'=4,'core'=2,'y'=4,'z'=8] {'z'}, dimensions={0} | all-to-all | bytes 1048576 | tf_op jit(solution)/shard_map/all_to_all | solution.py:36
  26.4 1.6 broadcast_in_dim.12
  28.0 4.3 %all-to-all-start.1 = ((bf16[4,128,2048]{2,1,0:T(8,128)(2,1)}), bf16[4,128,2048]{2,1,0:T(8,128)(2,1)S(1)}, u32[]{:S(2)}, u32[]{:S(2)}) async-start(bf16[4,128,2048]{2,1,0:T(8,128)(2,1)} %broadcast_in_dim.12), calls=%async_computation.1 | async-start | bytes 4194304 | tf_op jit(solution)/shard_map/all_to_all | solution.py:36
  32.6 3.8 %copy.36 = bf16[1024,896]{0,1:T(8,128)(2,1)} copy(bf16[1024,896]{1,0:T(8,128)(2,1)} %param.8) | data formatting | bytes 3670016 | tf_op args[2]
  36.4 3.8 %copy.38 = bf16[1024,896]{0,1:T(8,128)(2,1)} copy(bf16[1024,896]{1,0:T(8,128)(2,1)} %param.9) | data formatting | bytes 3670016 | tf_op args[3]
  40.1 16.0 %all-to-all-done.1 = bf16[4,128,2048]{2,1,0:T(8,128)(2,1)S(1)} async-done(((bf16[4,128,2048]{2,1,0:T(8,128)(2,1)}), bf16[4,128,2048]{2,1,0:T(8,128)(2,1)S(1)}, u32[]{:S(2)}, u32[]{:S(2)}) %all-to-all-start.1) | async-done | bytes 2097184 | tf_op jit(solution)/shard_map/all_to_all | solution.py:36
  56.4 3.9 %convolution_convert_fusion.1 = bf16[512,896]{1,0:T(8,128)(2,1)S(1)} fusion(bf16[512,2048]{1,0:T(8,128)(2,1)S(1)} %bitcast.75, bf16[896,1024]{1,0:T(8,128)(2,1)} %param.10, bf16[112,8,8,128]{3,2,1,0:T(8,128)(2,1)S(1)} %bitcast.89), kind=kOutput, calls=%fused_computation.15 | convolution fusion | flops 940900352 | bytes 5636096 | tf_op jit(solution)/shard_map/dot_general | solution.py:22
  60.7 1.3 convolution_convert_fusion.3
  62.4 1.3 copy-done.11
  63.6 1.3 convolution_convert_fusion.2
  65.4 9.0 %all_to_all.41 = bf16[2,4,64,2688]{3,2,1,0:T(8,128)(2,1)S(1)} all-to-all(bf16[2,4,64,2688]{3,2,1,0:T(8,128)(2,1)S(1)} %bitcast.74), channel_id=1, replica_groups=mesh['x'=4,'core'=2,'y'=4,'z'=8] {'core'}, dimensions={0} | all-to-all | bytes 5505024 | tf_op jit(solution)/shard_map/all_to_all | solution.py:61
  74.4 1.9 %reduce_sum.45 = bf16[4,64,2688]{2,1,0:T(8,128)(2,1)} reduce(bf16[2,4,64,2688]{3,2,1,0:T(8,128)(2,1)S(1)} %all_to_all.41, bf16[]{:T(256)} %constant.3.clone.1), dimensions={0}, to_apply=%region_0.0 | reduce | flops 688128 | bytes 4128770 | tf_op jit(solution)/shard_map/reduce_sum | solution.py:61
  76.4 22.1 %all_to_all.42 = bf16[4,64,2688]{2,1,0:T(8,128)(2,1)S(1)} all-to-all(bf16[4,64,2688]{2,1,0:T(8,128)(2,1)} %reduce_sum.45), channel_id=1, replica_groups=mesh['x'=4,'core'=2,'y'=4,'z'=8] {'x'}, dimensions={0} | all-to-all | bytes 2752512 | tf_op jit(solution)/shard_map/all_to_all | solution.py:62
  98.9 19.6 %all_to_all.43 = bf16[4,64,2688]{2,1,0:T(8,128)(2,1)S(1)} all-to-all(bf16[4,64,2688]{2,1,0:T(8,128)(2,1)S(1)} %broadcast_in_dim.13), channel_id=1, replica_groups=mesh['x'=4,'core'=2,'y'=4,'z'=8] {'x'}, dimensions={0} | all-to-all | bytes 2752512 | tf_op jit(solution)/shard_map/all_to_all | solution.py:36
  118.7 7.9 %all_to_all.44 = bf16[2,4,64,2688]{3,2,1,0:T(8,128)(2,1)S(1)} all-to-all(bf16[2,4,64,2688]{3,2,1,0:T(8,128)(2,1)S(1)} %broadcast_in_dim.14), channel_id=1, replica_groups=mesh['x'=4,'core'=2,'y'=4,'z'=8] {'core'}, dimensions={0} | all-to-all | bytes 5505024 | tf_op jit(solution)/shard_map/all_to_all | solution.py:71
  126.9 2.1 %copy-done.8 = bf16[1024,896]{0,1:T(8,128)(2,1)S(1)} copy-done((bf16[1024,896]{0,1:T(8,128)(2,1)S(1)}, bf16[1024,896]{0,1:T(8,128)(2,1)}, u32[]{:S(2)}) %copy-start.8) | copy-done | bytes 1835032
  129.7 1.3 fusion.6
  131.8 1.3 convolution_convert_fusion
  133.8 1.3 add_convert_fusion
  135.1 1.5 pad_maximum_fusion.1
  136.6 4.6 %all-to-all-start.6 = ((bf16[4,128,2048]{2,1,0:T(8,128)(2,1)}), bf16[4,128,2048]{2,1,0:T(8,128)(2,1)}, u32[]{:S(2)}, u32[]{:S(2)}) async-start(bf16[4,128,2048]{2,1,0:T(8,128)(2,1)} %bitcast.11), calls=%async_computation.6 | async-start | bytes 4194304 | tf_op jit(solution)/shard_map/all_to_all | solution.py:43
  141.8 2.7 %copy.66 = f32[112,8,8,128]{3,1,2,0:T(8,128)} copy(f32[112,8,8,128]{3,2,1,0:T(8,128)S(1)} %bitcast.71) | data formatting | bytes 7340032
  144.5 5.0 %copy.45 = f32[1024,896]{1,0:T(8,128)} copy(f32[1024,896]{0,1:T(8,128)} %bitcast.69) | data formatting | bytes 7340032 | tf_op jit(solution)/shard_map/mul | solution.py:14
  149.8 2.8 %copy.67 = f32[112,8,8,128]{3,1,2,0:T(8,128)} copy(f32[112,8,8,128]{3,2,1,0:T(8,128)S(1)} %bitcast.72) | data formatting | bytes 7340032
  152.6 5.0 %copy.43 = f32[1024,896]{1,0:T(8,128)} copy(f32[1024,896]{0,1:T(8,128)} %bitcast.70) | data formatting | bytes 7340032 | tf_op jit(solution)/shard_map/mul | solution.py:14
  157.6 9.5 %all-to-all-done.6 = bf16[4,128,2048]{2,1,0:T(8,128)(2,1)} async-done(((bf16[4,128,2048]{2,1,0:T(8,128)(2,1)}), bf16[4,128,2048]{2,1,0:T(8,128)(2,1)}, u32[]{:S(2)}, u32[]{:S(2)}) %all-to-all-start.6) | async-done | bytes 2097184 | tf_op jit(solution)/shard_map/all_to_all | solution.py:43
  167.1 2.9 %reduce_sum.47 = bf16[128,2048]{1,0:T(8,128)(2,1)} reduce(bf16[4,128,2048]{2,1,0:T(8,128)(2,1)} %all-to-all-done.6, bf16[]{:T(256)} %constant.3.clone.1), dimensions={0}, to_apply=%region_2.0 | reduce | flops 786432 | bytes 2621442 | tf_op jit(solution)/shard_map/reduce_sum | solution.py:44
  170.1 3.5 %all-to-all-start.7 = ((bf16[8,16,2048]{2,1,0:T(8,128)(2,1)}), bf16[8,16,2048]{2,1,0:T(8,128)(2,1)S(1)}, u32[]{:S(2)}, u32[]{:S(2)}) async-start(bf16[8,16,2048]{2,1,0:T(8,128)(2,1)} %bitcast.12), calls=%async_computation.7 | async-start | bytes 1048576 | tf_op jit(solution)/shard_map/all_to_all | solution.py:43
  173.6 5.0 %multiply_convert_fusion = bf16[1024,896]{1,0:T(8,128)(2,1)} fusion(f32[1024,896]{1,0:T(8,128)} %copy.45, bf16[512,2688]{1,0:T(8,128)(2,1)} %bitcast.84, bf16[512,2048]{1,0:T(8,128)(2,1)S(1)} %bitcast.78), kind=kOutput, calls=%fused_computation.4 | convolution fusion | flops 942276608 | bytes 7471104 | tf_op jit(solution)/shard_map/dot_general | solution.py:28
  178.6 2.6 %multiply_convert_fusion.1 = bf16[1024,896]{1,0:T(8,128)(2,1)} fusion(f32[1024,896]{1,0:T(8,128)S(1)} %copy-done, bf16[512,2688]{1,0:T(8,128)(2,1)S(1)} %bitcast.85, bf16[512,2048]{1,0:T(8,128)(2,1)S(1)} %bitcast.79), kind=kOutput, calls=%fused_computation.5 | convolution fusion | flops 942276608 | bytes 7471104 | tf_op jit(solution)/shard_map/dot_general | solution.py:28
  181.5 2.8 %fusion = bf16[896,1024]{1,0:T(8,128)(2,1)} fusion(f32[112,8,8,128]{3,2,1,0:T(8,128)S(1)} %bitcast.87, bf16[512,2048]{1,0:T(8,128)(2,1)S(1)} %bitcast.80, bf16[512,2688]{1,0:T(8,128)(2,1)S(1)} %bitcast.86), kind=kOutput, calls=%fused_computation.1 | convolution fusion | flops 942276608 | bytes 7471104 | tf_op jit(solution)/shard_map/dot_general | solution.py:28
  184.3 6.2 %all-to-all-done.7 = bf16[8,16,2048]{2,1,0:T(8,128)(2,1)S(1)} async-done(((bf16[8,16,2048]{2,1,0:T(8,128)(2,1)}), bf16[8,16,2048]{2,1,0:T(8,128)(2,1)S(1)}, u32[]{:S(2)}, u32[]{:S(2)}) %all-to-all-start.7) | async-done | bytes 524320 | tf_op jit(solution)/shard_map/all_to_all | solution.py:43
  (57 shorter events, 7.5 us)
Async XLA Ops:
  28.0 4.3 %copy-start.15 = (s32[3,8,7]{2,1,0:T(8,128)S(1)}, s32[3,8,7]{2,1,0:T(8,128)}, u32[]{:S(2)}) copy-start(s32[3,8,7]{2,1,0:T(8,128)} %param.11) | copy-start | bytes 2020
  28.0 28.1 %all-to-all-start.1 = ((bf16[4,128,2048]{2,1,0:T(8,128)(2,1)}), bf16[4,128,2048]{2,1,0:T(8,128)(2,1)S(1)}, u32[]{:S(2)}, u32[]{:S(2)}) async-start(bf16[4,128,2048]{2,1,0:T(8,128)(2,1)} %broadcast_in_dim.12), calls=%async_computation.1 | async-start | bytes 4194304 | tf_op jit(solution)/shard_map/all_to_all | solution.py:36
  56.1 6.3 %copy-start.1 = (bf16[4,128,2048]{2,1,0:T(8,128)(2,1)}, bf16[4,128,2048]{2,1,0:T(8,128)(2,1)S(1)}, u32[]{:S(2)}) copy-start(bf16[4,128,2048]{2,1,0:T(8,128)(2,1)S(1)} %all-to-all-done.1) | copy-start | bytes 6291460
  56.4 3.9 %copy-start.9 = (bf16[7,128,8,128]{3,2,1,0:T(8,128)(2,1)}, bf16[7,128,8,128]{3,2,1,0:T(8,128)(2,1)S(1)}, u32[]{:S(2)}) copy-start(bf16[7,128,8,128]{3,2,1,0:T(8,128)(2,1)S(1)} %mul.108) | copy-start | bytes 5505028
  56.4 4.3 %copy-start.7 = (bf16[1024,896]{0,1:T(8,128)(2,1)S(1)}, bf16[1024,896]{0,1:T(8,128)(2,1)}, u32[]{:S(2)}) copy-start(bf16[1024,896]{0,1:T(8,128)(2,1)} %copy.36) | copy-start | bytes 5505028
  60.7 1.4 copy-start.13
  60.7 2.9 %copy-start.5 = (bf16[1024,896]{0,1:T(8,128)(2,1)S(1)}, bf16[1024,896]{0,1:T(8,128)(2,1)}, u32[]{:S(2)}) copy-start(bf16[1024,896]{0,1:T(8,128)(2,1)} %copy.38) | copy-start | bytes 5505028
  62.4 1.3 copy-start.11
  126.7 2.3 %copy-start.8 = (bf16[1024,896]{0,1:T(8,128)(2,1)S(1)}, bf16[1024,896]{0,1:T(8,128)(2,1)}, u32[]{:S(2)}) copy-start(bf16[1024,896]{0,1:T(8,128)(2,1)} %copy.36) | copy-start | bytes 5505028
  126.7 3.0 %copy-start.14 = (bf16[8,128,7,128]{1,0,3,2:T(8,128)(2,1)S(1)}, bf16[8,128,7,128]{1,0,3,2:T(8,128)(2,1)}, u32[]{:S(2)}) copy-start(bf16[8,128,7,128]{1,0,3,2:T(8,128)(2,1)} %copy-done.13) | copy-start | bytes 5505028
  126.9 6.2 %copy-start.3 = (bf16[2,4,64,2688]{3,2,0,1:T(8,128)(2,1)}, bf16[2,4,64,2688]{3,2,0,1:T(8,128)(2,1)S(1)}, u32[]{:S(2)}) copy-start(bf16[2,4,64,2688]{3,2,0,1:T(8,128)(2,1)S(1)} %copy.41) | copy-start | bytes 8257540
  129.7 1.5 copy-start.10
  129.7 2.0 %copy-start.16 = (bf16[896,1024]{1,0:T(8,128)(2,1)S(1)}, bf16[896,1024]{1,0:T(8,128)(2,1)}, u32[]{:S(2)}) copy-start(bf16[896,1024]{1,0:T(8,128)(2,1)} %param.10) | copy-start | bytes 5505028
  131.8 1.5 copy-start.6
  131.8 2.0 %copy-start.12 = (bf16[8,128,7,128]{1,0,3,2:T(8,128)(2,1)S(1)}, bf16[8,128,7,128]{1,0,3,2:T(8,128)(2,1)}, u32[]{:S(2)}) copy-start(bf16[8,128,7,128]{1,0,3,2:T(8,128)(2,1)} %copy-done.11) | copy-start | bytes 5505028
  136.6 30.6 %all-to-all-start.6 = ((bf16[4,128,2048]{2,1,0:T(8,128)(2,1)}), bf16[4,128,2048]{2,1,0:T(8,128)(2,1)}, u32[]{:S(2)}, u32[]{:S(2)}) async-start(bf16[4,128,2048]{2,1,0:T(8,128)(2,1)} %bitcast.11), calls=%async_computation.6 | async-start | bytes 4194304 | tf_op jit(solution)/shard_map/all_to_all | solution.py:43
  157.6 15.9 %copy-start.2 = (bf16[4,128,2048]{2,1,0:T(8,128)(2,1)S(1)}, bf16[4,128,2048]{2,1,0:T(8,128)(2,1)}, u32[]{:S(2)}) copy-start(bf16[4,128,2048]{2,1,0:T(8,128)(2,1)} %copy-done.1) | copy-start | bytes 6291460
  170.1 20.5 %all-to-all-start.7 = ((bf16[8,16,2048]{2,1,0:T(8,128)(2,1)}), bf16[8,16,2048]{2,1,0:T(8,128)(2,1)S(1)}, u32[]{:S(2)}, u32[]{:S(2)}) async-start(bf16[8,16,2048]{2,1,0:T(8,128)(2,1)} %bitcast.12), calls=%async_computation.7 | async-start | bytes 1048576 | tf_op jit(solution)/shard_map/all_to_all | solution.py:43
  173.6 5.0 %copy-start = (f32[1024,896]{1,0:T(8,128)S(1)}, f32[1024,896]{1,0:T(8,128)}, u32[]{:S(2)}) copy-start(f32[1024,896]{1,0:T(8,128)} %copy.43) | copy-start | bytes 11010052
  173.6 5.0 %copy-start.4 = (bf16[2,4,64,2688]{3,2,0,1:T(8,128)(2,1)S(1)}, bf16[2,4,64,2688]{3,2,0,1:T(8,128)(2,1)}, u32[]{:S(2)}) copy-start(bf16[2,4,64,2688]{3,2,0,1:T(8,128)(2,1)} %copy-done.3) | copy-start | bytes 8257540

commit v6 on v5

--- a/solution.py
+++ b/solution.py
@@ -30,6 +30,13 @@
     )
 
 
+def add_blocks(got):
+    total = got[0].astype(jnp.float32)
+    for i in range(1, got.shape[0]):
+        total = total + got[i].astype(jnp.float32)
+    return total
+
+
 def gather_rows(local, axis):
     size = lax.axis_size(axis)
     sent = jnp.broadcast_to(local[None], (size,) + local.shape)
@@ -41,7 +48,7 @@
     size = lax.axis_size(axis)
     chunks = partial.astype(jnp.bfloat16).reshape((size, partial.shape[0] // size) + partial.shape[1:])
     got = lax.all_to_all(chunks, axis, 0, 0, tiled=False)
-    return got.astype(jnp.float32).sum(axis=0)
+    return add_blocks(got)
 
 
 def gather_col(local):
@@ -58,9 +65,8 @@
     rows = partial.shape[0] // (n_x * n_core)
     split = partial.astype(jnp.bfloat16).reshape((n_x, n_core, rows) + partial.shape[1:])
     split = jnp.swapaxes(split, 0, 1)
-    got = lax.all_to_all(split, "core", 0, 0, tiled=False).astype(jnp.float32).sum(axis=0)
-    got = lax.all_to_all(got.astype(jnp.bfloat16), "x", 0, 0, tiled=False)
-    return got.astype(jnp.float32).sum(axis=0)
+    got = add_blocks(lax.all_to_all(split, "core", 0, 0, tiled=False))
+    return add_blocks(lax.all_to_all(got.astype(jnp.bfloat16), "x", 0, 0, tiled=False))
 
 
 def gather_row(local):

time: 192 us -> 185 us (0.964)
  local copies, waits for them, and re-layouts: 34.1 us -> 29.6 us
    reduce_sum x4 -> x0, other arithmetic: 5.13 us -> none  [the longest x2 3 us: reduce_rows(): return got.astype(jnp.float32).sum(axis=0)]
    unnamed x38 -> x18, local copies, waits for them, and re-layouts: 18.7 us -> 14.2 us
    another operation x0 -> x1, other arithmetic: none -> 2.65 us
  transfers between devices with their start and end apart: 3 -> 3, of which waited for: 3 -> 3; matrix products, arithmetic and copies ran while one was open for 18% -> 19% of each run, Pallas kernels for 0% -> 0%
where the time goes in v6:
time: 185 us; the launch traced here: 184 us
  blocking collectives  83.4 us (45%)
  waiting for transfers between devices  31.7 us (17%)
  local copies, waits for them, and re-layouts  29.6 us (16%)
  matrix products  20 us (11%)
  starting transfers between devices  12.4 us (7%)
  other arithmetic  5.86 us (3%)
    all_to_all x2, blocking collectives, gather_rows(): got = lax.all_to_all(sent, axis, 0, 0, tiled=False)  44.5 us
    all_to_all x1, blocking collectives, reduce_row(): lax.all_to_all(got.astype(jnp.bfloat16), 'x', 0, 0, tiled=False)  21.9 us
    all_to_all x1, waiting for transfers between devices, gather_rows(): got = lax.all_to_all(sent, axis, 0, 0, tiled=False)  16 us
    all_to_all x2, waiting for transfers between devices, reduce_rows(): got = lax.all_to_all(chunks, axis, 0, 0, tiled=False)  15.7 us
    unnamed x18, local copies, waits for them, and re-layouts  14.2 us
    mul x8, local copies, waits for them, and re-layouts, masked(): shaped * mask.astype(weight.dtype)[:, None, :, None]  11.9 us
    dot_general x3, matrix products, contract_rows(): lax.dot_general(left, right, (((0,), (0,)), ((), ())), preferred_element_...  10.4 us
    all_to_all x1, blocking collectives, reduce_row(): got = add_blocks(lax.all_to_all(split, 'core', 0, 0, tiled=False))  9.04 us
  transfers between devices with their start and end apart: 3, of which 3 were waited for; matrix products, arithmetic and copies ran while one was open for 19% of the time, Pallas kernels for 0%

profile of v6, /device:TPU:1, one launch (start us, length us, event | category | flops | bytes accessed | tf_op | source)
XLA Modules:
  0.0 183.8 jit_solution(1030177190751116023)
XLA Ops:
  0.6 0.8 pad_maximum_fusion.3
  1.5 24.9 %all_to_all.40 = bf16[8,16,2048]{2,1,0:T(8,128)(2,1)S(1)} all-to-all(bf16[8,16,2048]{2,1,0:T(8,128)(2,1)S(1)} %broadcast_in_dim.10), channel_id=1, replica_groups=mesh['x'=4,'core'=2,'y'=4,'z'=8] {'z'}, dimensions={0} | all-to-all | bytes 1048576 | tf_op jit(solution)/shard_map/all_to_all | solution.py:43
  26.4 1.6 broadcast_in_dim.12
  28.0 4.3 %all-to-all-start.1 = ((bf16[4,128,2048]{2,1,0:T(8,128)(2,1)}), bf16[4,128,2048]{2,1,0:T(8,128)(2,1)S(1)}, u32[]{:S(2)}, u32[]{:S(2)}) async-start(bf16[4,128,2048]{2,1,0:T(8,128)(2,1)} %broadcast_in_dim.12), calls=%async_computation.1 | async-start | bytes 4194304 | tf_op jit(solution)/shard_map/all_to_all | solution.py:43
  32.6 3.8 %copy.24 = bf16[1024,896]{0,1:T(8,128)(2,1)} copy(bf16[1024,896]{1,0:T(8,128)(2,1)} %param.8) | data formatting | bytes 3670016 | tf_op args[2]
  36.4 3.8 %copy.26 = bf16[1024,896]{0,1:T(8,128)(2,1)} copy(bf16[1024,896]{1,0:T(8,128)(2,1)} %param.9) | data formatting | bytes 3670016 | tf_op args[3]
  40.1 16.0 %all-to-all-done.1 = bf16[4,128,2048]{2,1,0:T(8,128)(2,1)S(1)} async-done(((bf16[4,128,2048]{2,1,0:T(8,128)(2,1)}), bf16[4,128,2048]{2,1,0:T(8,128)(2,1)S(1)}, u32[]{:S(2)}, u32[]{:S(2)}) %all-to-all-start.1) | async-done | bytes 2097184 | tf_op jit(solution)/shard_map/all_to_all | solution.py:43
  56.4 2.9 %convolution_convert_fusion.1 = bf16[512,896]{1,0:T(8,128)(2,1)S(1)} fusion(bf16[512,2048]{1,0:T(8,128)(2,1)S(1)} %bitcast.81, bf16[896,1024]{1,0:T(8,128)(2,1)} %param.10, bf16[112,8,8,128]{3,2,1,0:T(8,128)(2,1)S(1)} %bitcast.96), kind=kOutput, calls=%fused_computation.15 | convolution fusion | flops 940900352 | bytes 5636096 | tf_op jit(solution)/shard_map/dot_general | solution.py:22
  59.7 1.4 convolution_convert_fusion.3
  61.4 1.4 convolution_convert_fusion.2
  63.2 9.0 %all_to_all.41 = bf16[2,4,64,2688]{3,2,1,0:T(8,128)(2,1)S(1)} all-to-all(bf16[2,4,64,2688]{3,2,1,0:T(8,128)(2,1)S(1)} %bitcast.80), channel_id=1, replica_groups=mesh['x'=4,'core'=2,'y'=4,'z'=8] {'core'}, dimensions={0} | all-to-all | bytes 5505024 | tf_op jit(solution)/shard_map/all_to_all | solution.py:68
  72.5 21.9 %all_to_all.42 = bf16[4,64,2688]{2,1,0:T(8,128)(2,1)S(1)} all-to-all(bf16[4,64,2688]{2,1,0:T(8,128)(2,1)S(1)} %fusion.1), channel_id=1, replica_groups=mesh['x'=4,'core'=2,'y'=4,'z'=8] {'x'}, dimensions={0} | all-to-all | bytes 2752512 | tf_op jit(solution)/shard_map/all_to_all | solution.py:69
  94.8 19.6 %all_to_all.43 = bf16[4,64,2688]{2,1,0:T(8,128)(2,1)S(1)} all-to-all(bf16[4,64,2688]{2,1,0:T(8,128)(2,1)S(1)} %broadcast_in_dim.13), channel_id=1, replica_groups=mesh['x'=4,'core'=2,'y'=4,'z'=8] {'x'}, dimensions={0} | all-to-all | bytes 2752512 | tf_op jit(solution)/shard_map/all_to_all | solution.py:43
  114.7 7.9 %all_to_all.44 = bf16[2,4,64,2688]{3,2,1,0:T(8,128)(2,1)S(1)} all-to-all(bf16[2,4,64,2688]{3,2,1,0:T(8,128)(2,1)S(1)} %broadcast_in_dim.14), channel_id=1, replica_groups=mesh['x'=4,'core'=2,'y'=4,'z'=8] {'core'}, dimensions={0} | all-to-all | bytes 5505024 | tf_op jit(solution)/shard_map/all_to_all | solution.py:77
  122.8 1.3 fusion.7
  124.1 1.2 copy-done.6
  125.3 1.3 convolution_convert_fusion
  126.6 1.3 add_convert_fusion.1
  127.9 1.5 pad_maximum_fusion.1
  129.5 4.6 %all-to-all-start.6 = ((bf16[4,128,2048]{2,1,0:T(8,128)(2,1)}), bf16[4,128,2048]{2,1,0:T(8,128)(2,1)}, u32[]{:S(2)}, u32[]{:S(2)}) async-start(bf16[4,128,2048]{2,1,0:T(8,128)(2,1)} %bitcast.87), calls=%async_computation.6 | async-start | bytes 4194304 | tf_op jit(solution)/shard_map/all_to_all | solution.py:50
  134.7 2.7 %copy.54 = f32[112,8,8,128]{3,1,2,0:T(8,128)} copy(f32[112,8,8,128]{3,2,1,0:T(8,128)S(1)} %bitcast.77) | data formatting | bytes 7340032
  137.4 5.0 %copy.33 = f32[1024,896]{1,0:T(8,128)} copy(f32[1024,896]{0,1:T(8,128)} %bitcast.75) | data formatting | bytes 7340032 | tf_op jit(solution)/shard_map/mul | solution.py:14
  142.7 2.8 %copy.55 = f32[112,8,8,128]{3,1,2,0:T(8,128)} copy(f32[112,8,8,128]{3,2,1,0:T(8,128)S(1)} %bitcast.78) | data formatting | bytes 7340032
  145.5 5.0 %copy.31 = f32[1024,896]{1,0:T(8,128)} copy(f32[1024,896]{0,1:T(8,128)} %bitcast.76) | data formatting | bytes 7340032 | tf_op jit(solution)/shard_map/mul | solution.py:14
  150.5 9.5 %all-to-all-done.6 = bf16[4,128,2048]{2,1,0:T(8,128)(2,1)} async-done(((bf16[4,128,2048]{2,1,0:T(8,128)(2,1)}), bf16[4,128,2048]{2,1,0:T(8,128)(2,1)}, u32[]{:S(2)}, u32[]{:S(2)}) %all-to-all-start.6) | async-done | bytes 2097184 | tf_op jit(solution)/shard_map/all_to_all | solution.py:50
  160.0 2.6 %add_convert_fusion.2 = bf16[1,128,2048]{2,1,0:T(8,128)(2,1)} fusion(bf16[4,128,2048]{2,1,0:T(8,128)(2,1)} %all-to-all-done.6), kind=kLoop, calls=%fused_computation.19 | loop fusion | flops 2097152 | bytes 2621440 | tf_op jit(solution)/shard_map/convert.4
  162.7 3.5 %all-to-all-start.7 = ((bf16[8,16,2048]{2,1,0:T(8,128)(2,1)}), bf16[8,16,2048]{2,1,0:T(8,128)(2,1)S(1)}, u32[]{:S(2)}, u32[]{:S(2)}) async-start(bf16[8,16,2048]{2,1,0:T(8,128)(2,1)} %bitcast.14), calls=%async_computation.7 | async-start | bytes 1048576 | tf_op jit(solution)/shard_map/all_to_all | solution.py:50
  166.2 5.0 %multiply_convert_fusion = bf16[1024,896]{1,0:T(8,128)(2,1)} fusion(f32[1024,896]{1,0:T(8,128)} %copy.33, bf16[512,2688]{1,0:T(8,128)(2,1)} %bitcast.91, bf16[512,2048]{1,0:T(8,128)(2,1)S(1)} %bitcast.84), kind=kOutput, calls=%fused_computation.4 | convolution fusion | flops 942276608 | bytes 7471104 | tf_op jit(solution)/shard_map/dot_general | solution.py:28
  171.2 2.6 %multiply_convert_fusion.1 = bf16[1024,896]{1,0:T(8,128)(2,1)} fusion(f32[1024,896]{1,0:T(8,128)S(1)} %copy-done, bf16[512,2688]{1,0:T(8,128)(2,1)S(1)} %bitcast.92, bf16[512,2048]{1,0:T(8,128)(2,1)S(1)} %bitcast.85), kind=kOutput, calls=%fused_computation.5 | convolution fusion | flops 942276608 | bytes 7471104 | tf_op jit(solution)/shard_map/dot_general | solution.py:28
  174.1 2.8 %fusion = bf16[896,1024]{1,0:T(8,128)(2,1)} fusion(f32[112,8,8,128]{3,2,1,0:T(8,128)S(1)} %bitcast.94, bf16[512,2048]{1,0:T(8,128)(2,1)S(1)} %bitcast.86, bf16[512,2688]{1,0:T(8,128)(2,1)S(1)} %bitcast.93), kind=kOutput, calls=%fused_computation.1 | convolution fusion | flops 942276608 | bytes 7471104 | tf_op jit(solution)/shard_map/dot_general | solution.py:28
  176.9 6.2 %all-to-all-done.7 = bf16[8,16,2048]{2,1,0:T(8,128)(2,1)S(1)} async-done(((bf16[8,16,2048]{2,1,0:T(8,128)(2,1)}), bf16[8,16,2048]{2,1,0:T(8,128)(2,1)S(1)}, u32[]{:S(2)}, u32[]{:S(2)}) %all-to-all-start.7) | async-done | bytes 524320 | tf_op jit(solution)/shard_map/all_to_all | solution.py:50
  183.2 0.6 fusion.19
  (37 shorter events, 4.1 us)
Async XLA Ops:
  28.0 4.3 %copy-start.5 = (s32[3,8,7]{2,1,0:T(8,128)S(1)}, s32[3,8,7]{2,1,0:T(8,128)}, u32[]{:S(2)}) copy-start(s32[3,8,7]{2,1,0:T(8,128)} %param.11) | copy-start | bytes 2020
  28.0 28.1 %all-to-all-start.1 = ((bf16[4,128,2048]{2,1,0:T(8,128)(2,1)}), bf16[4,128,2048]{2,1,0:T(8,128)(2,1)S(1)}, u32[]{:S(2)}, u32[]{:S(2)}) async-start(bf16[4,128,2048]{2,1,0:T(8,128)(2,1)} %broadcast_in_dim.12), calls=%async_computation.1 | async-start | bytes 4194304 | tf_op jit(solution)/shard_map/all_to_all | solution.py:43
  56.4 3.3 %copy-start.4 = (bf16[1024,896]{0,1:T(8,128)(2,1)S(1)}, bf16[1024,896]{0,1:T(8,128)(2,1)}, u32[]{:S(2)}) copy-start(bf16[1024,896]{0,1:T(8,128)(2,1)} %copy.24) | copy-start | bytes 5505028
  59.7 1.7 copy-start.3
  122.8 3.8 %copy-start.1 = (bf16[2,4,64,2688]{3,2,0,1:T(8,128)(2,1)}, bf16[2,4,64,2688]{3,2,0,1:T(8,128)(2,1)S(1)}, u32[]{:S(2)}) copy-start(bf16[2,4,64,2688]{3,2,0,1:T(8,128)(2,1)S(1)} %copy.29) | copy-start | bytes 8257540
  122.8 2.5 %copy-start.6 = (bf16[896,1024]{1,0:T(8,128)(2,1)S(1)}, bf16[896,1024]{1,0:T(8,128)(2,1)}, u32[]{:S(2)}) copy-start(bf16[896,1024]{1,0:T(8,128)(2,1)} %param.10) | copy-start | bytes 5505028
  129.5 30.6 %all-to-all-start.6 = ((bf16[4,128,2048]{2,1,0:T(8,128)(2,1)}), bf16[4,128,2048]{2,1,0:T(8,128)(2,1)}, u32[]{:S(2)}, u32[]{:S(2)}) async-start(bf16[4,128,2048]{2,1,0:T(8,128)(2,1)} %bitcast.87), calls=%async_computation.6 | async-start | bytes 4194304 | tf_op jit(solution)/shard_map/all_to_all | solution.py:50
  162.7 20.4 %all-to-all-start.7 = ((bf16[8,16,2048]{2,1,0:T(8,128)(2,1)}), bf16[8,16,2048]{2,1,0:T(8,128)(2,1)S(1)}, u32[]{:S(2)}, u32[]{:S(2)}) async-start(bf16[8,16,2048]{2,1,0:T(8,128)(2,1)} %bitcast.14), calls=%async_computation.7 | async-start | bytes 1048576 | tf_op jit(solution)/shard_map/all_to_all | solution.py:50
  166.2 5.0 %copy-start = (f32[1024,896]{1,0:T(8,128)S(1)}, f32[1024,896]{1,0:T(8,128)}, u32[]{:S(2)}) copy-start(f32[1024,896]{1,0:T(8,128)} %copy.31) | copy-start | bytes 11010052
  166.2 5.0 %copy-start.2 = (bf16[2,4,64,2688]{3,2,0,1:T(8,128)(2,1)S(1)}, bf16[2,4,64,2688]{3,2,0,1:T(8,128)(2,1)}, u32[]{:S(2)}) copy-start(bf16[2,4,64,2688]{3,2,0,1:T(8,128)(2,1)} %copy-done.1) | copy-start | bytes 8257540

commit v7 on v6

--- a/solution.py
+++ b/solution.py
@@ -63,8 +63,7 @@
     n_x = lax.axis_size("x")
     n_core = lax.axis_size("core")
     rows = partial.shape[0] // (n_x * n_core)
-    split = partial.astype(jnp.bfloat16).reshape((n_x, n_core, rows) + partial.shape[1:])
-    split = jnp.swapaxes(split, 0, 1)
+    split = partial.astype(jnp.bfloat16).reshape((n_core, n_x, rows) + partial.shape[1:])
     got = add_blocks(lax.all_to_all(split, "core", 0, 0, tiled=False))
     return add_blocks(lax.all_to_all(got.astype(jnp.bfloat16), "x", 0, 0, tiled=False))
 
@@ -75,7 +74,7 @@
     over_x = gather_rows(local, "x").reshape((n_x,) + local.shape)
     sent = jnp.broadcast_to(over_x[None], (n_core,) + over_x.shape)
     both = lax.all_to_all(sent, "core", 0, 0, tiled=False)
-    return jnp.swapaxes(both, 0, 1).reshape((n_x * n_core * local.shape[0],) + local.shape[1:])
+    return both.reshape((n_core * n_x * local.shape[0],) + local.shape[1:])
 
 
 def shards(tokens, cotangent, gate_weight, up_weight, down_weight, block_mask):

time: 185 us -> 184 us (level)
  no operation moved by 1% of the time
where the time goes in v7:
time: 184 us; the launch traced here: 183 us
  blocking collectives  83.4 us (45%)
  waiting for transfers between devices  31.7 us (17%)
  local copies, waits for them, and re-layouts  29.2 us (16%)
  matrix products  19.9 us (11%)
  starting transfers between devices  12.4 us (7%)
  other arithmetic  5.86 us (3%)
    all_to_all x2, blocking collectives, gather_rows(): got = lax.all_to_all(sent, axis, 0, 0, tiled=False)  44.5 us
    all_to_all x1, blocking collectives, reduce_row(): lax.all_to_all(got.astype(jnp.bfloat16), 'x', 0, 0, tiled=False)  21.9 us
    all_to_all x1, waiting for transfers between devices, gather_rows(): got = lax.all_to_all(sent, axis, 0, 0, tiled=False)  16 us
    all_to_all x2, waiting for transfers between devices, reduce_rows(): got = lax.all_to_all(chunks, axis, 0, 0, tiled=False)  15.7 us
    unnamed x18, local copies, waits for them, and re-layouts  14.2 us
    mul x8, local copies, waits for them, and re-layouts, masked(): shaped * mask.astype(weight.dtype)[:, None, :, None]  11.9 us
    dot_general x3, matrix products, contract_rows(): lax.dot_general(left, right, (((0,), (0,)), ((), ())), preferred_element_...  10.4 us
    all_to_all x1, blocking collectives, reduce_row(): got = add_blocks(lax.all_to_all(split, 'core', 0, 0, tiled=False))  9.04 us
  transfers between devices with their start and end apart: 3, of which 3 were waited for; matrix products, arithmetic and copies ran while one was open for 19% of the time, Pallas kernels for 0%

profile of v7, /device:TPU:1, one launch (start us, length us, event | category | flops | bytes accessed | tf_op | source)
XLA Modules:
  0.0 183.4 jit_solution(17357768493379599332)
XLA Ops:
  0.6 0.8 pad_maximum_fusion.3
  1.5 24.9 %all_to_all.40 = bf16[8,16,2048]{2,1,0:T(8,128)(2,1)S(1)} all-to-all(bf16[8,16,2048]{2,1,0:T(8,128)(2,1)S(1)} %broadcast_in_dim.10), channel_id=1, replica_groups=mesh['x'=4,'core'=2,'y'=4,'z'=8] {'z'}, dimensions={0} | all-to-all | bytes 1048576 | tf_op jit(solution)/shard_map/all_to_all | solution.py:43
  26.4 1.6 broadcast_in_dim.12
  28.0 4.3 %all-to-all-start.1 = ((bf16[4,128,2048]{2,1,0:T(8,128)(2,1)}), bf16[4,128,2048]{2,1,0:T(8,128)(2,1)S(1)}, u32[]{:S(2)}, u32[]{:S(2)}) async-start(bf16[4,128,2048]{2,1,0:T(8,128)(2,1)} %broadcast_in_dim.12), calls=%async_computation.1 | async-start | bytes 4194304 | tf_op jit(solution)/shard_map/all_to_all | solution.py:43
  32.6 3.8 %copy.14 = bf16[1024,896]{0,1:T(8,128)(2,1)} copy(bf16[1024,896]{1,0:T(8,128)(2,1)} %param.8) | data formatting | bytes 3670016 | tf_op args[2]
  36.4 3.8 %copy.16 = bf16[1024,896]{0,1:T(8,128)(2,1)} copy(bf16[1024,896]{1,0:T(8,128)(2,1)} %param.9) | data formatting | bytes 3670016 | tf_op args[3]
  40.1 16.0 %all-to-all-done.1 = bf16[4,128,2048]{2,1,0:T(8,128)(2,1)S(1)} async-done(((bf16[4,128,2048]{2,1,0:T(8,128)(2,1)}), bf16[4,128,2048]{2,1,0:T(8,128)(2,1)S(1)}, u32[]{:S(2)}, u32[]{:S(2)}) %all-to-all-start.1) | async-done | bytes 2097184 | tf_op jit(solution)/shard_map/all_to_all | solution.py:43
  56.4 2.9 %convolution_convert_fusion.1 = bf16[512,896]{1,0:T(8,128)(2,1)S(1)} fusion(bf16[512,2048]{1,0:T(8,128)(2,1)S(1)} %bitcast.75, bf16[896,1024]{1,0:T(8,128)(2,1)} %param.10, bf16[112,8,8,128]{3,2,1,0:T(8,128)(2,1)S(1)} %bitcast.90), kind=kOutput, calls=%fused_computation.14 | convolution fusion | flops 940900352 | bytes 5636096 | tf_op jit(solution)/shard_map/dot_general | solution.py:22
  59.7 1.4 convolution_convert_fusion.3
  61.4 1.4 convolution_convert_fusion.2
  63.0 9.0 %all_to_all.41 = bf16[2,4,64,2688]{3,2,1,0:T(8,128)(2,1)S(1)} all-to-all(bf16[2,4,64,2688]{3,2,1,0:T(8,128)(2,1)S(1)} %bitcast.74), channel_id=1, replica_groups=mesh['x'=4,'core'=2,'y'=4,'z'=8] {'core'}, dimensions={0} | all-to-all | bytes 5505024 | tf_op jit(solution)/shard_map/all_to_all | solution.py:67
  72.3 21.9 %all_to_all.42 = bf16[4,64,2688]{2,1,0:T(8,128)(2,1)S(1)} all-to-all(bf16[4,64,2688]{2,1,0:T(8,128)(2,1)S(1)} %fusion.1), channel_id=1, replica_groups=mesh['x'=4,'core'=2,'y'=4,'z'=8] {'x'}, dimensions={0} | all-to-all | bytes 2752512 | tf_op jit(solution)/shard_map/all_to_all | solution.py:68
  94.6 19.6 %all_to_all.43 = bf16[4,64,2688]{2,1,0:T(8,128)(2,1)S(1)} all-to-all(bf16[4,64,2688]{2,1,0:T(8,128)(2,1)S(1)} %broadcast_in_dim.13), channel_id=1, replica_groups=mesh['x'=4,'core'=2,'y'=4,'z'=8] {'x'}, dimensions={0} | all-to-all | bytes 2752512 | tf_op jit(solution)/shard_map/all_to_all | solution.py:43
  114.4 7.9 %all_to_all.44 = bf16[2,4,64,2688]{3,2,1,0:T(8,128)(2,1)S(1)} all-to-all(bf16[2,4,64,2688]{3,2,1,0:T(8,128)(2,1)S(1)} %broadcast_in_dim.14), channel_id=1, replica_groups=mesh['x'=4,'core'=2,'y'=4,'z'=8] {'core'}, dimensions={0} | all-to-all | bytes 5505024 | tf_op jit(solution)/shard_map/all_to_all | solution.py:76
  122.4 1.3 fusion.7
  123.7 1.2 copy-done.6
  124.9 1.3 convolution_convert_fusion
  126.2 1.3 add_convert_fusion.1
  127.5 1.5 pad_maximum_fusion.1
  129.0 4.6 %all-to-all-start.6 = ((bf16[4,128,2048]{2,1,0:T(8,128)(2,1)}), bf16[4,128,2048]{2,1,0:T(8,128)(2,1)}, u32[]{:S(2)}, u32[]{:S(2)}) async-start(bf16[4,128,2048]{2,1,0:T(8,128)(2,1)} %bitcast.81), calls=%async_computation.6 | async-start | bytes 4194304 | tf_op jit(solution)/shard_map/all_to_all | solution.py:50
  134.2 2.7 %copy.41 = f32[112,8,8,128]{3,1,2,0:T(8,128)} copy(f32[112,8,8,128]{3,2,1,0:T(8,128)S(1)} %bitcast.72) | data formatting | bytes 7340032
  136.9 5.0 %copy.21 = f32[1024,896]{1,0:T(8,128)} copy(f32[1024,896]{0,1:T(8,128)} %bitcast.70) | data formatting | bytes 7340032 | tf_op jit(solution)/shard_map/mul | solution.py:14
  142.2 2.8 %copy.42 = f32[112,8,8,128]{3,1,2,0:T(8,128)} copy(f32[112,8,8,128]{3,2,1,0:T(8,128)S(1)} %bitcast.73) | data formatting | bytes 7340032
  145.0 5.0 %copy.19 = f32[1024,896]{1,0:T(8,128)} copy(f32[1024,896]{0,1:T(8,128)} %bitcast.71) | data formatting | bytes 7340032 | tf_op jit(solution)/shard_map/mul | solution.py:14
  150.0 9.5 %all-to-all-done.6 = bf16[4,128,2048]{2,1,0:T(8,128)(2,1)} async-done(((bf16[4,128,2048]{2,1,0:T(8,128)(2,1)}), bf16[4,128,2048]{2,1,0:T(8,128)(2,1)}, u32[]{:S(2)}, u32[]{:S(2)}) %all-to-all-start.6) | async-done | bytes 2097184 | tf_op jit(solution)/shard_map/all_to_all | solution.py:50
  159.6 2.6 %add_convert_fusion.2 = bf16[1,128,2048]{2,1,0:T(8,128)(2,1)} fusion(bf16[4,128,2048]{2,1,0:T(8,128)(2,1)} %all-to-all-done.6), kind=kLoop, calls=%fused_computation.18 | loop fusion | flops 2097152 | bytes 2621440 | tf_op jit(solution)/shard_map/convert.4
  162.2 3.5 %all-to-all-start.7 = ((bf16[8,16,2048]{2,1,0:T(8,128)(2,1)}), bf16[8,16,2048]{2,1,0:T(8,128)(2,1)S(1)}, u32[]{:S(2)}, u32[]{:S(2)}) async-start(bf16[8,16,2048]{2,1,0:T(8,128)(2,1)} %bitcast.11), calls=%async_computation.7 | async-start | bytes 1048576 | tf_op jit(solution)/shard_map/all_to_all | solution.py:50
  165.7 5.0 %multiply_convert_fusion = bf16[1024,896]{1,0:T(8,128)(2,1)} fusion(f32[1024,896]{1,0:T(8,128)} %copy.21, bf16[512,2688]{1,0:T(8,128)(2,1)} %bitcast.85, bf16[512,2048]{1,0:T(8,128)(2,1)S(1)} %bitcast.78), kind=kOutput, calls=%fused_computation.4 | convolution fusion | flops 942276608 | bytes 7471104 | tf_op jit(solution)/shard_map/dot_general | solution.py:28
  170.7 2.6 %multiply_convert_fusion.1 = bf16[1024,896]{1,0:T(8,128)(2,1)} fusion(f32[1024,896]{1,0:T(8,128)S(1)} %copy-done, bf16[512,2688]{1,0:T(8,128)(2,1)S(1)} %bitcast.86, bf16[512,2048]{1,0:T(8,128)(2,1)S(1)} %bitcast.79), kind=kOutput, calls=%fused_computation.5 | convolution fusion | flops 942276608 | bytes 7471104 | tf_op jit(solution)/shard_map/dot_general | solution.py:28
  173.7 2.8 %fusion = bf16[896,1024]{1,0:T(8,128)(2,1)} fusion(f32[112,8,8,128]{3,2,1,0:T(8,128)S(1)} %bitcast.88, bf16[512,2048]{1,0:T(8,128)(2,1)S(1)} %bitcast.80, bf16[512,2688]{1,0:T(8,128)(2,1)S(1)} %bitcast.87), kind=kOutput, calls=%fused_computation.1 | convolution fusion | flops 942276608 | bytes 7471104 | tf_op jit(solution)/shard_map/dot_general | solution.py:28
  176.5 6.2 %all-to-all-done.7 = bf16[8,16,2048]{2,1,0:T(8,128)(2,1)S(1)} async-done(((bf16[8,16,2048]{2,1,0:T(8,128)(2,1)}), bf16[8,16,2048]{2,1,0:T(8,128)(2,1)S(1)}, u32[]{:S(2)}, u32[]{:S(2)}) %all-to-all-start.7) | async-done | bytes 524320 | tf_op jit(solution)/shard_map/all_to_all | solution.py:50
  182.7 0.6 fusion.19
  (35 shorter events, 3.6 us)
Async XLA Ops:
  28.0 4.3 %copy-start.5 = (s32[3,8,7]{2,1,0:T(8,128)S(1)}, s32[3,8,7]{2,1,0:T(8,128)}, u32[]{:S(2)}) copy-start(s32[3,8,7]{2,1,0:T(8,128)} %param.11) | copy-start | bytes 2020
  28.0 28.1 %all-to-all-start.1 = ((bf16[4,128,2048]{2,1,0:T(8,128)(2,1)}), bf16[4,128,2048]{2,1,0:T(8,128)(2,1)S(1)}, u32[]{:S(2)}, u32[]{:S(2)}) async-start(bf16[4,128,2048]{2,1,0:T(8,128)(2,1)} %broadcast_in_dim.12), calls=%async_computation.1 | async-start | bytes 4194304 | tf_op jit(solution)/shard_map/all_to_all | solution.py:43
  56.4 3.3 %copy-start.4 = (bf16[1024,896]{0,1:T(8,128)(2,1)S(1)}, bf16[1024,896]{0,1:T(8,128)(2,1)}, u32[]{:S(2)}) copy-start(bf16[1024,896]{0,1:T(8,128)(2,1)} %copy.14) | copy-start | bytes 5505028
  59.7 1.7 copy-start.3
  122.4 3.8 %copy-start.1 = (bf16[2,4,64,2688]{3,2,1,0:T(8,128)(2,1)}, bf16[2,4,64,2688]{3,2,1,0:T(8,128)(2,1)S(1)}, u32[]{:S(2)}) copy-start(bf16[2,4,64,2688]{3,2,1,0:T(8,128)(2,1)S(1)} %all_to_all.44) | copy-start | bytes 8257540
  122.4 2.5 %copy-start.6 = (bf16[896,1024]{1,0:T(8,128)(2,1)S(1)}, bf16[896,1024]{1,0:T(8,128)(2,1)}, u32[]{:S(2)}) copy-start(bf16[896,1024]{1,0:T(8,128)(2,1)} %param.10) | copy-start | bytes 5505028
  129.0 30.6 %all-to-all-start.6 = ((bf16[4,128,2048]{2,1,0:T(8,128)(2,1)}), bf16[4,128,2048]{2,1,0:T(8,128)(2,1)}, u32[]{:S(2)}, u32[]{:S(2)}) async-start(bf16[4,128,2048]{2,1,0:T(8,128)(2,1)} %bitcast.81), calls=%async_computation.6 | async-start | bytes 4194304 | tf_op jit(solution)/shard_map/all_to_all | solution.py:50
  162.2 20.5 %all-to-all-start.7 = ((bf16[8,16,2048]{2,1,0:T(8,128)(2,1)}), bf16[8,16,2048]{2,1,0:T(8,128)(2,1)S(1)}, u32[]{:S(2)}, u32[]{:S(2)}) async-start(bf16[8,16,2048]{2,1,0:T(8,128)(2,1)} %bitcast.11), calls=%async_computation.7 | async-start | bytes 1048576 | tf_op jit(solution)/shard_map/all_to_all | solution.py:50
  165.7 5.0 %copy-start = (f32[1024,896]{1,0:T(8,128)S(1)}, f32[1024,896]{1,0:T(8,128)}, u32[]{:S(2)}) copy-start(f32[1024,896]{1,0:T(8,128)} %copy.19) | copy-start | bytes 11010052
  165.7 5.0 %copy-start.2 = (bf16[2,4,64,2688]{3,2,1,0:T(8,128)(2,1)S(1)}, bf16[2,4,64,2688]{3,2,1,0:T(8,128)(2,1)}, u32[]{:S(2)}) copy-start(bf16[2,4,64,2688]{3,2,1,0:T(8,128)(2,1)} %copy-done.1) | copy-start | bytes 8257540

commit v8 on v7

--- a/solution.py
+++ b/solution.py
@@ -59,22 +59,28 @@
     return reduce_rows(reduce_rows(partial, "y"), "z")
 
 
+def swap_core(value):
+    return lax.ppermute(value, "core", [(0, 1), (1, 0)])
+
+
 def reduce_row(partial):
     n_x = lax.axis_size("x")
     n_core = lax.axis_size("core")
     rows = partial.shape[0] // (n_x * n_core)
     split = partial.astype(jnp.bfloat16).reshape((n_core, n_x, rows) + partial.shape[1:])
-    got = add_blocks(lax.all_to_all(split, "core", 0, 0, tiled=False))
+    me = lax.axis_index("core")
+    mine = lax.dynamic_index_in_dim(split, me, 0, keepdims=False)
+    other = lax.dynamic_index_in_dim(split, 1 - me, 0, keepdims=False)
+    got = mine.astype(jnp.float32) + swap_core(other).astype(jnp.float32)
     return add_blocks(lax.all_to_all(got.astype(jnp.bfloat16), "x", 0, 0, tiled=False))
 
 
 def gather_row(local):
-    n_x = lax.axis_size("x")
-    n_core = lax.axis_size("core")
-    over_x = gather_rows(local, "x").reshape((n_x,) + local.shape)
-    sent = jnp.broadcast_to(over_x[None], (n_core,) + over_x.shape)
-    both = lax.all_to_all(sent, "core", 0, 0, tiled=False)
-    return both.reshape((n_core * n_x * local.shape[0],) + local.shape[1:])
+    over_x = gather_rows(local, "x")
+    theirs = swap_core(over_x)
+    first = lax.axis_index("core") == 0
+    both = jnp.concatenate([jnp.where(first, over_x, theirs), jnp.where(first, theirs, over_x)], axis=0)
+    return both
 
 
 def shards(tokens, cotangent, gate_weight, up_weight, down_weight, block_mask):

time: 184 us -> 188 us (1.022)
  blocking collectives: 83.4 us -> 66.4 us
  local copies, waits for them, and re-layouts: 29.2 us -> 37.6 us
  starting transfers between devices: 12.4 us -> 18.2 us
  other arithmetic: 5.86 us -> 9.16 us
  waiting for transfers between devices: 31.7 us -> 34.4 us
    all_to_all x2 -> x0, blocking collectives: 17 us -> none  [the longest x1 9.04 us: reduce_row(): got = add_blocks(lax.all_to_all(split, 'core', 0, 0, tiled=False))]
    unnamed x18 -> x36, local copies, waits for them, and re-layouts: 14.2 us -> 21.7 us
    ppermute x0 -> x2, waiting for transfers between devices: none -> 5.98 us  [swap_core(): return lax.ppermute(value, 'core', [(0, 1), (1, 0)])]
    ppermute x0 -> x2, starting transfers between devices: none -> 5.85 us  [swap_core(): return lax.ppermute(value, 'core', [(0, 1), (1, 0)])]
    all_to_all x2, waiting for transfers between devices: 15.7 us -> 12.4 us  [reduce_rows(): got = lax.all_to_all(chunks, axis, 0, 0, tiled=False)]
    dot_general x3, matrix products: 10.4 us -> 12.6 us  [contract_rows(): lax.dot_general(left, right, (((0,), (0,)), ((), ())), preferred_element_...]
    select_n x0 -> x1, other arithmetic: none -> 2 us  [gather_row(): jnp.where(first, over_x, theirs)]
  transfers between devices with their start and end apart: 3 -> 5, of which waited for: 3 -> 5; matrix products, arithmetic and copies ran while one was open for 19% -> 20% of each run, Pallas kernels for 0% -> 0%
where the time goes in v8:
time: 188 us; the launch traced here: 187 us
  blocking collectives  66.4 us (35%)
  local copies, waits for them, and re-layouts  37.6 us (20%)
  waiting for transfers between devices  34.4 us (18%)
  matrix products  20.4 us (11%)
  starting transfers between devices  18.2 us (10%)
  other arithmetic  9.16 us (5%)
    all_to_all x2, blocking collectives, gather_rows(): got = lax.all_to_all(sent, axis, 0, 0, tiled=False)  44.5 us
    all_to_all x1, blocking collectives, reduce_row(): lax.all_to_all(got.astype(jnp.bfloat16), 'x', 0, 0, tiled=False)  21.9 us
    unnamed x36, local copies, waits for them, and re-layouts  21.7 us
    all_to_all x1, waiting for transfers between devices, gather_rows(): got = lax.all_to_all(sent, axis, 0, 0, tiled=False)  16 us
    dot_general x3, matrix products, contract_rows(): lax.dot_general(left, right, (((0,), (0,)), ((), ())), preferred_element_...  12.6 us
    all_to_all x2, waiting for transfers between devices, reduce_rows(): got = lax.all_to_all(chunks, axis, 0, 0, tiled=False)  12.4 us
    mul x8, local copies, waits for them, and re-layouts, masked(): shaped * mask.astype(weight.dtype)[:, None, :, None]  11.9 us
    all_to_all x2, starting transfers between devices, reduce_rows(): got = lax.all_to_all(chunks, axis, 0, 0, tiled=False)  8.13 us
  transfers between devices with their start and end apart: 5, of which 5 were waited for; matrix products, arithmetic and copies ran while one was open for 20% of the time, Pallas kernels for 0%

profile of v8, /device:TPU:1, one launch (start us, length us, event | category | flops | bytes accessed | tf_op | source)
XLA Modules:
  0.0 186.9 jit_solution(2945339200762360722)
XLA Ops:
  1.5 24.9 %all_to_all.30 = bf16[8,16,2048]{2,1,0:T(8,128)(2,1)S(1)} all-to-all(bf16[8,16,2048]{2,1,0:T(8,128)(2,1)S(1)} %broadcast_in_dim.8), channel_id=1, replica_groups=mesh['x'=4,'core'=2,'y'=4,'z'=8] {'z'}, dimensions={0} | all-to-all | bytes 1048576 | tf_op jit(solution)/shard_map/all_to_all | solution.py:43
  26.4 1.6 broadcast_in_dim.10
  28.0 4.2 %all-to-all-start.1 = ((bf16[4,128,2048]{2,1,0:T(8,128)(2,1)}), bf16[4,128,2048]{2,1,0:T(8,128)(2,1)S(1)}, u32[]{:S(2)}, u32[]{:S(2)}) async-start(bf16[4,128,2048]{2,1,0:T(8,128)(2,1)} %broadcast_in_dim.10), calls=%async_computation.1 | async-start | bytes 4194304 | tf_op jit(solution)/shard_map/all_to_all | solution.py:43
  32.2 3.8 %copy.16 = bf16[1024,896]{0,1:T(8,128)(2,1)} copy(bf16[1024,896]{1,0:T(8,128)(2,1)} %param.9) | data formatting | bytes 3670016 | tf_op args[3]
  36.1 3.8 %copy.14 = bf16[1024,896]{0,1:T(8,128)(2,1)} copy(bf16[1024,896]{1,0:T(8,128)(2,1)} %param.8) | data formatting | bytes 3670016 | tf_op args[2]
  40.0 16.0 %all-to-all-done.1 = bf16[4,128,2048]{2,1,0:T(8,128)(2,1)S(1)} async-done(((bf16[4,128,2048]{2,1,0:T(8,128)(2,1)}), bf16[4,128,2048]{2,1,0:T(8,128)(2,1)S(1)}, u32[]{:S(2)}, u32[]{:S(2)}) %all-to-all-start.1) | async-done | bytes 2097184 | tf_op jit(solution)/shard_map/all_to_all | solution.py:43
  57.5 1.3 copy-done.14
  58.8 1.3 convolution_convert_fusion.1
  62.2 1.3 convolution_convert_fusion.2
  65.5 1.3 convolution_convert_fusion.3
  68.2 3.5 %collective-permute-start = (bf16[4,64,2688]{2,1,0:T(8,128)(2,1)}, bf16[4,64,2688]{2,1,0:T(8,128)(2,1)}, u32[]{:S(2)}, u32[]{:S(2)}) collective-permute-start(bf16[4,64,2688]{2,1,0:T(8,128)(2,1)} %dynamic-slice_bitcast_fusion), channel_id=1, source_target_pairs={{0,32},{32,0},{1,33},{33,1},{2,34},{34,2},{3,35},{35,3},{4,36},{36... | collective-permute-start | bytes 4128776 | tf_op jit(solution)/shard_map/ppermute | solution.py:63
  71.7 3.1 %collective-permute-done = bf16[4,64,2688]{2,1,0:T(8,128)(2,1)} collective-permute-done((bf16[4,64,2688]{2,1,0:T(8,128)(2,1)}, bf16[4,64,2688]{2,1,0:T(8,128)(2,1)}, u32[]{:S(2)}, u32[]{:S(2)}) %collective-permute-start) | collective-permute-done | bytes 1376288 | tf_op jit(solution)/shard_map/ppermute | solution.py:63
  74.8 1.7 fusion.1
  76.5 21.9 %all_to_all.31 = bf16[4,64,2688]{2,1,0:T(8,128)(2,1)S(1)} all-to-all(bf16[4,64,2688]{2,1,0:T(8,128)(2,1)S(1)} %fusion.1), channel_id=1, replica_groups=mesh['x'=4,'core'=2,'y'=4,'z'=8] {'x'}, dimensions={0} | all-to-all | bytes 2752512 | tf_op jit(solution)/shard_map/all_to_all | solution.py:75
  98.8 19.6 %all_to_all.32 = bf16[4,64,2688]{2,1,0:T(8,128)(2,1)S(1)} all-to-all(bf16[4,64,2688]{2,1,0:T(8,128)(2,1)S(1)} %broadcast_in_dim.11), channel_id=1, replica_groups=mesh['x'=4,'core'=2,'y'=4,'z'=8] {'x'}, dimensions={0} | all-to-all | bytes 2752512 | tf_op jit(solution)/shard_map/all_to_all | solution.py:43
  118.4 2.4 %collective-permute-start.1 = (bf16[256,2688]{1,0:T(8,128)(2,1)S(1)}, bf16[256,2688]{1,0:T(8,128)(2,1)}, u32[]{:S(2)}, u32[]{:S(2)}) collective-permute-start(bf16[256,2688]{1,0:T(8,128)(2,1)S(1)} %bitcast.88), channel_id=1, source_target_pairs={{0,32},{32,0},{1,33},{33,1},{2,34},{34,2},{3,35},{35,3},{4,36},{36... | collective-permute-start | bytes 4128776 | tf_op jit(solution)/shard_map/ppermute | solution.py:63
  120.7 2.9 %collective-permute-done.1 = bf16[256,2688]{1,0:T(8,128)(2,1)} collective-permute-done((bf16[256,2688]{1,0:T(8,128)(2,1)S(1)}, bf16[256,2688]{1,0:T(8,128)(2,1)}, u32[]{:S(2)}, u32[]{:S(2)}) %collective-permute-start.1) | collective-permute-done | bytes 1376288 | tf_op jit(solution)/shard_map/ppermute | solution.py:63
  123.6 2.0 %broadcast_select_fusion.1 = (bf16[256,2688]{1,0:T(8,128)(2,1)S(1)}, bf16[256,2688]{1,0:T(8,128)(2,1)S(1)}) fusion(bf16[256,2688]{1,0:T(8,128)(2,1)} %collective-permute-done.1, pred[]{:T(512)S(6)} %eq.3, bf16[4,64,2688]{2,1,0:T(8,128)(2,1)} %copy-done.2), kind=kLoop, calls=%fused_computation.24 | loop fusion | flops 1376256 | bytes 5505025 | tf_op jit(solution)/shard_map/jit(_where)/select_n | solution.py:82
  129.8 1.3 add_convert_fusion
  131.1 1.5 pad_maximum_fusion.1
  132.6 4.6 %all-to-all-start.4 = ((bf16[4,128,2048]{2,1,0:T(8,128)(2,1)}), bf16[4,128,2048]{2,1,0:T(8,128)(2,1)}, u32[]{:S(2)}, u32[]{:S(2)}) async-start(bf16[4,128,2048]{2,1,0:T(8,128)(2,1)} %bitcast.87), calls=%async_computation.4 | async-start | bytes 4194304 | tf_op jit(solution)/shard_map/all_to_all | solution.py:50
  137.6 2.7 %copy.42 = f32[112,8,8,128]{3,1,2,0:T(8,128)} copy(f32[112,8,8,128]{3,2,1,0:T(8,128)S(1)} %bitcast.77) | data formatting | bytes 7340032
  140.3 5.0 %copy.19 = f32[1024,896]{1,0:T(8,128)} copy(f32[1024,896]{0,1:T(8,128)} %bitcast.75) | data formatting | bytes 7340032 | tf_op jit(solution)/shard_map/mul | solution.py:14
  145.7 2.7 %copy.41 = f32[112,8,8,128]{3,1,2,0:T(8,128)} copy(f32[112,8,8,128]{3,2,1,0:T(8,128)S(1)} %bitcast.78) | data formatting | bytes 7340032
  148.4 5.0 %copy.21 = f32[1024,896]{1,0:T(8,128)} copy(f32[1024,896]{0,1:T(8,128)} %bitcast.76) | data formatting | bytes 7340032 | tf_op jit(solution)/shard_map/mul | solution.py:14
  153.5 4.9 %multiply_convert_fusion = bf16[1024,896]{1,0:T(8,128)(2,1)} fusion(f32[1024,896]{1,0:T(8,128)} %copy.21, bf16[512,2048]{1,0:T(8,128)(2,1)} %bitcast.84, bf16[256,2688]{1,0:T(8,128)(2,1)S(1)} %get-tuple-element.6, bf16[256,2688]{1,0:T(8,128)(2,1)S(1)} %get-tuple-element.5), kind=kOutput, calls=%fused_computation.4 | convolution fusion | flops 944111616 | bytes 9306112 | tf_op jit(solution)/shard_map/dot_general | solution.py:28
  158.4 4.8 %all-to-all-done.4 = bf16[4,128,2048]{2,1,0:T(8,128)(2,1)} async-done(((bf16[4,128,2048]{2,1,0:T(8,128)(2,1)}), bf16[4,128,2048]{2,1,0:T(8,128)(2,1)}, u32[]{:S(2)}, u32[]{:S(2)}) %all-to-all-start.4) | async-done | bytes 2097184 | tf_op jit(solution)/shard_map/all_to_all | solution.py:50
  163.1 2.6 %add_convert_fusion.1 = bf16[1,128,2048]{2,1,0:T(8,128)(2,1)} fusion(bf16[4,128,2048]{2,1,0:T(8,128)(2,1)} %all-to-all-done.4), kind=kLoop, calls=%fused_computation.25 | loop fusion | flops 2097152 | bytes 2621440 | tf_op jit(solution)/shard_map/convert.5
  165.8 3.5 %all-to-all-start.5 = ((bf16[8,16,2048]{2,1,0:T(8,128)(2,1)}), bf16[8,16,2048]{2,1,0:T(8,128)(2,1)S(1)}, u32[]{:S(2)}, u32[]{:S(2)}) async-start(bf16[8,16,2048]{2,1,0:T(8,128)(2,1)} %bitcast.12), calls=%async_computation.5 | async-start | bytes 1048576 | tf_op jit(solution)/shard_map/all_to_all | solution.py:50
  169.3 4.9 %multiply_convert_fusion.1 = bf16[1024,896]{1,0:T(8,128)(2,1)} fusion(f32[1024,896]{1,0:T(8,128)} %copy.19, bf16[512,2048]{1,0:T(8,128)(2,1)} %bitcast.85, bf16[256,2688]{1,0:T(8,128)(2,1)S(1)} %get-tuple-element.5, bf16[256,2688]{1,0:T(8,128)(2,1)S(1)} %get-tuple-element.6), kind=kOutput, calls=%fused_computation.5 | convolution fusion | flops 944111616 | bytes 9306112 | tf_op jit(solution)/shard_map/dot_general | solution.py:28
  175.7 2.8 %fusion = bf16[896,1024]{1,0:T(8,128)(2,1)} fusion(f32[112,8,8,128]{3,2,1,0:T(8,128)S(1)} %bitcast.89, bf16[512,2048]{1,0:T(8,128)(2,1)S(1)} %bitcast.86, bf16[256,2688]{1,0:T(8,128)(2,1)S(1)} %get-tuple-element.5, bf16[256,2688]{1,0:T(8,128)(2,1)S(1)} %get-tuple-element.6), kind=kOutput, calls=%fused_computation.1 | convolution fusion | flops 944111616 | bytes 9306112 | tf_op jit(solution)/shard_map/dot_general | solution.py:28
  178.6 7.7 %all-to-all-done.5 = bf16[8,16,2048]{2,1,0:T(8,128)(2,1)S(1)} async-done(((bf16[8,16,2048]{2,1,0:T(8,128)(2,1)}), bf16[8,16,2048]{2,1,0:T(8,128)(2,1)S(1)}, u32[]{:S(2)}, u32[]{:S(2)}) %all-to-all-start.5) | async-done | bytes 524320 | tf_op jit(solution)/shard_map/all_to_all | solution.py:50
  (56 shorter events, 15.7 us)
Async XLA Ops:
  28.0 28.0 %all-to-all-start.1 = ((bf16[4,128,2048]{2,1,0:T(8,128)(2,1)}), bf16[4,128,2048]{2,1,0:T(8,128)(2,1)S(1)}, u32[]{:S(2)}, u32[]{:S(2)}) async-start(bf16[4,128,2048]{2,1,0:T(8,128)(2,1)} %broadcast_in_dim.10), calls=%async_computation.1 | async-start | bytes 4194304 | tf_op jit(solution)/shard_map/all_to_all | solution.py:43
  32.2 3.8 %copy-start.13 = (s32[3,8,7]{2,1,0:T(8,128)S(1)}, s32[3,8,7]{2,1,0:T(8,128)}, u32[]{:S(2)}) copy-start(s32[3,8,7]{2,1,0:T(8,128)} %param.11) | copy-start | bytes 2020
  56.0 7.8 %copy-start = (bf16[4,128,2048]{2,1,0:T(8,128)(2,1)}, bf16[4,128,2048]{2,1,0:T(8,128)(2,1)S(1)}, u32[]{:S(2)}) copy-start(bf16[4,128,2048]{2,1,0:T(8,128)(2,1)S(1)} %all-to-all-done.1) | copy-start | bytes 6291460
  56.0 2.9 %copy-start.14 = (bf16[896,1024]{1,0:T(8,128)(2,1)S(1)}, bf16[896,1024]{1,0:T(8,128)(2,1)}, u32[]{:S(2)}) copy-start(bf16[896,1024]{1,0:T(8,128)(2,1)} %param.10) | copy-start | bytes 5505028
  56.3 1.2 copy-start.7
  60.1 2.0 %copy-start.3 = (bf16[1024,896]{0,1:T(8,128)(2,1)S(1)}, bf16[1024,896]{0,1:T(8,128)(2,1)}, u32[]{:S(2)}) copy-start(bf16[1024,896]{0,1:T(8,128)(2,1)} %copy.16) | copy-start | bytes 5505028
  60.5 1.2 copy-start.11
  63.5 2.0 %copy-start.5 = (bf16[1024,896]{0,1:T(8,128)(2,1)S(1)}, bf16[1024,896]{0,1:T(8,128)(2,1)}, u32[]{:S(2)}) copy-start(bf16[1024,896]{0,1:T(8,128)(2,1)} %copy.14) | copy-start | bytes 5505028
  63.8 1.3 copy-start.9
  68.2 6.6 %collective-permute-start = (bf16[4,64,2688]{2,1,0:T(8,128)(2,1)}, bf16[4,64,2688]{2,1,0:T(8,128)(2,1)}, u32[]{:S(2)}, u32[]{:S(2)}) collective-permute-start(bf16[4,64,2688]{2,1,0:T(8,128)(2,1)} %dynamic-slice_bitcast_fusion), channel_id=1, source_target_pairs={{0,32},{32,0},{1,33},{33,1},{2,34},{34,2},{3,35},{35,3},{4,36},{36... | collective-permute-start | bytes 4128776 | tf_op jit(solution)/shard_map/ppermute | solution.py:63
  118.4 2.4 %copy-start.2 = (bf16[4,64,2688]{2,1,0:T(8,128)(2,1)}, bf16[4,64,2688]{2,1,0:T(8,128)(2,1)S(1)}, u32[]{:S(2)}) copy-start(bf16[4,64,2688]{2,1,0:T(8,128)(2,1)S(1)} %all_to_all.32) | copy-start | bytes 4128772
  118.4 5.3 %collective-permute-start.1 = (bf16[256,2688]{1,0:T(8,128)(2,1)S(1)}, bf16[256,2688]{1,0:T(8,128)(2,1)}, u32[]{:S(2)}, u32[]{:S(2)}) collective-permute-start(bf16[256,2688]{1,0:T(8,128)(2,1)S(1)} %bitcast.88), channel_id=1, source_target_pairs={{0,32},{32,0},{1,33},{33,1},{2,34},{34,2},{3,35},{35,3},{4,36},{36... | collective-permute-start | bytes 4128776 | tf_op jit(solution)/shard_map/ppermute | solution.py:63
  120.7 4.9 %copy-start.4 = (bf16[1024,896]{0,1:T(8,128)(2,1)S(1)}, bf16[1024,896]{0,1:T(8,128)(2,1)}, u32[]{:S(2)}) copy-start(bf16[1024,896]{0,1:T(8,128)(2,1)} %copy.16) | copy-start | bytes 5505028
  120.7 4.9 %copy-start.12 = (bf16[8,128,7,128]{1,0,3,2:T(8,128)(2,1)S(1)}, bf16[8,128,7,128]{1,0,3,2:T(8,128)(2,1)}, u32[]{:S(2)}) copy-start(bf16[8,128,7,128]{1,0,3,2:T(8,128)(2,1)} %copy-done.11) | copy-start | bytes 5505028
  125.7 1.5 copy-start.8
  125.7 2.0 %copy-start.15 = (bf16[896,1024]{1,0:T(8,128)(2,1)S(1)}, bf16[896,1024]{1,0:T(8,128)(2,1)}, u32[]{:S(2)}) copy-start(bf16[896,1024]{1,0:T(8,128)(2,1)} %param.10) | copy-start | bytes 5505028
  127.7 1.5 copy-start.6
  127.7 2.0 %copy-start.10 = (bf16[8,128,7,128]{1,0,3,2:T(8,128)(2,1)S(1)}, bf16[8,128,7,128]{1,0,3,2:T(8,128)(2,1)}, u32[]{:S(2)}) copy-start(bf16[8,128,7,128]{1,0,3,2:T(8,128)(2,1)} %copy-done.9) | copy-start | bytes 5505028
  132.6 30.6 %all-to-all-start.4 = ((bf16[4,128,2048]{2,1,0:T(8,128)(2,1)}), bf16[4,128,2048]{2,1,0:T(8,128)(2,1)}, u32[]{:S(2)}, u32[]{:S(2)}) async-start(bf16[4,128,2048]{2,1,0:T(8,128)(2,1)} %bitcast.87), calls=%async_computation.4 | async-start | bytes 4194304 | tf_op jit(solution)/shard_map/all_to_all | solution.py:50
  165.8 20.5 %all-to-all-start.5 = ((bf16[8,16,2048]{2,1,0:T(8,128)(2,1)}), bf16[8,16,2048]{2,1,0:T(8,128)(2,1)S(1)}, u32[]{:S(2)}, u32[]{:S(2)}) async-start(bf16[8,16,2048]{2,1,0:T(8,128)(2,1)} %bitcast.12), calls=%async_computation.5 | async-start | bytes 1048576 | tf_op jit(solution)/shard_map/all_to_all | solution.py:50
  174.2 1.6 copy-start.1

commit v9 on v7

--- a/solution.py
+++ b/solution.py
@@ -110,7 +110,7 @@
     out_partials = jnp.concatenate(
         [
             product(act_full, masked_down).astype(jnp.bfloat16),
-            (product_t(dgate_full, masked_gate) + product_t(dup_full, masked_up)).astype(
+            product_t(full[:, width:], jnp.concatenate([masked_gate, masked_up], axis=1)).astype(
                 jnp.bfloat16
             ),
         ],

time: 184 us -> 182 us (0.989)
  waiting for transfers between devices: 31.7 us -> 27.4 us
  other arithmetic: 5.86 us -> 8.2 us
    all_to_all x1, waiting for transfers between devices: 16 us -> 11.6 us  [gather_rows(): got = lax.all_to_all(sent, axis, 0, 0, tiled=False)]
    mul x0 -> x1, other arithmetic: none -> 2.31 us  [masked(): shaped * mask.astype(weight.dtype)[:, None, :, None]]
    dot_general x3 -> x2, matrix products: 5.53 us -> 3.45 us  [product_t(): lax.dot_general(left, weight, (((1,), (1,)), ((), ())), preferred_element...]
    unnamed x18 -> x22, local copies, waits for them, and re-layouts: 14.2 us -> 14.5 us
  transfers between devices with their start and end apart: 3 -> 3, of which waited for: 3 -> 3; matrix products, arithmetic and copies ran while one was open for 19% -> 21% of each run, Pallas kernels for 0% -> 0%
where the time goes in v9:
time: 182 us; the launch traced here: 181 us
  blocking collectives  83.5 us (46%)
  local copies, waits for them, and re-layouts  29.4 us (16%)
  waiting for transfers between devices  27.4 us (15%)
  matrix products  19.4 us (11%)
  starting transfers between devices  12.4 us (7%)
  other arithmetic  8.2 us (5%)
    all_to_all x2, blocking collectives, gather_rows(): got = lax.all_to_all(sent, axis, 0, 0, tiled=False)  44.5 us
    all_to_all x1, blocking collectives, reduce_row(): lax.all_to_all(got.astype(jnp.bfloat16), 'x', 0, 0, tiled=False)  21.9 us
    all_to_all x2, waiting for transfers between devices, reduce_rows(): got = lax.all_to_all(chunks, axis, 0, 0, tiled=False)  15.7 us
    unnamed x22, local copies, waits for them, and re-layouts  14.5 us
    mul x8, local copies, waits for them, and re-layouts, masked(): shaped * mask.astype(weight.dtype)[:, None, :, None]  11.8 us
    all_to_all x1, waiting for transfers between devices, gather_rows(): got = lax.all_to_all(sent, axis, 0, 0, tiled=False)  11.6 us
    dot_general x3, matrix products, contract_rows(): lax.dot_general(left, right, (((0,), (0,)), ((), ())), preferred_element_...  10.4 us
    all_to_all x1, blocking collectives, reduce_row(): got = add_blocks(lax.all_to_all(split, 'core', 0, 0, tiled=False))  9.05 us
  transfers between devices with their start and end apart: 3, of which 3 were waited for; matrix products, arithmetic and copies ran while one was open for 21% of the time, Pallas kernels for 0%

profile of v9, /device:TPU:1, one launch (start us, length us, event | category | flops | bytes accessed | tf_op | source)
XLA Modules:
  0.0 181.2 jit_solution(17049648620874589524)
XLA Ops:
  0.6 0.8 pad_maximum_fusion.3
  1.5 24.9 %all_to_all.40 = bf16[8,16,2048]{2,1,0:T(8,128)(2,1)S(1)} all-to-all(bf16[8,16,2048]{2,1,0:T(8,128)(2,1)S(1)} %broadcast_in_dim.10), channel_id=1, replica_groups=mesh['x'=4,'core'=2,'y'=4,'z'=8] {'z'}, dimensions={0} | all-to-all | bytes 1048576 | tf_op jit(solution)/shard_map/all_to_all | solution.py:43
  26.4 1.6 broadcast_in_dim.12
  28.0 4.3 %all-to-all-start.1 = ((bf16[4,128,2048]{2,1,0:T(8,128)(2,1)}), bf16[4,128,2048]{2,1,0:T(8,128)(2,1)S(1)}, u32[]{:S(2)}, u32[]{:S(2)}) async-start(bf16[4,128,2048]{2,1,0:T(8,128)(2,1)} %broadcast_in_dim.12), calls=%async_computation.1 | async-start | bytes 4194304 | tf_op jit(solution)/shard_map/all_to_all | solution.py:43
  32.6 3.8 %copy.14 = bf16[1024,896]{0,1:T(8,128)(2,1)} copy(bf16[1024,896]{1,0:T(8,128)(2,1)} %param.8) | data formatting | bytes 3670016 | tf_op args[2]
  36.4 3.8 %copy.16 = bf16[1024,896]{0,1:T(8,128)(2,1)} copy(bf16[1024,896]{1,0:T(8,128)(2,1)} %param.9) | data formatting | bytes 3670016 | tf_op args[3]
  40.8 0.9 copy-done.3
  42.2 2.3 %bitcast_multiply_fusion.2 = (bf16[1024,896]{0,1:T(8,128)(2,1)}, bf16[1024,896]{0,1:T(8,128)(2,1)}) fusion(bf16[1024,896]{0,1:T(8,128)(2,1)S(1)} %copy-done.4, bf16[112,8,8,128]{3,2,1,0:T(8,128)(2,1)S(1)} %bitcast.85, bf16[1024,896]{0,1:T(8,128)(2,1)S(1)} %copy-done.3, bf16[112,8,8,128]{3,2,1,0:T(8,128)(2,1)S(1)} %bitcast.86), kind=kLoop, calls=%fused_computation.14 | loop fusion | flops 1835008 | bytes 11010048 | tf_op jit(solution)/shard_map/mul | solution.py:14
  44.5 11.6 %all-to-all-done.1 = bf16[4,128,2048]{2,1,0:T(8,128)(2,1)S(1)} async-done(((bf16[4,128,2048]{2,1,0:T(8,128)(2,1)}), bf16[4,128,2048]{2,1,0:T(8,128)(2,1)S(1)}, u32[]{:S(2)}, u32[]{:S(2)}) %all-to-all-start.1) | async-done | bytes 2097184 | tf_op jit(solution)/shard_map/all_to_all | solution.py:43
  56.1 2.9 %convolution_convert_fusion.2 = bf16[512,896]{1,0:T(8,128)(2,1)S(1)} fusion(bf16[1024,896]{0,1:T(8,128)(2,1)} %get-tuple-element.16, bf16[512,2048]{1,0:T(8,128)(2,1)S(1)} %bitcast.73), kind=kOutput, calls=%fused_computation.20 | convolution fusion | flops 939982848 | bytes 3801088 | tf_op jit(solution)/shard_map/dot_general | solution.py:18
  59.1 1.3 convolution_convert_fusion.3
  60.7 1.4 convolution_convert_fusion.1
  62.3 9.0 %all_to_all.41 = bf16[2,4,64,2688]{3,2,1,0:T(8,128)(2,1)S(1)} all-to-all(bf16[2,4,64,2688]{3,2,1,0:T(8,128)(2,1)S(1)} %bitcast.72), channel_id=1, replica_groups=mesh['x'=4,'core'=2,'y'=4,'z'=8] {'core'}, dimensions={0} | all-to-all | bytes 5505024 | tf_op jit(solution)/shard_map/all_to_all | solution.py:67
  71.6 21.9 %all_to_all.42 = bf16[4,64,2688]{2,1,0:T(8,128)(2,1)S(1)} all-to-all(bf16[4,64,2688]{2,1,0:T(8,128)(2,1)S(1)} %fusion.11), channel_id=1, replica_groups=mesh['x'=4,'core'=2,'y'=4,'z'=8] {'x'}, dimensions={0} | all-to-all | bytes 2752512 | tf_op jit(solution)/shard_map/all_to_all | solution.py:68
  93.9 19.6 %all_to_all.43 = bf16[4,64,2688]{2,1,0:T(8,128)(2,1)S(1)} all-to-all(bf16[4,64,2688]{2,1,0:T(8,128)(2,1)S(1)} %broadcast_in_dim.13), channel_id=1, replica_groups=mesh['x'=4,'core'=2,'y'=4,'z'=8] {'x'}, dimensions={0} | all-to-all | bytes 2752512 | tf_op jit(solution)/shard_map/all_to_all | solution.py:43
  113.8 8.1 %all_to_all.44 = bf16[2,4,64,2688]{3,2,1,0:T(8,128)(2,1)S(1)} all-to-all(bf16[2,4,64,2688]{3,2,1,0:T(8,128)(2,1)S(1)} %broadcast_in_dim.14), channel_id=1, replica_groups=mesh['x'=4,'core'=2,'y'=4,'z'=8] {'core'}, dimensions={0} | all-to-all | bytes 5505024 | tf_op jit(solution)/shard_map/all_to_all | solution.py:76
  121.9 2.1 %fusion.6 = bf16[512,1024]{1,0:T(8,128)(2,1)S(1)} fusion(bf16[1024,896]{0,1:T(8,128)(2,1)S(1)} %copy-done.5, bf16[1024,896]{0,1:T(8,128)(2,1)S(1)} %copy-done.6, bf16[512,2688]{1,0:T(8,128)(2,1)S(1)} %bitcast.80), kind=kOutput, calls=%fused_computation.18 | convolution fusion | flops 1886912512 | bytes 6553600 | tf_op jit(solution)/shard_map/dot_general | solution.py:22
  124.0 1.3 convolution_convert_fusion
  125.3 1.5 pad_maximum_fusion.1
  126.8 4.6 %all-to-all-start.6 = ((bf16[4,128,2048]{2,1,0:T(8,128)(2,1)}), bf16[4,128,2048]{2,1,0:T(8,128)(2,1)}, u32[]{:S(2)}, u32[]{:S(2)}) async-start(bf16[4,128,2048]{2,1,0:T(8,128)(2,1)} %bitcast.79), calls=%async_computation.6 | async-start | bytes 4194304 | tf_op jit(solution)/shard_map/all_to_all | solution.py:50
  132.0 2.7 %copy.37 = f32[112,8,8,128]{3,1,2,0:T(8,128)} copy(f32[112,8,8,128]{3,2,1,0:T(8,128)S(1)} %bitcast.70) | data formatting | bytes 7340032
  134.7 5.0 %copy.21 = f32[1024,896]{1,0:T(8,128)} copy(f32[1024,896]{0,1:T(8,128)} %bitcast.68) | data formatting | bytes 7340032 | tf_op jit(solution)/shard_map/mul | solution.py:14
  140.0 2.8 %copy.38 = f32[112,8,8,128]{3,1,2,0:T(8,128)} copy(f32[112,8,8,128]{3,2,1,0:T(8,128)S(1)} %bitcast.71) | data formatting | bytes 7340032
  142.8 5.0 %copy.19 = f32[1024,896]{1,0:T(8,128)} copy(f32[1024,896]{0,1:T(8,128)} %bitcast.69) | data formatting | bytes 7340032 | tf_op jit(solution)/shard_map/mul | solution.py:14
  147.8 9.5 %all-to-all-done.6 = bf16[4,128,2048]{2,1,0:T(8,128)(2,1)} async-done(((bf16[4,128,2048]{2,1,0:T(8,128)(2,1)}), bf16[4,128,2048]{2,1,0:T(8,128)(2,1)}, u32[]{:S(2)}, u32[]{:S(2)}) %all-to-all-start.6) | async-done | bytes 2097184 | tf_op jit(solution)/shard_map/all_to_all | solution.py:50
  157.4 2.7 %add_convert_fusion.1 = bf16[1,128,2048]{2,1,0:T(8,128)(2,1)} fusion(bf16[4,128,2048]{2,1,0:T(8,128)(2,1)} %all-to-all-done.6), kind=kLoop, calls=%fused_computation.23 | loop fusion | flops 2097152 | bytes 2621440 | tf_op jit(solution)/shard_map/convert.4
  160.0 3.5 %all-to-all-start.7 = ((bf16[8,16,2048]{2,1,0:T(8,128)(2,1)}), bf16[8,16,2048]{2,1,0:T(8,128)(2,1)S(1)}, u32[]{:S(2)}, u32[]{:S(2)}) async-start(bf16[8,16,2048]{2,1,0:T(8,128)(2,1)} %bitcast.11), calls=%async_computation.7 | async-start | bytes 1048576 | tf_op jit(solution)/shard_map/all_to_all | solution.py:50
  163.6 5.0 %multiply_convert_fusion = bf16[1024,896]{1,0:T(8,128)(2,1)} fusion(f32[1024,896]{1,0:T(8,128)} %copy.21, bf16[512,2688]{1,0:T(8,128)(2,1)} %bitcast.82, bf16[512,2048]{1,0:T(8,128)(2,1)S(1)} %bitcast.76), kind=kOutput, calls=%fused_computation.8 | convolution fusion | flops 942276608 | bytes 7471104 | tf_op jit(solution)/shard_map/dot_general | solution.py:28
  168.6 2.6 %multiply_convert_fusion.1 = bf16[1024,896]{1,0:T(8,128)(2,1)} fusion(f32[1024,896]{1,0:T(8,128)S(1)} %copy-done, bf16[512,2688]{1,0:T(8,128)(2,1)S(1)} %bitcast.83, bf16[512,2048]{1,0:T(8,128)(2,1)S(1)} %bitcast.77), kind=kOutput, calls=%fused_computation.9 | convolution fusion | flops 942276608 | bytes 7471104 | tf_op jit(solution)/shard_map/dot_general | solution.py:28
  171.5 2.8 %fusion = bf16[896,1024]{1,0:T(8,128)(2,1)} fusion(f32[112,8,8,128]{3,2,1,0:T(8,128)S(1)} %bitcast.87, bf16[512,2048]{1,0:T(8,128)(2,1)S(1)} %bitcast.78, bf16[512,2688]{1,0:T(8,128)(2,1)S(1)} %bitcast.84), kind=kOutput, calls=%fused_computation.1 | convolution fusion | flops 942276608 | bytes 7471104 | tf_op jit(solution)/shard_map/dot_general | solution.py:28
  174.3 6.2 %all-to-all-done.7 = bf16[8,16,2048]{2,1,0:T(8,128)(2,1)S(1)} async-done(((bf16[8,16,2048]{2,1,0:T(8,128)(2,1)}), bf16[8,16,2048]{2,1,0:T(8,128)(2,1)S(1)}, u32[]{:S(2)}, u32[]{:S(2)}) %all-to-all-start.7) | async-done | bytes 524320 | tf_op jit(solution)/shard_map/all_to_all | solution.py:50
  180.6 0.6 fusion.27
  (39 shorter events, 4.2 us)
Async XLA Ops:
  28.0 4.3 %copy-start.7 = (s32[3,8,7]{2,1,0:T(8,128)S(1)}, s32[3,8,7]{2,1,0:T(8,128)}, u32[]{:S(2)}) copy-start(s32[3,8,7]{2,1,0:T(8,128)} %param.11) | copy-start | bytes 2020
  28.0 28.1 %all-to-all-start.1 = ((bf16[4,128,2048]{2,1,0:T(8,128)(2,1)}), bf16[4,128,2048]{2,1,0:T(8,128)(2,1)S(1)}, u32[]{:S(2)}, u32[]{:S(2)}) async-start(bf16[4,128,2048]{2,1,0:T(8,128)(2,1)} %broadcast_in_dim.12), calls=%async_computation.1 | async-start | bytes 4194304 | tf_op jit(solution)/shard_map/all_to_all | solution.py:43
  40.1 1.5 copy-start.3
  40.1 2.0 %copy-start.4 = (bf16[1024,896]{0,1:T(8,128)(2,1)S(1)}, bf16[1024,896]{0,1:T(8,128)(2,1)}, u32[]{:S(2)}) copy-start(bf16[1024,896]{0,1:T(8,128)(2,1)} %copy.16) | copy-start | bytes 5505028
  56.1 2.9 %copy-start.6 = (bf16[1024,896]{0,1:T(8,128)(2,1)S(1)}, bf16[1024,896]{0,1:T(8,128)(2,1)}, u32[]{:S(2)}) copy-start(bf16[1024,896]{0,1:T(8,128)(2,1)} %get-tuple-element.17) | copy-start | bytes 5505028
  59.0 1.6 copy-start.8
  113.8 8.1 %copy-start.5 = (bf16[1024,896]{0,1:T(8,128)(2,1)S(1)}, bf16[1024,896]{0,1:T(8,128)(2,1)}, u32[]{:S(2)}) copy-start(bf16[1024,896]{0,1:T(8,128)(2,1)} %get-tuple-element.16) | copy-start | bytes 5505028
  121.9 2.1 %copy-start.1 = (bf16[2,4,64,2688]{3,2,1,0:T(8,128)(2,1)}, bf16[2,4,64,2688]{3,2,1,0:T(8,128)(2,1)S(1)}, u32[]{:S(2)}) copy-start(bf16[2,4,64,2688]{3,2,1,0:T(8,128)(2,1)S(1)} %all_to_all.44) | copy-start | bytes 8257540
  126.8 30.6 %all-to-all-start.6 = ((bf16[4,128,2048]{2,1,0:T(8,128)(2,1)}), bf16[4,128,2048]{2,1,0:T(8,128)(2,1)}, u32[]{:S(2)}, u32[]{:S(2)}) async-start(bf16[4,128,2048]{2,1,0:T(8,128)(2,1)} %bitcast.79), calls=%async_computation.6 | async-start | bytes 4194304 | tf_op jit(solution)/shard_map/all_to_all | solution.py:50
  160.0 20.5 %all-to-all-start.7 = ((bf16[8,16,2048]{2,1,0:T(8,128)(2,1)}), bf16[8,16,2048]{2,1,0:T(8,128)(2,1)S(1)}, u32[]{:S(2)}, u32[]{:S(2)}) async-start(bf16[8,16,2048]{2,1,0:T(8,128)(2,1)} %bitcast.11), calls=%async_computation.7 | async-start | bytes 1048576 | tf_op jit(solution)/shard_map/all_to_all | solution.py:50
  163.5 5.0 %copy-start = (f32[1024,896]{1,0:T(8,128)S(1)}, f32[1024,896]{1,0:T(8,128)}, u32[]{:S(2)}) copy-start(f32[1024,896]{1,0:T(8,128)} %copy.19) | copy-start | bytes 11010052
  163.5 5.0 %copy-start.2 = (bf16[2,4,64,2688]{3,2,1,0:T(8,128)(2,1)S(1)}, bf16[2,4,64,2688]{3,2,1,0:T(8,128)(2,1)}, u32[]{:S(2)}) copy-start(bf16[2,4,64,2688]{3,2,1,0:T(8,128)(2,1)} %copy-done.1) | copy-start | bytes 8257540

commit v10 on v9

--- a/solution.py
+++ b/solution.py
@@ -81,6 +81,7 @@
     masked_gate = masked(gate_weight, block_mask[0])
     masked_up = masked(up_weight, block_mask[1])
     masked_down = masked(down_weight, block_mask[2].T)
+    gate_up = jnp.concatenate([masked_gate, masked_up], axis=1)
     feat = tokens.shape[1]
     both = gather_col(jnp.concatenate([tokens, cotangent], axis=1))
     panel = both[:, :feat]
@@ -89,8 +90,7 @@
     width = masked_gate.shape[1]
     partials = jnp.concatenate(
         [
-            product(panel, masked_gate).astype(jnp.bfloat16),
-            product(panel, masked_up).astype(jnp.bfloat16),
+            product(panel, gate_up).astype(jnp.bfloat16),
             product_t(grad_panel, masked_down).astype(jnp.bfloat16),
         ],
         axis=1,
@@ -110,7 +110,7 @@
     out_partials = jnp.concatenate(
         [
             product(act_full, masked_down).astype(jnp.bfloat16),
-            product_t(full[:, width:], jnp.concatenate([masked_gate, masked_up], axis=1)).astype(
+            product_t(full[:, width:], gate_up).astype(
                 jnp.bfloat16
             ),
         ],

time: 182 us -> 182 us (level)
    dot_general x3 -> x2, matrix products: 5.52 us -> 3.41 us  [product(): return jnp.dot(left, weight, preferred_element_type=jnp.float32)]
where the time goes in v10:
time: 182 us; the launch traced here: 181 us
  blocking collectives  83.4 us (46%)
  local copies, waits for them, and re-layouts  29.8 us (16%)
  waiting for transfers between devices  27.4 us (15%)
  matrix products  18.9 us (10%)
  starting transfers between devices  12.4 us (7%)
  other arithmetic  8.19 us (4%)
    all_to_all x2, blocking collectives, gather_rows(): got = lax.all_to_all(sent, axis, 0, 0, tiled=False)  44.5 us
    all_to_all x1, blocking collectives, reduce_row(): lax.all_to_all(got.astype(jnp.bfloat16), 'x', 0, 0, tiled=False)  21.9 us
    all_to_all x2, waiting for transfers between devices, reduce_rows(): got = lax.all_to_all(chunks, axis, 0, 0, tiled=False)  15.8 us
    unnamed x22, local copies, waits for them, and re-layouts  14.9 us
    mul x8, local copies, waits for them, and re-layouts, masked(): shaped * mask.astype(weight.dtype)[:, None, :, None]  11.8 us
    all_to_all x1, waiting for transfers between devices, gather_rows(): got = lax.all_to_all(sent, axis, 0, 0, tiled=False)  11.6 us
    dot_general x3, matrix products, contract_rows(): lax.dot_general(left, right, (((0,), (0,)), ((), ())), preferred_element_...  10.4 us
    all_to_all x1, blocking collectives, reduce_row(): got = add_blocks(lax.all_to_all(split, 'core', 0, 0, tiled=False))  9.04 us
  transfers between devices with their start and end apart: 3, of which 3 were waited for; matrix products, arithmetic and copies ran while one was open for 21% of the time, Pallas kernels for 0%

profile of v10, /device:TPU:1, one launch (start us, length us, event | category | flops | bytes accessed | tf_op | source)
XLA Modules:
  0.0 180.9 jit_solution(13711154392889082169)
XLA Ops:
  0.6 0.8 pad_maximum_fusion.8
  1.5 24.9 %all_to_all.40 = bf16[8,16,2048]{2,1,0:T(8,128)(2,1)S(1)} all-to-all(bf16[8,16,2048]{2,1,0:T(8,128)(2,1)S(1)} %broadcast_in_dim.10), channel_id=1, replica_groups=mesh['x'=4,'core'=2,'y'=4,'z'=8] {'z'}, dimensions={0} | all-to-all | bytes 1048576 | tf_op jit(solution)/shard_map/all_to_all | solution.py:43
  26.4 1.6 broadcast_in_dim.12
  28.0 4.3 %all-to-all-start.1 = ((bf16[4,128,2048]{2,1,0:T(8,128)(2,1)}), bf16[4,128,2048]{2,1,0:T(8,128)(2,1)S(1)}, u32[]{:S(2)}, u32[]{:S(2)}) async-start(bf16[4,128,2048]{2,1,0:T(8,128)(2,1)} %broadcast_in_dim.12), calls=%async_computation.1 | async-start | bytes 4194304 | tf_op jit(solution)/shard_map/all_to_all | solution.py:43
  32.6 3.8 %copy.14 = bf16[1024,896]{0,1:T(8,128)(2,1)} copy(bf16[1024,896]{1,0:T(8,128)(2,1)} %param.8) | data formatting | bytes 3670016 | tf_op args[2]
  36.4 3.8 %copy.16 = bf16[1024,896]{0,1:T(8,128)(2,1)} copy(bf16[1024,896]{1,0:T(8,128)(2,1)} %param.9) | data formatting | bytes 3670016 | tf_op args[3]
  40.8 0.9 copy-done.3
  41.6 0.6 copy-done.4
  42.2 2.3 %bitcast_multiply_fusion.2 = (bf16[1024,896]{0,1:T(8,128)(2,1)}, bf16[1024,896]{0,1:T(8,128)(2,1)}) fusion(bf16[1024,896]{0,1:T(8,128)(2,1)S(1)} %copy-done.4, bf16[112,8,8,128]{3,2,1,0:T(8,128)(2,1)S(1)} %bitcast.82, bf16[1024,896]{0,1:T(8,128)(2,1)S(1)} %copy-done.3, bf16[112,8,8,128]{3,2,1,0:T(8,128)(2,1)S(1)} %bitcast.83), kind=kLoop, calls=%fused_computation.13 | loop fusion | flops 1835008 | bytes 11010048 | tf_op jit(solution)/shard_map/mul | solution.py:14
  44.5 11.6 %all-to-all-done.1 = bf16[4,128,2048]{2,1,0:T(8,128)(2,1)S(1)} async-done(((bf16[4,128,2048]{2,1,0:T(8,128)(2,1)}), bf16[4,128,2048]{2,1,0:T(8,128)(2,1)S(1)}, u32[]{:S(2)}, u32[]{:S(2)}) %all-to-all-start.1) | async-done | bytes 2097184 | tf_op jit(solution)/shard_map/all_to_all | solution.py:43
  56.4 3.0 %convolution_convert_fusion.2 = bf16[512,896]{1,0:T(8,128)(2,1)S(1)} fusion(bf16[512,2048]{1,0:T(8,128)(2,1)S(1)} %bitcast.71, bf16[896,1024]{1,0:T(8,128)(2,1)} %param.10, bf16[112,8,8,128]{3,2,1,0:T(8,128)(2,1)S(1)} %bitcast.86), kind=kOutput, calls=%fused_computation.18 | convolution fusion | flops 940900352 | bytes 5636096 | tf_op jit(solution)/shard_map/dot_general | solution.py:22
  59.4 2.1 %convolution_convert_fusion = bf16[512,1792]{1,0:T(8,128)(2,1)S(1)} fusion(bf16[1024,896]{0,1:T(8,128)(2,1)S(1)} %copy-done.5, bf16[1024,896]{0,1:T(8,128)(2,1)S(1)} %copy-done.6, bf16[512,2048]{1,0:T(8,128)(2,1)S(1)} %bitcast.72), kind=kOutput, calls=%fused_computation.7 | convolution fusion | flops 1887305728 | bytes 6553600 | tf_op jit(solution)/shard_map/dot_general | solution.py:18
  61.7 9.0 %all_to_all.41 = bf16[2,4,64,2688]{3,2,1,0:T(8,128)(2,1)S(1)} all-to-all(bf16[2,4,64,2688]{3,2,1,0:T(8,128)(2,1)S(1)} %bitcast.70), channel_id=1, replica_groups=mesh['x'=4,'core'=2,'y'=4,'z'=8] {'core'}, dimensions={0} | all-to-all | bytes 5505024 | tf_op jit(solution)/shard_map/all_to_all | solution.py:67
  71.1 21.9 %all_to_all.42 = bf16[4,64,2688]{2,1,0:T(8,128)(2,1)S(1)} all-to-all(bf16[4,64,2688]{2,1,0:T(8,128)(2,1)S(1)} %fusion.6), channel_id=1, replica_groups=mesh['x'=4,'core'=2,'y'=4,'z'=8] {'x'}, dimensions={0} | all-to-all | bytes 2752512 | tf_op jit(solution)/shard_map/all_to_all | solution.py:68
  93.4 19.6 %all_to_all.43 = bf16[4,64,2688]{2,1,0:T(8,128)(2,1)S(1)} all-to-all(bf16[4,64,2688]{2,1,0:T(8,128)(2,1)S(1)} %broadcast_in_dim.13), channel_id=1, replica_groups=mesh['x'=4,'core'=2,'y'=4,'z'=8] {'x'}, dimensions={0} | all-to-all | bytes 2752512 | tf_op jit(solution)/shard_map/all_to_all | solution.py:43
  113.2 7.9 %all_to_all.44 = bf16[2,4,64,2688]{3,2,1,0:T(8,128)(2,1)S(1)} all-to-all(bf16[2,4,64,2688]{3,2,1,0:T(8,128)(2,1)S(1)} %broadcast_in_dim.14), channel_id=1, replica_groups=mesh['x'=4,'core'=2,'y'=4,'z'=8] {'core'}, dimensions={0} | all-to-all | bytes 5505024 | tf_op jit(solution)/shard_map/all_to_all | solution.py:76
  121.2 2.1 %fusion.3 = bf16[512,1024]{1,0:T(8,128)(2,1)S(1)} fusion(bf16[1024,896]{0,1:T(8,128)(2,1)S(1)} %copy-done.5, bf16[1024,896]{0,1:T(8,128)(2,1)S(1)} %copy-done.6, bf16[512,2688]{1,0:T(8,128)(2,1)S(1)} %bitcast.77), kind=kOutput, calls=%fused_computation.17 | convolution fusion | flops 1886912512 | bytes 6553600 | tf_op jit(solution)/shard_map/dot_general | solution.py:22
  123.7 1.3 convolution_convert_fusion.1
  125.0 1.5 pad_maximum_fusion.4
  126.5 4.6 %all-to-all-start.6 = ((bf16[4,128,2048]{2,1,0:T(8,128)(2,1)}), bf16[4,128,2048]{2,1,0:T(8,128)(2,1)}, u32[]{:S(2)}, u32[]{:S(2)}) async-start(bf16[4,128,2048]{2,1,0:T(8,128)(2,1)} %bitcast.76), calls=%async_computation.6 | async-start | bytes 4194304 | tf_op jit(solution)/shard_map/all_to_all | solution.py:50
  131.7 2.7 %copy.37 = f32[112,8,8,128]{3,1,2,0:T(8,128)} copy(f32[112,8,8,128]{3,2,1,0:T(8,128)S(1)} %bitcast.68) | data formatting | bytes 7340032
  134.4 5.0 %copy.21 = f32[1024,896]{1,0:T(8,128)} copy(f32[1024,896]{0,1:T(8,128)} %bitcast.66) | data formatting | bytes 7340032 | tf_op jit(solution)/shard_map/mul | solution.py:14
  139.7 2.8 %copy.38 = f32[112,8,8,128]{3,1,2,0:T(8,128)} copy(f32[112,8,8,128]{3,2,1,0:T(8,128)S(1)} %bitcast.69) | data formatting | bytes 7340032
  142.5 5.0 %copy.19 = f32[1024,896]{1,0:T(8,128)} copy(f32[1024,896]{0,1:T(8,128)} %bitcast.67) | data formatting | bytes 7340032 | tf_op jit(solution)/shard_map/mul | solution.py:14
  147.5 9.5 %all-to-all-done.6 = bf16[4,128,2048]{2,1,0:T(8,128)(2,1)} async-done(((bf16[4,128,2048]{2,1,0:T(8,128)(2,1)}), bf16[4,128,2048]{2,1,0:T(8,128)(2,1)}, u32[]{:S(2)}, u32[]{:S(2)}) %all-to-all-start.6) | async-done | bytes 2097184 | tf_op jit(solution)/shard_map/all_to_all | solution.py:50
  157.1 2.7 %add_convert_fusion.1 = bf16[1,128,2048]{2,1,0:T(8,128)(2,1)} fusion(bf16[4,128,2048]{2,1,0:T(8,128)(2,1)} %all-to-all-done.6), kind=kLoop, calls=%fused_computation.20 | loop fusion | flops 2097152 | bytes 2621440 | tf_op jit(solution)/shard_map/convert.4
  159.7 3.5 %all-to-all-start.7 = ((bf16[8,16,2048]{2,1,0:T(8,128)(2,1)}), bf16[8,16,2048]{2,1,0:T(8,128)(2,1)S(1)}, u32[]{:S(2)}, u32[]{:S(2)}) async-start(bf16[8,16,2048]{2,1,0:T(8,128)(2,1)} %bitcast.11), calls=%async_computation.7 | async-start | bytes 1048576 | tf_op jit(solution)/shard_map/all_to_all | solution.py:50
  163.3 5.0 %multiply_convert_fusion = bf16[1024,896]{1,0:T(8,128)(2,1)} fusion(f32[1024,896]{1,0:T(8,128)} %copy.21, bf16[512,2688]{1,0:T(8,128)(2,1)} %bitcast.79, bf16[512,2048]{1,0:T(8,128)(2,1)S(1)} %bitcast.73), kind=kOutput, calls=%fused_computation.5 | convolution fusion | flops 942276608 | bytes 7471104 | tf_op jit(solution)/shard_map/dot_general | solution.py:28
  168.3 2.6 %multiply_convert_fusion.1 = bf16[1024,896]{1,0:T(8,128)(2,1)} fusion(f32[1024,896]{1,0:T(8,128)S(1)} %copy-done, bf16[512,2688]{1,0:T(8,128)(2,1)S(1)} %bitcast.80, bf16[512,2048]{1,0:T(8,128)(2,1)S(1)} %bitcast.74), kind=kOutput, calls=%fused_computation.6 | convolution fusion | flops 942276608 | bytes 7471104 | tf_op jit(solution)/shard_map/dot_general | solution.py:28
  171.2 2.8 %fusion = bf16[896,1024]{1,0:T(8,128)(2,1)} fusion(f32[112,8,8,128]{3,2,1,0:T(8,128)S(1)} %bitcast.84, bf16[512,2048]{1,0:T(8,128)(2,1)S(1)} %bitcast.75, bf16[512,2688]{1,0:T(8,128)(2,1)S(1)} %bitcast.81), kind=kOutput, calls=%fused_computation.1 | convolution fusion | flops 942276608 | bytes 7471104 | tf_op jit(solution)/shard_map/dot_general | solution.py:28
  174.0 6.2 %all-to-all-done.7 = bf16[8,16,2048]{2,1,0:T(8,128)(2,1)S(1)} async-done(((bf16[8,16,2048]{2,1,0:T(8,128)(2,1)}), bf16[8,16,2048]{2,1,0:T(8,128)(2,1)S(1)}, u32[]{:S(2)}, u32[]{:S(2)}) %all-to-all-start.7) | async-done | bytes 524320 | tf_op jit(solution)/shard_map/all_to_all | solution.py:50
  180.3 0.6 fusion.22
  (38 shorter events, 4.0 us)
Async XLA Ops:
  28.0 4.3 %copy-start.7 = (s32[3,8,7]{2,1,0:T(8,128)S(1)}, s32[3,8,7]{2,1,0:T(8,128)}, u32[]{:S(2)}) copy-start(s32[3,8,7]{2,1,0:T(8,128)} %param.11) | copy-start | bytes 2020
  28.0 28.1 %all-to-all-start.1 = ((bf16[4,128,2048]{2,1,0:T(8,128)(2,1)}), bf16[4,128,2048]{2,1,0:T(8,128)(2,1)S(1)}, u32[]{:S(2)}, u32[]{:S(2)}) async-start(bf16[4,128,2048]{2,1,0:T(8,128)(2,1)} %broadcast_in_dim.12), calls=%async_computation.1 | async-start | bytes 4194304 | tf_op jit(solution)/shard_map/all_to_all | solution.py:43
  40.1 1.5 copy-start.3
  40.1 2.0 %copy-start.4 = (bf16[1024,896]{0,1:T(8,128)(2,1)S(1)}, bf16[1024,896]{0,1:T(8,128)(2,1)}, u32[]{:S(2)}) copy-start(bf16[1024,896]{0,1:T(8,128)(2,1)} %copy.16) | copy-start | bytes 5505028
  56.4 3.0 %copy-start.5 = (bf16[1024,896]{0,1:T(8,128)(2,1)S(1)}, bf16[1024,896]{0,1:T(8,128)(2,1)}, u32[]{:S(2)}) copy-start(bf16[1024,896]{0,1:T(8,128)(2,1)} %get-tuple-element.16) | copy-start | bytes 5505028
  56.4 3.0 %copy-start.6 = (bf16[1024,896]{0,1:T(8,128)(2,1)S(1)}, bf16[1024,896]{0,1:T(8,128)(2,1)}, u32[]{:S(2)}) copy-start(bf16[1024,896]{0,1:T(8,128)(2,1)} %get-tuple-element.17) | copy-start | bytes 5505028
  121.2 2.1 %copy-start.1 = (bf16[2,4,64,2688]{3,2,1,0:T(8,128)(2,1)}, bf16[2,4,64,2688]{3,2,1,0:T(8,128)(2,1)S(1)}, u32[]{:S(2)}) copy-start(bf16[2,4,64,2688]{3,2,1,0:T(8,128)(2,1)S(1)} %all_to_all.44) | copy-start | bytes 8257540
  121.2 2.5 %copy-start.8 = (bf16[896,1024]{1,0:T(8,128)(2,1)S(1)}, bf16[896,1024]{1,0:T(8,128)(2,1)}, u32[]{:S(2)}) copy-start(bf16[896,1024]{1,0:T(8,128)(2,1)} %param.10) | copy-start | bytes 5505028
  126.5 30.6 %all-to-all-start.6 = ((bf16[4,128,2048]{2,1,0:T(8,128)(2,1)}), bf16[4,128,2048]{2,1,0:T(8,128)(2,1)}, u32[]{:S(2)}, u32[]{:S(2)}) async-start(bf16[4,128,2048]{2,1,0:T(8,128)(2,1)} %bitcast.76), calls=%async_computation.6 | async-start | bytes 4194304 | tf_op jit(solution)/shard_map/all_to_all | solution.py:50
  159.7 20.5 %all-to-all-start.7 = ((bf16[8,16,2048]{2,1,0:T(8,128)(2,1)}), bf16[8,16,2048]{2,1,0:T(8,128)(2,1)S(1)}, u32[]{:S(2)}, u32[]{:S(2)}) async-start(bf16[8,16,2048]{2,1,0:T(8,128)(2,1)} %bitcast.11), calls=%async_computation.7 | async-start | bytes 1048576 | tf_op jit(solution)/shard_map/all_to_all | solution.py:50
  163.2 5.0 %copy-start = (f32[1024,896]{1,0:T(8,128)S(1)}, f32[1024,896]{1,0:T(8,128)}, u32[]{:S(2)}) copy-start(f32[1024,896]{1,0:T(8,128)} %copy.19) | copy-start | bytes 11010052
  163.3 5.0 %copy-start.2 = (bf16[2,4,64,2688]{3,2,1,0:T(8,128)(2,1)S(1)}, bf16[2,4,64,2688]{3,2,1,0:T(8,128)(2,1)}, u32[]{:S(2)}) copy-start(bf16[2,4,64,2688]{3,2,1,0:T(8,128)(2,1)} %copy-done.1) | copy-start | bytes 8257540

commit v11 on v9

--- a/solution.py
+++ b/solution.py
@@ -51,8 +51,18 @@
     return add_blocks(got)
 
 
+def permute_gather(local, axis):
+    size = lax.axis_size(axis)
+    me = lax.axis_index(axis)
+    got = [local] + [
+        lax.ppermute(local, axis, [(i, (i + k) % size) for i in range(size)]) for k in range(1, size)
+    ]
+    order = (me - jnp.arange(size)) % size
+    return jnp.take(jnp.stack(got), order, axis=0).reshape((size * local.shape[0],) + local.shape[1:])
+
+
 def gather_col(local):
-    return gather_rows(gather_rows(local, "z"), "y")
+    return gather_rows(permute_gather(local, "z"), "y")
 
 
 def reduce_col(partial):

time: 182 us -> 188 us (1.033)
  blocking collectives: 83.5 us -> 60.4 us
  waiting for transfers between devices: 27.4 us -> 41.9 us
  starting transfers between devices: 12.4 us -> 25.6 us
  local copies, waits for them, and re-layouts: 29.4 us -> 31.7 us
    all_to_all x2 -> x1, blocking collectives: 44.5 us -> 19.6 us  [gather_rows(): got = lax.all_to_all(sent, axis, 0, 0, tiled=False)]
    ppermute x0 -> x7, waiting for transfers between devices: none -> 16.2 us  [permute_gather(): lax.ppermute(local, axis, [(i, (i + k) % size) for i in range(size)])]
    ppermute x0 -> x7, starting transfers between devices: none -> 13.2 us  [permute_gather(): lax.ppermute(local, axis, [(i, (i + k) % size) for i in range(size)])]
    unnamed x22 -> x30, local copies, waits for them, and re-layouts: 14.5 us -> 15.3 us
  transfers between devices with their start and end apart: 3 -> 10, of which waited for: 3 -> 6; matrix products, arithmetic and copies ran while one was open for 21% -> 20% of each run, Pallas kernels for 0% -> 0%
where the time goes in v11:
time: 188 us; the launch traced here: 187 us
  blocking collectives  60.4 us (32%)
  waiting for transfers between devices  41.9 us (22%)
  local copies, waits for them, and re-layouts  31.7 us (17%)
  starting transfers between devices  25.6 us (14%)
  matrix products  19.4 us (10%)
  other arithmetic  7.54 us (4%)
    all_to_all x1, blocking collectives, reduce_row(): lax.all_to_all(got.astype(jnp.bfloat16), 'x', 0, 0, tiled=False)  21.9 us
    all_to_all x1, blocking collectives, gather_rows(): got = lax.all_to_all(sent, axis, 0, 0, tiled=False)  19.6 us
    ppermute x7, waiting for transfers between devices, permute_gather(): lax.ppermute(local, axis, [(i, (i + k) % size) for i in range(size)])  16.2 us
    all_to_all x2, waiting for transfers between devices, reduce_rows(): got = lax.all_to_all(chunks, axis, 0, 0, tiled=False)  15.9 us
    unnamed x30, local copies, waits for them, and re-layouts  15.3 us
    ppermute x7, starting transfers between devices, permute_gather(): lax.ppermute(local, axis, [(i, (i + k) % size) for i in range(size)])  13.2 us
    mul x8, local copies, waits for them, and re-layouts, masked(): shaped * mask.astype(weight.dtype)[:, None, :, None]  11.8 us
    all_to_all x1, blocking collectives, reduce_row(): got = add_blocks(lax.all_to_all(split, 'core', 0, 0, tiled=False))  10.9 us
  transfers between devices with their start and end apart: 10, of which 6 were waited for; matrix products, arithmetic and copies ran while one was open for 20% of the time, Pallas kernels for 0%

profile of v11, /device:TPU:1, one launch (start us, length us, event | category | flops | bytes accessed | tf_op | source)
XLA Modules:
  0.0 187.5 jit_solution(17903464614578485797)
XLA Ops:
  2.2 6.4 %collective-permute-start.6 = (bf16[16,2048]{1,0:T(8,128)(2,1)S(1)}, bf16[16,2048]{1,0:T(8,128)(2,1)S(1)}, u32[]{:S(2)}, u32[]{:S(2)}) collective-permute-start(bf16[16,2048]{1,0:T(8,128)(2,1)S(1)} %constant_dynamic-update-slice_fusion), channel_id=1, source_target_pairs={{0,7},{1,0},{2,1},{3,2},{4,3},{5,4},{6,5},{7,6},{8,15},{9,8},{10,9... | collective-permute-start | bytes 196616 | tf_op jit(solution)/shard_map/ppermute | solution.py:58
  10.2 4.5 %collective-permute-start.3 = (bf16[16,2048]{1,0:T(8,128)(2,1)S(1)}, bf16[16,2048]{1,0:T(8,128)(2,1)S(1)}, u32[]{:S(2)}, u32[]{:S(2)}) collective-permute-start(bf16[16,2048]{1,0:T(8,128)(2,1)S(1)} %constant_dynamic-update-slice_fusion), channel_id=1, source_target_pairs={{0,4},{1,5},{2,6},{3,7},{4,0},{5,1},{6,2},{7,3},{8,12},{9,13},{10,... | collective-permute-start | bytes 196616 | tf_op jit(solution)/shard_map/ppermute | solution.py:58
  15.6 4.7 %collective-permute-done = bf16[16,2048]{1,0:T(8,128)(2,1)S(1)} collective-permute-done((bf16[16,2048]{1,0:T(8,128)(2,1)S(1)}, bf16[16,2048]{1,0:T(8,128)(2,1)S(1)}, u32[]{:S(2)}, u32[]{:S(2)}) %collective-permute-start) | collective-permute-done | bytes 65568 | tf_op jit(solution)/shard_map/ppermute | solution.py:58
  20.4 5.2 %collective-permute-done.1 = bf16[16,2048]{1,0:T(8,128)(2,1)S(1)} collective-permute-done((bf16[16,2048]{1,0:T(8,128)(2,1)S(1)}, bf16[16,2048]{1,0:T(8,128)(2,1)S(1)}, u32[]{:S(2)}, u32[]{:S(2)}) %collective-permute-start.1) | collective-permute-done | bytes 65568 | tf_op jit(solution)/shard_map/ppermute | solution.py:58
  25.6 6.2 %collective-permute-done.2 = bf16[16,2048]{1,0:T(8,128)(2,1)S(1)} collective-permute-done((bf16[16,2048]{1,0:T(8,128)(2,1)S(1)}, bf16[16,2048]{1,0:T(8,128)(2,1)S(1)}, u32[]{:S(2)}, u32[]{:S(2)}) %collective-permute-start.2) | collective-permute-done | bytes 65568 | tf_op jit(solution)/shard_map/ppermute | solution.py:58
  32.6 1.6 broadcast_in_dim.40
  34.2 4.4 %all-to-all-start = ((bf16[4,128,2048]{2,1,0:T(8,128)(2,1)}), bf16[4,128,2048]{2,1,0:T(8,128)(2,1)S(1)}, u32[]{:S(2)}, u32[]{:S(2)}) async-start(bf16[4,128,2048]{2,1,0:T(8,128)(2,1)} %broadcast_in_dim.40), calls=%async_computation | async-start | bytes 4194304 | tf_op jit(solution)/shard_map/all_to_all | solution.py:43
  38.9 3.8 %copy.14 = bf16[1024,896]{0,1:T(8,128)(2,1)} copy(bf16[1024,896]{1,0:T(8,128)(2,1)} %param.8) | data formatting | bytes 3670016 | tf_op args[2]
  42.7 3.8 %copy.16 = bf16[1024,896]{0,1:T(8,128)(2,1)} copy(bf16[1024,896]{1,0:T(8,128)(2,1)} %param.9) | data formatting | bytes 3670016 | tf_op args[3]
  48.5 2.3 %bitcast_multiply_fusion.2 = (bf16[1024,896]{0,1:T(8,128)(2,1)}, bf16[1024,896]{0,1:T(8,128)(2,1)}) fusion(bf16[1024,896]{0,1:T(8,128)(2,1)S(1)} %copy-done.4, bf16[112,8,8,128]{3,2,1,0:T(8,128)(2,1)S(1)} %bitcast.104, bf16[1024,896]{0,1:T(8,128)(2,1)S(1)} %copy-done.3, bf16[112,8,8,128]{3,2,1,0:T(8,128)(2,1)S(1)} %bitcast.105), kind=kLoop, calls=%fused_computation.15 | loop fusion | flops 1835008 | bytes 11010048 | tf_op jit(solution)/shard_map/mul | solution.py:14
  50.8 9.8 %all-to-all-done = bf16[4,128,2048]{2,1,0:T(8,128)(2,1)S(1)} async-done(((bf16[4,128,2048]{2,1,0:T(8,128)(2,1)}), bf16[4,128,2048]{2,1,0:T(8,128)(2,1)S(1)}, u32[]{:S(2)}, u32[]{:S(2)}) %all-to-all-start) | async-done | bytes 2097184 | tf_op jit(solution)/shard_map/all_to_all | solution.py:43
  60.6 2.9 %convolution_convert_fusion.2 = bf16[512,896]{1,0:T(8,128)(2,1)S(1)} fusion(bf16[1024,896]{0,1:T(8,128)(2,1)} %get-tuple-element.16, bf16[512,2048]{1,0:T(8,128)(2,1)S(1)} %bitcast.92), kind=kOutput, calls=%fused_computation.21 | convolution fusion | flops 939982848 | bytes 3801088 | tf_op jit(solution)/shard_map/dot_general | solution.py:18
  63.5 1.3 convolution_convert_fusion.3
  65.2 1.4 convolution_convert_fusion.1
  66.7 10.9 %all_to_all.35 = bf16[2,4,64,2688]{3,2,1,0:T(8,128)(2,1)S(1)} all-to-all(bf16[2,4,64,2688]{3,2,1,0:T(8,128)(2,1)S(1)} %bitcast.91), channel_id=1, replica_groups=mesh['x'=4,'core'=2,'y'=4,'z'=8] {'core'}, dimensions={0} | all-to-all | bytes 5505024 | tf_op jit(solution)/shard_map/all_to_all | solution.py:77
  78.0 21.9 %all_to_all.36 = bf16[4,64,2688]{2,1,0:T(8,128)(2,1)S(1)} all-to-all(bf16[4,64,2688]{2,1,0:T(8,128)(2,1)S(1)} %fusion.11), channel_id=1, replica_groups=mesh['x'=4,'core'=2,'y'=4,'z'=8] {'x'}, dimensions={0} | all-to-all | bytes 2752512 | tf_op jit(solution)/shard_map/all_to_all | solution.py:78
  100.3 19.6 %all_to_all.37 = bf16[4,64,2688]{2,1,0:T(8,128)(2,1)S(1)} all-to-all(bf16[4,64,2688]{2,1,0:T(8,128)(2,1)S(1)} %broadcast_in_dim.41), channel_id=1, replica_groups=mesh['x'=4,'core'=2,'y'=4,'z'=8] {'x'}, dimensions={0} | all-to-all | bytes 2752512 | tf_op jit(solution)/shard_map/all_to_all | solution.py:43
  120.1 8.1 %all_to_all.38 = bf16[2,4,64,2688]{3,2,1,0:T(8,128)(2,1)S(1)} all-to-all(bf16[2,4,64,2688]{3,2,1,0:T(8,128)(2,1)S(1)} %broadcast_in_dim.42), channel_id=1, replica_groups=mesh['x'=4,'core'=2,'y'=4,'z'=8] {'core'}, dimensions={0} | all-to-all | bytes 5505024 | tf_op jit(solution)/shard_map/all_to_all | solution.py:86
  128.2 2.1 %fusion.6 = bf16[512,1024]{1,0:T(8,128)(2,1)S(1)} fusion(bf16[1024,896]{0,1:T(8,128)(2,1)S(1)} %copy-done.5, bf16[1024,896]{0,1:T(8,128)(2,1)S(1)} %copy-done.6, bf16[512,2688]{1,0:T(8,128)(2,1)S(1)} %bitcast.99), kind=kOutput, calls=%fused_computation.19 | convolution fusion | flops 1886912512 | bytes 6553600 | tf_op jit(solution)/shard_map/dot_general | solution.py:22
  131.6 1.5 pad_maximum_fusion.1
  133.1 4.4 %all-to-all-start.5 = ((bf16[4,128,2048]{2,1,0:T(8,128)(2,1)}), bf16[4,128,2048]{2,1,0:T(8,128)(2,1)}, u32[]{:S(2)}, u32[]{:S(2)}) async-start(bf16[4,128,2048]{2,1,0:T(8,128)(2,1)} %bitcast.98), calls=%async_computation.5 | async-start | bytes 4194304 | tf_op jit(solution)/shard_map/all_to_all | solution.py:50
  138.1 2.7 %copy.37 = f32[112,8,8,128]{3,1,2,0:T(8,128)} copy(f32[112,8,8,128]{3,2,1,0:T(8,128)S(1)} %bitcast.89) | data formatting | bytes 7340032
  140.8 5.0 %copy.21 = f32[1024,896]{1,0:T(8,128)} copy(f32[1024,896]{0,1:T(8,128)} %bitcast.87) | data formatting | bytes 7340032 | tf_op jit(solution)/shard_map/mul | solution.py:14
  146.1 2.8 %copy.38 = f32[112,8,8,128]{3,1,2,0:T(8,128)} copy(f32[112,8,8,128]{3,2,1,0:T(8,128)S(1)} %bitcast.90) | data formatting | bytes 7340032
  148.9 5.0 %copy.19 = f32[1024,896]{1,0:T(8,128)} copy(f32[1024,896]{0,1:T(8,128)} %bitcast.88) | data formatting | bytes 7340032 | tf_op jit(solution)/shard_map/mul | solution.py:14
  153.9 9.7 %all-to-all-done.5 = bf16[4,128,2048]{2,1,0:T(8,128)(2,1)} async-done(((bf16[4,128,2048]{2,1,0:T(8,128)(2,1)}), bf16[4,128,2048]{2,1,0:T(8,128)(2,1)}, u32[]{:S(2)}, u32[]{:S(2)}) %all-to-all-start.5) | async-done | bytes 2097184 | tf_op jit(solution)/shard_map/all_to_all | solution.py:50
  163.7 2.6 %add_convert_fusion.1 = bf16[1,128,2048]{2,1,0:T(8,128)(2,1)} fusion(bf16[4,128,2048]{2,1,0:T(8,128)(2,1)} %all-to-all-done.5), kind=kLoop, calls=%fused_computation.24 | loop fusion | flops 2097152 | bytes 2621440 | tf_op jit(solution)/shard_map/convert.4
  166.3 3.5 %all-to-all-start.6 = ((bf16[8,16,2048]{2,1,0:T(8,128)(2,1)}), bf16[8,16,2048]{2,1,0:T(8,128)(2,1)S(1)}, u32[]{:S(2)}, u32[]{:S(2)}) async-start(bf16[8,16,2048]{2,1,0:T(8,128)(2,1)} %bitcast.20), calls=%async_computation.6 | async-start | bytes 1048576 | tf_op jit(solution)/shard_map/all_to_all | solution.py:50
  169.8 5.0 %multiply_convert_fusion = bf16[1024,896]{1,0:T(8,128)(2,1)} fusion(f32[1024,896]{1,0:T(8,128)} %copy.21, bf16[512,2688]{1,0:T(8,128)(2,1)} %bitcast.101, bf16[512,2048]{1,0:T(8,128)(2,1)S(1)} %bitcast.95), kind=kOutput, calls=%fused_computation.9 | convolution fusion | flops 942276608 | bytes 7471104 | tf_op jit(solution)/shard_map/dot_general | solution.py:28
  174.8 2.6 %multiply_convert_fusion.1 = bf16[1024,896]{1,0:T(8,128)(2,1)} fusion(f32[1024,896]{1,0:T(8,128)S(1)} %copy-done, bf16[512,2688]{1,0:T(8,128)(2,1)S(1)} %bitcast.102, bf16[512,2048]{1,0:T(8,128)(2,1)S(1)} %bitcast.96), kind=kOutput, calls=%fused_computation.10 | convolution fusion | flops 942276608 | bytes 7471104 | tf_op jit(solution)/shard_map/dot_general | solution.py:28
  177.7 2.8 %fusion = bf16[896,1024]{1,0:T(8,128)(2,1)} fusion(f32[112,8,8,128]{3,2,1,0:T(8,128)S(1)} %bitcast.106, bf16[512,2048]{1,0:T(8,128)(2,1)S(1)} %bitcast.97, bf16[512,2688]{1,0:T(8,128)(2,1)S(1)} %bitcast.103), kind=kOutput, calls=%fused_computation.2 | convolution fusion | flops 942276608 | bytes 7471104 | tf_op jit(solution)/shard_map/dot_general | solution.py:28
  180.5 6.2 %all-to-all-done.6 = bf16[8,16,2048]{2,1,0:T(8,128)(2,1)S(1)} async-done(((bf16[8,16,2048]{2,1,0:T(8,128)(2,1)}), bf16[8,16,2048]{2,1,0:T(8,128)(2,1)S(1)}, u32[]{:S(2)}, u32[]{:S(2)}) %all-to-all-start.6) | async-done | bytes 524320 | tf_op jit(solution)/shard_map/all_to_all | solution.py:50
  (67 shorter events, 11.8 us)
Async XLA Ops:
  2.2 29.7 %collective-permute-start.6 = (bf16[16,2048]{1,0:T(8,128)(2,1)S(1)}, bf16[16,2048]{1,0:T(8,128)(2,1)S(1)}, u32[]{:S(2)}, u32[]{:S(2)}) collective-permute-start(bf16[16,2048]{1,0:T(8,128)(2,1)S(1)} %constant_dynamic-update-slice_fusion), channel_id=1, source_target_pairs={{0,7},{1,0},{2,1},{3,2},{4,3},{5,4},{6,5},{7,6},{8,15},{9,8},{10,9... | collective-permute-start | bytes 196616 | tf_op jit(solution)/shard_map/ppermute | solution.py:58
  8.5 23.3 %collective-permute-start.5 = (bf16[16,2048]{1,0:T(8,128)(2,1)S(1)}, bf16[16,2048]{1,0:T(8,128)(2,1)S(1)}, u32[]{:S(2)}, u32[]{:S(2)}) collective-permute-start(bf16[16,2048]{1,0:T(8,128)(2,1)S(1)} %constant_dynamic-update-slice_fusion), channel_id=1, source_target_pairs={{0,6},{1,7},{2,0},{3,1},{4,2},{5,3},{6,4},{7,5},{8,14},{9,15},{10,... | collective-permute-start | bytes 196616 | tf_op jit(solution)/shard_map/ppermute | solution.py:58
  9.7 22.1 %collective-permute-start.4 = (bf16[16,2048]{1,0:T(8,128)(2,1)S(1)}, bf16[16,2048]{1,0:T(8,128)(2,1)S(1)}, u32[]{:S(2)}, u32[]{:S(2)}) collective-permute-start(bf16[16,2048]{1,0:T(8,128)(2,1)S(1)} %constant_dynamic-update-slice_fusion), channel_id=1, source_target_pairs={{0,5},{1,6},{2,7},{3,0},{4,1},{5,2},{6,3},{7,4},{8,13},{9,14},{10,... | collective-permute-start | bytes 196616 | tf_op jit(solution)/shard_map/ppermute | solution.py:58
  10.2 21.6 %collective-permute-start.3 = (bf16[16,2048]{1,0:T(8,128)(2,1)S(1)}, bf16[16,2048]{1,0:T(8,128)(2,1)S(1)}, u32[]{:S(2)}, u32[]{:S(2)}) collective-permute-start(bf16[16,2048]{1,0:T(8,128)(2,1)S(1)} %constant_dynamic-update-slice_fusion), channel_id=1, source_target_pairs={{0,4},{1,5},{2,6},{3,7},{4,0},{5,1},{6,2},{7,3},{8,12},{9,13},{10,... | collective-permute-start | bytes 196616 | tf_op jit(solution)/shard_map/ppermute | solution.py:58
  14.6 5.7 %collective-permute-start = (bf16[16,2048]{1,0:T(8,128)(2,1)S(1)}, bf16[16,2048]{1,0:T(8,128)(2,1)S(1)}, u32[]{:S(2)}, u32[]{:S(2)}) collective-permute-start(bf16[16,2048]{1,0:T(8,128)(2,1)S(1)} %constant_dynamic-update-slice_fusion), channel_id=1, source_target_pairs={{0,1},{1,2},{2,3},{3,4},{4,5},{5,6},{6,7},{7,0},{8,9},{9,10},{10,1... | collective-permute-start | bytes 196616 | tf_op jit(solution)/shard_map/ppermute | solution.py:58
  20.3 5.2 %collective-permute-start.1 = (bf16[16,2048]{1,0:T(8,128)(2,1)S(1)}, bf16[16,2048]{1,0:T(8,128)(2,1)S(1)}, u32[]{:S(2)}, u32[]{:S(2)}) collective-permute-start(bf16[16,2048]{1,0:T(8,128)(2,1)S(1)} %constant_dynamic-update-slice_fusion), channel_id=1, source_target_pairs={{0,2},{1,3},{2,4},{3,5},{4,6},{5,7},{6,0},{7,1},{8,10},{9,11},{10,... | collective-permute-start | bytes 196616 | tf_op jit(solution)/shard_map/ppermute | solution.py:58
  25.6 6.2 %collective-permute-start.2 = (bf16[16,2048]{1,0:T(8,128)(2,1)S(1)}, bf16[16,2048]{1,0:T(8,128)(2,1)S(1)}, u32[]{:S(2)}, u32[]{:S(2)}) collective-permute-start(bf16[16,2048]{1,0:T(8,128)(2,1)S(1)} %constant_dynamic-update-slice_fusion), channel_id=1, source_target_pairs={{0,3},{1,4},{2,5},{3,6},{4,7},{5,0},{6,1},{7,2},{8,11},{9,12},{10,... | collective-permute-start | bytes 196616 | tf_op jit(solution)/shard_map/ppermute | solution.py:58
  34.2 4.4 %copy-start.7 = (s32[3,8,7]{2,1,0:T(8,128)S(1)}, s32[3,8,7]{2,1,0:T(8,128)}, u32[]{:S(2)}) copy-start(s32[3,8,7]{2,1,0:T(8,128)} %param.11) | copy-start | bytes 2020
  34.2 26.4 %all-to-all-start = ((bf16[4,128,2048]{2,1,0:T(8,128)(2,1)}), bf16[4,128,2048]{2,1,0:T(8,128)(2,1)S(1)}, u32[]{:S(2)}, u32[]{:S(2)}) async-start(bf16[4,128,2048]{2,1,0:T(8,128)(2,1)} %broadcast_in_dim.40), calls=%async_computation | async-start | bytes 4194304 | tf_op jit(solution)/shard_map/all_to_all | solution.py:43
  46.5 1.5 copy-start.3
  46.5 2.0 %copy-start.4 = (bf16[1024,896]{0,1:T(8,128)(2,1)S(1)}, bf16[1024,896]{0,1:T(8,128)(2,1)}, u32[]{:S(2)}) copy-start(bf16[1024,896]{0,1:T(8,128)(2,1)} %copy.16) | copy-start | bytes 5505028
  60.6 2.9 %copy-start.6 = (bf16[1024,896]{0,1:T(8,128)(2,1)S(1)}, bf16[1024,896]{0,1:T(8,128)(2,1)}, u32[]{:S(2)}) copy-start(bf16[1024,896]{0,1:T(8,128)(2,1)} %get-tuple-element.17) | copy-start | bytes 5505028
  63.5 1.6 copy-start.8
  120.1 8.1 %copy-start.5 = (bf16[1024,896]{0,1:T(8,128)(2,1)S(1)}, bf16[1024,896]{0,1:T(8,128)(2,1)}, u32[]{:S(2)}) copy-start(bf16[1024,896]{0,1:T(8,128)(2,1)} %get-tuple-element.16) | copy-start | bytes 5505028
  128.2 2.1 %copy-start.1 = (bf16[2,4,64,2688]{3,2,1,0:T(8,128)(2,1)}, bf16[2,4,64,2688]{3,2,1,0:T(8,128)(2,1)S(1)}, u32[]{:S(2)}) copy-start(bf16[2,4,64,2688]{3,2,1,0:T(8,128)(2,1)S(1)} %all_to_all.38) | copy-start | bytes 8257540
  133.1 30.6 %all-to-all-start.5 = ((bf16[4,128,2048]{2,1,0:T(8,128)(2,1)}), bf16[4,128,2048]{2,1,0:T(8,128)(2,1)}, u32[]{:S(2)}, u32[]{:S(2)}) async-start(bf16[4,128,2048]{2,1,0:T(8,128)(2,1)} %bitcast.98), calls=%async_computation.5 | async-start | bytes 4194304 | tf_op jit(solution)/shard_map/all_to_all | solution.py:50
  166.3 20.5 %all-to-all-start.6 = ((bf16[8,16,2048]{2,1,0:T(8,128)(2,1)}), bf16[8,16,2048]{2,1,0:T(8,128)(2,1)S(1)}, u32[]{:S(2)}, u32[]{:S(2)}) async-start(bf16[8,16,2048]{2,1,0:T(8,128)(2,1)} %bitcast.20), calls=%async_computation.6 | async-start | bytes 1048576 | tf_op jit(solution)/shard_map/all_to_all | solution.py:50
  169.8 5.0 %copy-start = (f32[1024,896]{1,0:T(8,128)S(1)}, f32[1024,896]{1,0:T(8,128)}, u32[]{:S(2)}) copy-start(f32[1024,896]{1,0:T(8,128)} %copy.19) | copy-start | bytes 11010052
  169.8 5.0 %copy-start.2 = (bf16[2,4,64,2688]{3,2,1,0:T(8,128)(2,1)S(1)}, bf16[2,4,64,2688]{3,2,1,0:T(8,128)(2,1)}, u32[]{:S(2)}) copy-start(bf16[2,4,64,2688]{3,2,1,0:T(8,128)(2,1)} %copy-done.1) | copy-start | bytes 8257540
